TPU v7x, 32 devices: a whole 2x2x4 slice. The times are simulated.
32 devices in a mesh: groups: 2 (over y), wide: 4 (over z), ctx: 4 (over x, core).
Axes of the slice: x: 2, y: 2, z: 4, core: 2. Of those that a mesh axis runs over, the one named last changes fastest.
Arguments:
- queries: bfloat16 [4096, 6144], P(('groups', 'ctx'), 'wide'), parts along dimension 0, may hold values from -48 to 48
- key_rows: bfloat16 [4096, 1024], P(('groups', 'ctx')), parts along dimension 0, may hold values from -48 to 48
- value_head_rows: bfloat16 [4096, 1024], P(('groups', 'ctx')), parts along dimension 0, may hold values from -18 to 18
- residual: bfloat16 [4096, 6144], P(('groups', 'ctx'), 'wide'), parts along dimension 0, may hold values from -48 to 48
- out_weight: bfloat16 [6144, 6144], P('wide'), may hold values from -0.109375 to 0.109375
- norm_gain: bfloat16 [6144], P('wide'), may hold values from 0.25 to 1.75
- router_weight: bfloat16 [6144, 8], P('wide'), may hold values from -0.078125 to 0.078125
- gate_weight: bfloat16 [6144, 8192], P('wide', 'ctx'), may hold values from -0.078125 to 0.078125
- up_weight: bfloat16 [6144, 8192], P('wide', 'ctx'), may hold values from -0.078125 to 0.078125
- down_weight: bfloat16 [8192, 6144], P('ctx', 'wide'), may hold values from -0.0625 to 0.0625
- expert_ids: int32 [4096, 2], P('groups'), parts along dimension 0, may hold values from 0 to 7, as said below
- slot_ids: int32 [4096, 2], P('groups'), parts along dimension 0, may hold values from -1 to 639, as said below
Outputs:
- layer_out: bfloat16 [4096, 6144], P(('groups', 'ctx'), 'wide'), parts along dimension 0
There are 2 independent parts, one for each index of `groups`. A program takes and returns all parts, laid end to end along the dimension named above; an argument that names none is the same for every part. Nothing has to cross between parts.
Inputs may be any that keep to these rules, and one draw needn't show every extreme that they name: `expert_ids`: each row names 2 different experts; expert 0 is named by at least 704 rows, so its buffer is full in every draw. `slot_ids`: the rows naming one expert take its buffer rows 0, 1, 2 and so on in the order of positions (for one position, the earlier column first); once 640 rows are taken, further choices of that expert hold -1. Rows of one expert's buffer are never shared.
All inputs are finite; a program needn't handle non-finite values.
Results may differ from a plain program's by a relative error of at most 0.015.
Values may be sent and summed in bfloat16 or wider, within the bound.
No kernel may reach another device: no remote copies, remote signals or barrier semaphores. Data moves between devices by JAX's collectives and lax.ppermute only.
A program may use at most 192 MiB of HBM per device.

v0:
```python
import math

import jax
import jax.numpy as jnp
from jax import lax
from jax.sharding import PartitionSpec as P

D = 6144
QUERY_HEADS = 48
KEY_VALUE_HEADS = 8
HEAD_SIZE = 128


NEG_FILL = -1e30
EPSILON = 1e-05


def token_slots(expert_ids, slot_ids, capacity):
    in_window = jnp.logical_and(expert_ids == 0, slot_ids >= 0)
    picked = jnp.max(jnp.where(in_window, slot_ids, -1), axis=1)
    return jnp.where(picked >= 0, picked, capacity)


def other_experts(expert_ids, slot_of_token, capacity):
    partner = jnp.sum(expert_ids, axis=1)
    return jnp.zeros((capacity,), jnp.int32).at[slot_of_token].set(partner, mode="drop")


def expert_hidden(gate_sum, up_sum, square_sum, logit_sum, slot_other, model_width):
    inverse_rms = lax.rsqrt(square_sum / model_width + EPSILON)
    gate_value = gate_sum * inverse_rms[:, None]
    up_value = up_sum * inverse_rms[:, None]
    logit_value = logit_sum * inverse_rms[:, None]
    columns = jnp.arange(logit_value.shape[1], dtype=jnp.int32)
    partner_logit = jnp.sum(
        jnp.where(columns[None, :] == slot_other[:, None], logit_value, 0.0), axis=1
    )
    mixing = jax.nn.sigmoid(logit_value[:, 0] - partner_logit)
    return (jax.nn.silu(gate_value) * up_value * mixing[:, None]).astype(jnp.bfloat16)


def local(
    queries,
    key_rows,
    value_head_rows,
    residual,
    out_weight,
    norm_gain,
    router_weight,
    gate_weight,
    up_weight,
    down_weight,
    expert_ids,
    slot_ids,
):
    ctx_count = lax.axis_size("ctx")
    wide_index = lax.axis_index("wide")
    ctx_index = lax.axis_index("ctx")
    rows_local = queries.shape[0]
    heads_local = queries.shape[1] // HEAD_SIZE
    query_group_width = QUERY_HEADS // KEY_VALUE_HEADS
    shared_heads = max(1, heads_local // query_group_width)
    per_shared = heads_local // shared_heads
    first_shared = wide_index * heads_local // query_group_width
    key_used = lax.dynamic_slice_in_dim(
        key_rows, first_shared * HEAD_SIZE, shared_heads * HEAD_SIZE, 1
    )
    value_used = lax.dynamic_slice_in_dim(
        value_head_rows, first_shared * HEAD_SIZE, shared_heads * HEAD_SIZE, 1
    )
    query_blocks = queries.reshape(rows_local, shared_heads, per_shared, HEAD_SIZE)
    query_pos = ctx_index * rows_local + jnp.arange(rows_local, dtype=jnp.int32)
    last_query = ctx_index * rows_local + rows_local - 1
    scale_factor = 1.0 / math.sqrt(HEAD_SIZE)
    start_state = (
        jnp.full((shared_heads, per_shared, rows_local), -jnp.inf, jnp.float32),
        jnp.zeros((shared_heads, per_shared, rows_local), jnp.float32),
        jnp.zeros((shared_heads, per_shared, rows_local, HEAD_SIZE), jnp.float32),
    )
    pieces = (
        lax.all_gather(key_used, "ctx", axis=0, tiled=True),
        lax.all_gather(value_used, "ctx", axis=0, tiled=True),
    )

    def update(state):
        running_max, running_sum, running_acc = state
        key_piece = pieces[0].reshape(-1, shared_heads, HEAD_SIZE)
        value_piece = pieces[1].reshape(-1, shared_heads, HEAD_SIZE)
        scores = (
            jnp.einsum(
                "skqd,rkd->kqsr", query_blocks, key_piece, preferred_element_type=jnp.float32
            )
            * scale_factor
        )
        key_pos = jnp.arange(key_piece.shape[0], dtype=jnp.int32)
        allowed = (key_pos[None, :] <= query_pos[:, None])[None, None, :, :]
        masked = jnp.where(allowed, scores, NEG_FILL)
        new_max = jnp.max(masked, axis=-1)
        weights = jnp.where(allowed, jnp.exp(masked - new_max[..., None]), 0.0)
        decay = jnp.exp(running_max - new_max)
        new_sum = running_sum * decay + jnp.sum(weights, axis=-1)
        added = jnp.einsum(
            "kqsr,rkd->kqsd",
            weights.astype(jnp.bfloat16),
            value_piece,
            preferred_element_type=jnp.float32,
        )
        return (new_max, new_sum, running_acc * decay[..., None] + added)

    final_max, final_sum, final_acc = lax.cond(
        jnp.int32(0) > last_query, lambda state: state, update, start_state
    )
    attended = final_acc / final_sum[..., None]
    attended = (
        jnp.transpose(attended, (2, 0, 1, 3))
        .reshape(rows_local, heads_local * HEAD_SIZE)
        .astype(jnp.bfloat16)
    )
    partial_out = jnp.dot(attended, out_weight, preferred_element_type=jnp.float32)
    head_sum = lax.psum_scatter(
        partial_out.astype(jnp.bfloat16), "wide", scatter_dimension=1, tiled=True
    ).astype(jnp.float32)
    resid = (residual.astype(jnp.float32) + head_sum).astype(jnp.bfloat16)
    seq_len = rows_local * ctx_count
    capacity = seq_len * 5 // 16
    width_local = resid.shape[1]
    slot_of_token = token_slots(expert_ids, slot_ids, capacity)
    slot_other = other_experts(expert_ids, slot_of_token, capacity)
    buffer = (
        jnp.zeros((capacity, width_local), jnp.bfloat16)
        .at[slot_of_token]
        .set(lax.all_gather(resid, "ctx", axis=0, tiled=True), mode="drop")
    )
    buffer_wide = buffer.astype(jnp.float32)
    square_part = jnp.sum(buffer_wide * buffer_wide, axis=1)
    scaled = (buffer_wide * norm_gain.astype(jnp.float32)[None, :]).astype(jnp.bfloat16)
    gate_part = jnp.dot(scaled, gate_weight, preferred_element_type=jnp.float32)
    up_part = jnp.dot(scaled, up_weight, preferred_element_type=jnp.float32)
    logit_part = jnp.dot(scaled, router_weight, preferred_element_type=jnp.float32)
    gate_sum, up_sum, square_sum, logit_sum = (
        lax.psum(gate_part.astype(jnp.bfloat16), "wide").astype(jnp.float32),
        lax.psum(up_part.astype(jnp.bfloat16), "wide").astype(jnp.float32),
        lax.psum(square_part.astype(jnp.bfloat16), "wide").astype(jnp.float32),
        lax.psum(logit_part.astype(jnp.bfloat16), "wide").astype(jnp.float32),
    )
    hidden = expert_hidden(gate_sum, up_sum, square_sum, logit_sum, slot_other, D)
    expert_part = jnp.dot(hidden, down_weight, preferred_element_type=jnp.float32)
    expert_pad = jnp.concatenate([expert_part, jnp.zeros((1, width_local), jnp.float32)], axis=0)
    moe_rows = lax.psum_scatter(
        jnp.take(expert_pad, slot_of_token, axis=0).astype(jnp.bfloat16),
        "ctx",
        scatter_dimension=0,
        tiled=True,
    ).astype(jnp.float32)
    return (resid.astype(jnp.float32) + moe_rows).astype(jnp.bfloat16)


def solution(mesh):
    placed = (
        P(("groups", "ctx"), "wide"),
        P(("groups", "ctx"), None),
        P(("groups", "ctx"), None),
        P(("groups", "ctx"), "wide"),
        P("wide", None),
        P("wide"),
        P("wide", None),
        P("wide", "ctx"),
        P("wide", "ctx"),
        P("ctx", "wide"),
        P("groups", None),
        P("groups", None),
    )
    return jax.shard_map(
        local, mesh=mesh, in_specs=placed, out_specs=P(("groups", "ctx"), "wide"), check_vma=False
    )
```

profile of v0, /device:TPU:0, one launch (start us, length us, event | category | flops | bytes accessed | tf_op | source)
XLA Modules:
  0.0 613.0 jit_solution(8369827461181199514)
XLA Ops:
  6.5 1.2 copy-done
  7.8 0.7 constant_dynamic-slice_fusion.1
  8.6 1.7 constant_dynamic-slice_fusion
  10.3 18.0 %all-gather.4.cloned.1.call-done = bf16[2048,256]{1,0:T(8,128)(2,1)} async-done(((bf16[512,256]{1,0:T(8,128)(2,1)}), bf16[2048,256]{1,0:T(8,128)(2,1)}) %all-gather.4.cloned.1.call-update) | async-done | bytes 1048592 | tf_op jit(solution)/shard_map/all_gather | solution.py:81
  28.3 18.3 %all-gather.6.cloned.1.call-done = bf16[2048,256]{1,0:T(8,128)(2,1)} async-done(((bf16[512,256]{1,0:T(8,128)(2,1)}), bf16[2048,256]{1,0:T(8,128)(2,1)}) %all-gather.6.cloned.1.call-update) | async-done | bytes 1048592 | tf_op jit(solution)/shard_map/all_gather | solution.py:82
  46.6 75.7 %conditional.1 = (f32[2,6,512]{2,1,0:T(8,128)S(1)}, f32[2,6,512,128]{2,3,1,0:T(8,128)}) conditional(s32[]{:T(128)} %convert_element_type.76, (s32[]{:T(128)}, s32[512]{0:T(512)S(1)}, bf16[2048,256]{1,0:T(8,128)(2,1)}, bf16[512,1536]{1,0:T(8,128)(2,1)}, bf16[2048,256]{1,0:T(8,128)(2,1)}) %tuple.13, () %tuple.14), branch_computations={%region_0.3_spmd, %region_3.4_spmd} | conditional | flops 6607870464 | bytes 180058160 | solution.py:110
  46.6 0.8 iota_compare_fusion
  47.5 1.7 copy.28
  49.2 2.1 reshape.71
  51.3 21.1 %fusion = (f32[2,6,512]{2,1,0:T(8,128)S(1)}, f32[2,2048,512,6]{2,1,3,0:T(8,128)}) fusion(pred[512,2048]{0,1:T(8,128)(4,1)S(1)} %iota_compare_fusion, bf16[512,2,6,128]{0,3,2,1:T(8,128)(2,1)S(1)} %bitcast.29, bf16[2048,2,128,1]{2,1,0,3:T(2,128)(2,1)} %bitcast.30), kind=kOutput, calls=%fused_computation.5 | convolution fusion | flops 3258968064 | bytes 54026240 | tf_op jit(solution)/shard_map/cond/branch_0_fun/skqd,rkd->kqsr/dot_general | solution.py:90
  72.4 22.0 %fusion.2 = f32[2,6,512]{2,1,0:T(8,128)S(1)} fusion(f32[2,2048,512,6]{2,1,3,0:T(8,128)} %get-tuple-element.49, f32[2,6,512]{2,1,0:T(8,128)S(1)} %get-tuple-element.48, pred[512,2048]{0,1:T(8,128)(4,1)S(1)} %iota_compare_fusion), kind=kLoop, calls=%fused_computation.7 | loop fusion | flops 62908416 | bytes 51429376 | tf_op jit(solution)/shard_map/cond/branch_0_fun/reduce_sum | solution.py:101
  94.4 0.3 reshape.73
  94.7 24.0 %fusion.6 = f32[2,6,512,128]{3,2,1,0:T(8,128)} fusion(f32[2,2048,512,6]{2,1,3,0:T(8,128)} %get-tuple-element.49, f32[2,6,512]{2,1,0:T(8,128)S(1)} %get-tuple-element.48, pred[512,2048]{0,1:T(8,128)(4,1)S(1)} %iota_compare_fusion, f32[2,6,512]{2,1,0:T(8,128)S(1)} %get-tuple-element.46, bf16[2048,2,128,1]{2,1,0,3:T(2,128)(2,1)S(1)} %bitcast.32), kind=kOutput, calls=%fused_computation.11 | convolution fusion | flops 3284926464 | bytes 55623680 | tf_op jit(solution)/shard_map/cond/branch_0_fun/kqsr,rkd->kqsd/dot_general | solution.py:102
  118.8 3.5 copy.38
  122.3 2.3 divide_convert_fusion
  124.7 15.7 %convolution_convert_fusion = bf16[512,6144]{1,0:T(8,128)(2,1)} fusion(bf16[512,1536]{0,1:T(8,128)(2,1)S(1)} %bitcast.31, bf16[1536,6144]{1,0:T(8,128)(2,1)} %param.18), kind=kOutput, calls=%fused_computation.22 | convolution fusion | flops 9666822144 | bytes 26738688 | tf_op jit(solution)/shard_map/dot_general | solution.py:119
  140.5 110.8 %reduce-scatter.3.cloned.1.call-done = bf16[512,1536]{1,0:T(8,128)(2,1)} async-done(((bf16[512,6144]{1,0:T(8,128)(2,1)}), bf16[512,1536]{1,0:T(8,128)(2,1)}) %reduce-scatter.3.cloned.1.call-update) | async-done | bytes 1572880 | tf_op jit(solution)/shard_map/reduce_scatter | solution.py:120
  251.3 2.9 add_convert_fusion.1
  254.4 46.9 %all-gather.8.cloned.1.call-done = bf16[2048,1536]{1,0:T(8,128)(2,1)} async-done(((bf16[512,1536]{1,0:T(8,128)(2,1)}), bf16[2048,1536]{1,0:T(8,128)(2,1)}) %all-gather.8.cloned.1.call-update) | async-done | bytes 6291472 | tf_op jit(solution)/shard_map/all_gather | solution.py:132
  301.3 11.4 %scatter_custom_fusion = bf16[640,1536]{1,0:T(8,128)(2,1)S(1)} fusion(s32[2048]{0:T(1024)S(1)} %bitcast.35, bf16[2048,1536]{1,0:T(8,128)(2,1)} %all-gather.8.cloned.1.call-done, bf16[]{:T(256)} %constant.48.clone.1), kind=kCustom, calls=%fused_computation.36 | custom fusion | bytes 1966592 | tf_op jit(solution)/shard_map/scatter | solution.py:132
  312.8 8.5 %convolution_convert_fusion.1 = bf16[640,2048]{1,0:T(8,128)(2,1)} fusion(bf16[1536,2048]{1,0:T(8,128)(2,1)} %param.22, bf16[640,1536]{1,0:T(8,128)(2,1)S(1)} %scatter_custom_fusion, f32[1536]{0:T(1024)S(1)} %convert_element_type.85), kind=kOutput, calls=%fused_computation.28 | convolution fusion | flops 4030791680 | bytes 10885120 | tf_op jit(solution)/shard_map/dot_general | solution.py:138
  321.2 8.2 %convolution_convert_fusion.2 = bf16[640,2048]{1,0:T(8,128)(2,1)} fusion(bf16[1536,2048]{1,0:T(8,128)(2,1)} %param.21, bf16[640,1536]{1,0:T(8,128)(2,1)S(1)} %scatter_custom_fusion, f32[1536]{0:T(1024)S(1)} %convert_element_type.85), kind=kOutput, calls=%fused_computation.29 | convolution fusion | flops 4030791680 | bytes 10885120 | tf_op jit(solution)/shard_map/dot_general | solution.py:137
  329.6 8.0 %scatter_custom_fusion.1 = s32[640]{0:T(1024)S(1)} fusion(s32[2048]{0:T(1024)S(1)} %bitcast.36, s32[2048]{0:T(1024)S(1)} %get-tuple-element.40, s32[]{:T(128)} %constant.22.clone.1), kind=kCustom, calls=%fused_computation.54 | custom fusion | bytes 2564 | tf_op jit(solution)/shard_map/scatter | solution.py:26
  337.7 0.5 fusion.17
  338.1 0.6 fusion.23
  338.7 19.9 %all-reduce.1 = (bf16[640]{0:T(1024)(128)(2,1)S(1)}, bf16[640,8]{0,1:T(8,128)(2,1)S(1)}) all-reduce(bf16[640]{0:T(1024)(128)(2,1)S(1)} %fusion.17, bf16[640,8]{0,1:T(8,128)(2,1)S(1)} %fusion.23), channel_id=1, replica_groups=mesh['groups'=2,'wide'=4,'ctx'=4] {'wide'}, use_global_device_ids=true, to_apply=%region_9.10 | all-reduce | flops 5760 | bytes 23040 | tf_op jit(solution)/shard_map/psum | solution.py:143
  358.7 160.5 %all-reduce.5.cloned.1.call-done = (bf16[640,2048]{1,0:T(8,128)(2,1)}, bf16[640,2048]{1,0:T(8,128)(2,1)}) async-done(((bf16[640,2048]{1,0:T(8,128)(2,1)}, bf16[640,2048]{1,0:T(8,128)(2,1)}), (bf16[640,2048]{1,0:T(8,128)(2,1)}, bf16[640,2048]{1,0:T(8,128)(2,1)})) %all-reduce.5.cloned.1.call-update) | async-done | bytes 5242896 | tf_op jit(solution)/shard_map/psum | solution.py:142
  519.2 9.2 %fusion.18 = bf16[640,1536]{1,0:T(8,128)(2,1)S(1)} fusion(bf16[2048,1536]{1,0:T(8,128)(2,1)} %param.23, bf16[640,2048]{1,0:T(8,128)(2,1)} %get-tuple-element.44, bf16[640,2048]{1,0:T(8,128)(2,1)} %get-tuple-element.45, f32[640]{0:T(1024)S(1)} %divide_reduce_fusion, f32[640]{0:T(1024)S(1)} %add_rsqrt_fusion), kind=kOutput, calls=%fused_computation.33 | convolution fusion | flops 4040949760 | bytes 13505536 | tf_op jit(solution)/shard_map/dot_general | solution.py:147
  528.5 10.1 %gather_fusion = bf16[2048,1536]{1,0:T(8,128)(2,1)} fusion(bf16[641,1536]{1,0:T(8,128)(2,1)S(1)} %concatenate.3, s32[2048]{0:T(1024)S(1)} %broadcast_clamp_fusion), kind=kCustom, calls=%fused_computation | custom fusion | bytes 12591104 | tf_op jit(solution)/shard_map/jit(_take)/gather | solution.py:150
  538.7 6.6 %select_convert_fusion = bf16[2048,1536]{1,0:T(8,128)(2,1)} fusion(bf16[2048,1536]{1,0:T(8,128)(2,1)} %gather_fusion, pred[2048]{0:T(1024)(128)(4,1)S(1)} %compare_and_fusion), kind=kLoop, calls=%fused_computation.21 | loop fusion | flops 3145728 | bytes 12584960 | tf_op jit(solution)/shard_map/convert_element_type | solution.py:150
  545.3 58.0 %reduce-scatter.5.cloned.1.call-done = bf16[512,1536]{1,0:T(8,128)(2,1)} async-done(((bf16[2048,1536]{1,0:T(8,128)(2,1)}), bf16[512,1536]{1,0:T(8,128)(2,1)}) %reduce-scatter.5.cloned.1.call-update) | async-done | bytes 1572880 | tf_op jit(solution)/shard_map/reduce_scatter | solution.py:149
  603.2 2.9 add_convert_fusion
  (41 shorter events, 0.7 us)
Async XLA Ops:
  6.5 1.2 copy-start
  6.5 21.8 %all-gather.4.cloned.1.call-start = ((), (), s32[]{:S(2)}) async-start(), calls=%async_computation.2 | async-start | bytes 1310720 | tf_op jit(solution)/shard_map/all_gather | solution.py:81
  8.5 38.1 %all-gather.6.cloned.1.call-start = ((), (), s32[]{:S(2)}) async-start(), calls=%async_computation.3 | async-start | bytes 1310720 | tf_op jit(solution)/shard_map/all_gather | solution.py:82
  10.3 241.0 %reduce-scatter.3.cloned.1.call-start = ((), (), s32[]{:S(2)}) async-start(), calls=%async_computation.4 | async-start | bytes 7864320 | tf_op jit(solution)/shard_map/reduce_scatter | solution.py:120
  72.4 22.0 %copy-start.4 = (bf16[2048,256]{1,0:T(8,128)(2,1)S(1)}, bf16[2048,256]{1,0:T(8,128)(2,1)}, u32[]{:S(2)}) copy-start(bf16[2048,256]{1,0:T(8,128)(2,1)} %get-tuple-element.22) | copy-start | bytes 3145732 | tf_op jit(solution)/shard_map/cond
  140.3 111.0 %copy-start.3 = (bf16[512,1536]{1,0:T(8,128)(2,1)S(1)}, bf16[512,1536]{1,0:T(8,128)(2,1)}, u32[]{:S(2)}) copy-start(bf16[512,1536]{1,0:T(8,128)(2,1)} %param.17) | copy-start | bytes 4718596
  140.4 113.9 %copy-start.7 = (bf16[1536]{0:T(1024)(128)(2,1)S(1)}, bf16[1536]{0:T(1024)(128)(2,1)}, u32[]{:S(2)}) copy-start(bf16[1536]{0:T(1024)(128)(2,1)} %param.19) | copy-start | bytes 9220
  140.4 114.0 %copy-start.5 = (s32[2048,2]{0,1:T(2,128)S(1)}, s32[2048,2]{0,1:T(2,128)}, u32[]{:S(2)}) copy-start(s32[2048,2]{0,1:T(2,128)} %param.24) | copy-start | bytes 49156
  140.4 114.0 %copy-start.6 = (s32[2048,2]{0,1:T(2,128)S(1)}, s32[2048,2]{0,1:T(2,128)}, u32[]{:S(2)}) copy-start(s32[2048,2]{0,1:T(2,128)} %param.25) | copy-start | bytes 49156
  140.4 160.9 %all-gather.8.cloned.1.call-start = ((), (), s32[]{:S(2)}) async-start(), calls=%async_computation.5 | async-start | bytes 7864320 | tf_op jit(solution)/shard_map/all_gather | solution.py:132
  254.3 264.9 %all-reduce.5.cloned.1.call-start = ((), (), s32[]{:S(2)}) async-start(), calls=%async_computation.7 | async-start | bytes 10485760 | tf_op jit(solution)/shard_map/psum | solution.py:142
  329.5 8.6 %copy-start.8 = (bf16[1536,8]{0,1:T(8,128)(2,1)S(1)}, bf16[1536,8]{0,1:T(8,128)(2,1)}, u32[]{:S(2)}) copy-start(bf16[1536,8]{0,1:T(8,128)(2,1)} %param.20) | copy-start | bytes 73732
  329.5 273.7 %reduce-scatter.5.cloned.1.call-start = ((), (), s32[]{:S(2)}) async-start(), calls=%async_computation.6 | async-start | bytes 7864320 | tf_op jit(solution)/shard_map/reduce_scatter | solution.py:149
  545.3 58.0 %copy-start.2 = (bf16[512,1536]{1,0:T(8,128)(2,1)S(1)}, bf16[512,1536]{1,0:T(8,128)(2,1)}, u32[]{:S(2)}) copy-start(bf16[512,1536]{1,0:T(8,128)(2,1)} %add_convert_fusion.1) | copy-start | bytes 4718596
  545.3 60.9 %copy-start.1 = (bf16[512,1024]{1,0:T(8,128)(2,1)S(1)}, bf16[512,1024]{1,0:T(8,128)(2,1)}, u32[]{:S(2)}) copy-start(bf16[512,1024]{1,0:T(8,128)(2,1)} %param.15) | copy-start | bytes 3145732
Sparse Core Ops, SparseCore 0:
  8.9 19.4 all-gather.3
  29.9 16.6 all-gather.5
  140.5 110.7 reduce-scatter.2
  254.4 46.8 all-gather.7
  329.6 189.4 all-reduce.4
  545.4 57.7 reduce-scatter.4
where the time goes:
time: 614 us; the launch traced here: 613 us
  waiting for transfers between devices  413 us (67%)
  matrix products  87.4 us (14%)
  local copies, waits for them, and re-layouts  41.1 us (7%)
  other arithmetic  38.2 us (6%)
  blocking collectives  19.9 us (3%)
  between operations  13.6 us (2%)
    psum x1, waiting for transfers between devices, local(): lax.psum(up_part.astype(jnp.bfloat16), 'wide').astype(jnp.float32)  160 us
    reduce_scatter x1, waiting for transfers between devices, local(): lax.psum_scatter(partial_out.astype(jnp.bfloat16), 'wide', scatter_dimens...  111 us
    reduce_scatter x1, waiting for transfers between devices, local(): lax.psum_scatter(jnp.take(expert_pad, slot_of_token, axis=0).astype(jnp.b...  58 us
    all_gather x1, waiting for transfers between devices, local(): lax.all_gather(resid, 'ctx', axis=0, tiled=True)  46.9 us
    dot_general x1, matrix products, update(): jnp.einsum('kqsr,rkd->kqsd', weights.astype(jnp.bfloat16), value_piece, p...  24 us
    reduce_sum x1, other arithmetic, update(): new_sum = running_sum * decay + jnp.sum(weights, axis=-1)  22 us
    dot_general x1, matrix products, update(): jnp.einsum('skqd,rkd->kqsr', query_blocks, key_piece, preferred_element_t...  21.1 us
    psum x1, blocking collectives, local(): lax.psum(square_part.astype(jnp.bfloat16), 'wide').astype(jnp.float32)  19.9 us
  transfers between devices with their start and end apart: 6, of which 6 were waited for; matrix products, arithmetic and copies ran while one was open for 2% of the time, Pallas kernels for 0%

commit v1 on v0

--- a/solution.py
+++ b/solution.py
@@ -77,9 +77,12 @@
         jnp.zeros((shared_heads, per_shared, rows_local), jnp.float32),
         jnp.zeros((shared_heads, per_shared, rows_local, HEAD_SIZE), jnp.float32),
     )
+    packed_kv = lax.all_gather(
+        jnp.concatenate([key_used, value_used], axis=1), "ctx", axis=0, tiled=True
+    )
     pieces = (
-        lax.all_gather(key_used, "ctx", axis=0, tiled=True),
-        lax.all_gather(value_used, "ctx", axis=0, tiled=True),
+        packed_kv[:, : shared_heads * HEAD_SIZE],
+        packed_kv[:, shared_heads * HEAD_SIZE :],
     )
 
     def update(state):
@@ -124,34 +127,50 @@
     seq_len = rows_local * ctx_count
     capacity = seq_len * 5 // 16
     width_local = resid.shape[1]
+    wide_count = lax.axis_size("wide")
+    chunk = capacity // wide_count
     slot_of_token = token_slots(expert_ids, slot_ids, capacity)
     slot_other = other_experts(expert_ids, slot_of_token, capacity)
-    buffer = (
-        jnp.zeros((capacity, width_local), jnp.bfloat16)
-        .at[slot_of_token]
-        .set(lax.all_gather(resid, "ctx", axis=0, tiled=True), mode="drop")
+    slot_local = lax.dynamic_slice_in_dim(slot_of_token, ctx_index * rows_local, rows_local)
+    own_rows = jnp.zeros((capacity, width_local), jnp.bfloat16).at[slot_local].set(
+        resid, mode="drop"
     )
+    buffer = lax.psum(own_rows, "ctx")
     buffer_wide = buffer.astype(jnp.float32)
     square_part = jnp.sum(buffer_wide * buffer_wide, axis=1)
     scaled = (buffer_wide * norm_gain.astype(jnp.float32)[None, :]).astype(jnp.bfloat16)
     gate_part = jnp.dot(scaled, gate_weight, preferred_element_type=jnp.float32)
     up_part = jnp.dot(scaled, up_weight, preferred_element_type=jnp.float32)
     logit_part = jnp.dot(scaled, router_weight, preferred_element_type=jnp.float32)
-    gate_sum, up_sum, square_sum, logit_sum = (
-        lax.psum(gate_part.astype(jnp.bfloat16), "wide").astype(jnp.float32),
-        lax.psum(up_part.astype(jnp.bfloat16), "wide").astype(jnp.float32),
-        lax.psum(square_part.astype(jnp.bfloat16), "wide").astype(jnp.float32),
-        lax.psum(logit_part.astype(jnp.bfloat16), "wide").astype(jnp.float32),
+    hidden_local = gate_part.shape[1]
+    experts = logit_part.shape[1]
+    pad = 128 - (experts + 1) % 128
+    packed = jnp.concatenate(
+        [
+            gate_part,
+            up_part,
+            logit_part,
+            square_part[:, None],
+            jnp.zeros((capacity, pad), jnp.float32),
+        ],
+        axis=1,
+    ).astype(jnp.bfloat16)
+    reduced = lax.psum_scatter(packed, "wide", scatter_dimension=0, tiled=True).astype(
+        jnp.float32
     )
-    hidden = expert_hidden(gate_sum, up_sum, square_sum, logit_sum, slot_other, D)
+    gate_sum = reduced[:, :hidden_local]
+    up_sum = reduced[:, hidden_local : 2 * hidden_local]
+    logit_sum = reduced[:, 2 * hidden_local : 2 * hidden_local + experts]
+    square_sum = reduced[:, 2 * hidden_local + experts]
+    other_chunk = lax.dynamic_slice_in_dim(slot_other, wide_index * chunk, chunk)
+    hidden_chunk = expert_hidden(gate_sum, up_sum, square_sum, logit_sum, other_chunk, D)
+    hidden = lax.all_gather(hidden_chunk, "wide", axis=0, tiled=True)
     expert_part = jnp.dot(hidden, down_weight, preferred_element_type=jnp.float32)
-    expert_pad = jnp.concatenate([expert_part, jnp.zeros((1, width_local), jnp.float32)], axis=0)
-    moe_rows = lax.psum_scatter(
-        jnp.take(expert_pad, slot_of_token, axis=0).astype(jnp.bfloat16),
-        "ctx",
-        scatter_dimension=0,
-        tiled=True,
-    ).astype(jnp.float32)
+    expert_sum = lax.psum(expert_part.astype(jnp.bfloat16), "ctx")
+    expert_pad = jnp.concatenate(
+        [expert_sum, jnp.zeros((1, width_local), jnp.bfloat16)], axis=0
+    )
+    moe_rows = jnp.take(expert_pad, slot_local, axis=0).astype(jnp.float32)
     return (resid.astype(jnp.float32) + moe_rows).astype(jnp.bfloat16)
 
 

time: 614 us -> 550 us (0.90)
  waiting for transfers between devices: 413 us -> 377 us
  blocking collectives: 19.9 us -> 0 us
  local copies, waits for them, and re-layouts: 41.1 us -> 34.6 us
    unnamed x6 -> x7, waiting for transfers between devices: 0.1 us -> 88.6 us
    psum x1 -> x2, waiting for transfers between devices: 160 us -> 97.7 us  [the longest x1 49.7 us: local(): buffer = lax.psum(own_rows, 'ctx')]
    reduce_scatter x1 -> x0, waiting for transfers between devices: 58 us -> none  [local(): lax.psum_scatter(jnp.take(expert_pad, slot_of_token, axis=0).astype(jnp.b...]
    psum x1 -> x0, blocking collectives: 19.9 us -> none  [local(): lax.psum(square_part.astype(jnp.bfloat16), 'wide').astype(jnp.float32)]
    scatter x1 -> x0, local copies, waits for them, and re-layouts: 11.4 us -> none  [local(): buffer = jnp.zeros((capacity, width_local), jnp.bfloat16).at[slot_of_toke...]
    concatenate x1 -> x2, local copies, waits for them, and re-layouts: 0.13 us -> 10.2 us  [the longest x1 8.52 us: local(): jnp.concatenate([gate_part, up_part, logit_part, square_part[:, None], jn...]
    convert_element_type x2, other arithmetic: 9.5 us -> 1.01 us  [the longest x1 0.67 us: expert_hidden(): (jax.nn.silu(gate_value) * up_value * mixing[:, None]).astype(jnp.bfloat16)]
    gather x1, local copies, waits for them, and re-layouts: 10.1 us -> 2.94 us  [local(): moe_rows = jnp.take(expert_pad, slot_local, axis=0).astype(jnp.float32)]
where the time goes in v1:
time: 550 us
  waiting for transfers between devices  377 us (69%)
  matrix products  88.1 us (16%)
  other arithmetic  35.6 us (6%)
  local copies, waits for them, and re-layouts  34.6 us (6%)
  between operations  13.6 us (2%)
    reduce_scatter x1, waiting for transfers between devices, local(): lax.psum_scatter(partial_out.astype(jnp.bfloat16), 'wide', scatter_dimens...  110 us
    unnamed x7, waiting for transfers between devices  88.6 us
    all_gather x1, waiting for transfers between devices, local(): hidden = lax.all_gather(hidden_chunk, 'wide', axis=0, tiled=True)  55.1 us
    psum x1, waiting for transfers between devices, local(): buffer = lax.psum(own_rows, 'ctx')  49.7 us
    psum x1, waiting for transfers between devices, local(): expert_sum = lax.psum(expert_part.astype(jnp.bfloat16), 'ctx')  48.1 us
    all_gather x1, waiting for transfers between devices, local(): lax.all_gather(jnp.concatenate([key_used, value_used], axis=1), 'ctx', ax...  25.4 us
    dot_general x1, matrix products, update(): jnp.einsum('kqsr,rkd->kqsd', weights.astype(jnp.bfloat16), value_piece, p...  24.6 us
    reduce_sum x1, other arithmetic, update(): new_sum = running_sum * decay + jnp.sum(weights, axis=-1)  22 us
  transfers between devices with their start and end apart: 6, of which 6 were waited for; matrix products, arithmetic and copies ran while one was open for 2% of the time, Pallas kernels for 0%

profile of v1, /device:TPU:0, one launch (start us, length us, event | category | flops | bytes accessed | tf_op | source)
XLA Modules:
  0.0 549.5 jit_solution(17282798978934206464)
XLA Ops:
  6.5 1.1 constant_dynamic-slice_fusion
  7.9 0.8 pad_maximum_fusion
  8.8 25.4 %all-gather.3.cloned.1.call-done = bf16[2048,512]{0,1:T(8,128)(2,1)} async-done(((bf16[512,512]{0,1:T(8,128)(2,1)}), bf16[2048,512]{0,1:T(8,128)(2,1)}) %all-gather.3.cloned.1.call-update) | async-done | bytes 2097168 | tf_op jit(solution)/shard_map/all_gather | solution.py:80
  34.2 74.9 %conditional.1 = (f32[2,6,512]{2,1,0:T(8,128)S(1)}, f32[2,6,512,128]{2,3,1,0:T(8,128)S(1)}) conditional(s32[]{:T(128)} %convert_element_type.56, (s32[]{:T(128)}, s32[512]{0:T(512)S(1)}, bf16[2048,512]{0,1:T(8,128)(2,1)}, bf16[512,1536]{1,0:T(8,128)(2,1)}) %tuple.13, () %tuple.14), branch_computations={%region_0.3_spmd, %region_3.4_spmd} | conditional | flops 6607870464 | bytes 180058160 | solution.py:113
  34.2 0.8 iota_compare_fusion
  35.1 3.1 fusion.34
  38.2 1.7 copy.55
  39.9 20.2 %fusion = (f32[2,6,512]{2,1,0:T(8,128)S(1)}, f32[2,2048,512,6]{2,1,3,0:T(8,128)}) fusion(pred[512,2048]{0,1:T(8,128)(4,1)S(1)} %iota_compare_fusion, bf16[2048,2,128,1]{0,2,3,1:T(8,128)(2,1)} %bitcast.44, bf16[512,2,6,128]{0,3,2,1:T(8,128)(2,1)S(1)} %bitcast.43), kind=kOutput, calls=%fused_computation.5 | convolution fusion | flops 3258968064 | bytes 54026240 | tf_op jit(solution)/shard_map/cond/branch_0_fun/skqd,rkd->kqsr/dot_general | solution.py:93
  60.1 22.0 %fusion.2 = f32[2,6,512]{2,1,0:T(8,128)S(1)} fusion(f32[2,2048,512,6]{2,1,3,0:T(8,128)} %get-tuple-element.57, f32[2,6,512]{2,1,0:T(8,128)S(1)} %get-tuple-element.56, pred[512,2048]{0,1:T(8,128)(4,1)S(1)} %iota_compare_fusion), kind=kLoop, calls=%fused_computation.7 | loop fusion | flops 62908416 | bytes 51429376 | tf_op jit(solution)/shard_map/cond/branch_0_fun/reduce_sum | solution.py:104
  82.2 24.6 %fusion.6 = f32[2,6,512,128]{3,2,1,0:T(8,128)} fusion(bf16[2048,2,128,1]{0,2,3,1:T(8,128)(2,1)S(1)} %bitcast.46, f32[2,2048,512,6]{2,1,3,0:T(8,128)} %get-tuple-element.57, f32[2,6,512]{2,1,0:T(8,128)S(1)} %get-tuple-element.56, pred[512,2048]{0,1:T(8,128)(4,1)S(1)} %iota_compare_fusion, f32[2,6,512]{2,1,0:T(8,128)S(1)} %get-tuple-element.54), kind=kOutput, calls=%fused_computation.11 | convolution fusion | flops 3284926464 | bytes 55623680 | tf_op jit(solution)/shard_map/cond/branch_0_fun/kqsr,rkd->kqsd/dot_general | solution.py:105
  106.8 2.4 copy.71
  109.1 0.5 divide_convert_fusion
  109.6 15.9 %convolution_convert_fusion = bf16[512,6144]{1,0:T(8,128)(2,1)} fusion(bf16[512,1536]{0,1:T(8,128)(2,1)S(1)} %bitcast.45, bf16[1536,6144]{1,0:T(8,128)(2,1)} %param.18), kind=kOutput, calls=%fused_computation.18 | convolution fusion | flops 9666822144 | bytes 26738688 | tf_op jit(solution)/shard_map/dot_general | solution.py:122
  125.6 0.6 copy-done.5
  126.4 110.1 %reduce-scatter.5.cloned.1.call-done = bf16[512,1536]{1,0:T(8,128)(2,1)} async-done(((bf16[512,6144]{1,0:T(8,128)(2,1)}), bf16[512,1536]{1,0:T(8,128)(2,1)}) %reduce-scatter.5.cloned.1.call-update) | async-done | bytes 1572880 | tf_op jit(solution)/shard_map/reduce_scatter | solution.py:123
  236.5 5.4 scatter_custom_fusion
  242.2 49.7 %all-reduce.4.cloned.1.call-done = bf16[640,1536]{1,0:T(8,128)(2,1)} async-done(((bf16[640,1536]{1,0:T(8,128)(2,1)}), bf16[640,1536]{1,0:T(8,128)(2,1)}) %all-reduce.4.cloned.1.call-update) | async-done | bytes 1966096 | tf_op jit(solution)/shard_map/psum | solution.py:138
  291.8 2.3 fusion.22
  295.0 7.7 %convolution_convert_fusion.2 = bf16[640,2048]{1,0:T(8,128)(2,1)S(1)} fusion(bf16[1536,2048]{1,0:T(8,128)(2,1)} %param.22, bf16[640,1536]{1,0:T(8,128)(2,1)} %all-reduce.4.cloned.1.call-done, f32[1536]{0:T(1024)S(1)} %convert_element_type.65), kind=kOutput, calls=%fused_computation.24 | convolution fusion | flops 4030791680 | bytes 10885120 | tf_op jit(solution)/shard_map/dot_general | solution.py:143
  302.7 8.3 %convolution_convert_fusion.3 = bf16[640,2048]{1,0:T(8,128)(2,1)} fusion(bf16[1536,2048]{1,0:T(8,128)(2,1)} %param.21, bf16[640,1536]{1,0:T(8,128)(2,1)S(1)} %copy-done.3, f32[1536]{0:T(1024)S(1)} %convert_element_type.65), kind=kOutput, calls=%fused_computation.25 | convolution fusion | flops 4030791680 | bytes 10885120 | tf_op jit(solution)/shard_map/dot_general | solution.py:142
  311.1 8.5 %concatenate.11 = bf16[640,4224]{1,0:T(8,128)(2,1)} concatenate(bf16[640,2048]{1,0:T(8,128)(2,1)} %convolution_convert_fusion.3, bf16[640,2048]{1,0:T(8,128)(2,1)S(1)} %convolution_convert_fusion.2, bf16[640,8]{1,0:T(8,128)(2,1)S(1)} %copy.57, bf16[640,1]{1,0:T(8,128)(2,1)S(1)} %broadcast_in_dim.100, bf16[640,119]{1,0:T(8,128)(2,1)S(1)} %broadcast_in_dim.94), dimensions={1} | concatenate | bytes 10813440 | tf_op jit(solution)/shard_map/concatenate | solution.py:148
  319.7 8.0 %scatter_custom_fusion.1 = s32[640]{0:T(1024)S(1)} fusion(s32[2048]{0:T(1024)S(1)} %bitcast.50, s32[2048]{0:T(1024)S(1)} %get-tuple-element.46, s32[]{:T(128)} %constant.35.clone.1), kind=kCustom, calls=%fused_computation.50 | custom fusion | bytes 2564 | tf_op jit(solution)/shard_map/scatter | solution.py:26
  327.8 88.5 %reduce-scatter.7.cloned.1.call-done = bf16[160,4224]{1,0:T(8,128)(2,1)} async-done(((bf16[640,4224]{1,0:T(8,128)(2,1)}), bf16[160,4224]{1,0:T(8,128)(2,1)}) %reduce-scatter.7.cloned.1.call-update) | async-done | bytes 1351696
  416.3 2.6 copy.70
  419.3 0.7 fusion.17
  419.9 1.2 copy.60
  421.5 55.1 %all-gather.5.cloned.1.call-done = bf16[640,2048]{1,0:T(8,128)(2,1)} async-done(((bf16[160,2048]{1,0:T(8,128)(2,1)}), bf16[640,2048]{1,0:T(8,128)(2,1)}) %all-gather.5.cloned.1.call-update) | async-done | bytes 2621456 | tf_op jit(solution)/shard_map/all_gather | solution.py:167
  476.6 9.1 %convolution_convert_fusion.1 = bf16[640,1536]{1,0:T(8,128)(2,1)} fusion(bf16[640,2048]{1,0:T(8,128)(2,1)} %all-gather.5.cloned.1.call-done, bf16[2048,1536]{1,0:T(8,128)(2,1)} %param.23), kind=kOutput, calls=%fused_computation.23 | convolution fusion | flops 4027514880 | bytes 10878976 | tf_op jit(solution)/shard_map/dot_general | solution.py:168
  485.8 48.1 %all-reduce.6.cloned.1.call-done = bf16[640,1536]{1,0:T(8,128)(2,1)} async-done(((bf16[640,1536]{1,0:T(8,128)(2,1)}), bf16[640,1536]{1,0:T(8,128)(2,1)}) %all-reduce.6.cloned.1.call-update) | async-done | bytes 1966096 | tf_op jit(solution)/shard_map/psum | solution.py:169
  533.9 1.7 concatenate.12
  535.5 2.9 gather_fusion
  538.5 4.2 add_convert_fusion
  (47 shorter events, 2.7 us)
Async XLA Ops:
  6.5 285.3 %copy-start = (bf16[1536,8]{0,1:T(8,128)(2,1)S(1)}, bf16[1536,8]{0,1:T(8,128)(2,1)}, u32[]{:S(2)}) copy-start(bf16[1536,8]{0,1:T(8,128)(2,1)} %param.20) | copy-start | bytes 73732
  6.5 27.7 %all-gather.3.cloned.1.call-start = ((), (), s32[]{:S(2)}) async-start(), calls=%async_computation.2 | async-start | bytes 2621440 | tf_op jit(solution)/shard_map/all_gather | solution.py:80
  8.8 227.7 %reduce-scatter.5.cloned.1.call-start = ((), (), s32[]{:S(2)}) async-start(), calls=%async_computation.3 | async-start | bytes 7864320 | tf_op jit(solution)/shard_map/reduce_scatter | solution.py:123
  60.1 22.1 %copy-start.4 = (bf16[2048,256]{0,1:T(8,128)(2,1)S(1)}, bf16[2048,256]{0,1:T(8,128)(2,1)}, u32[]{:S(2)}) copy-start(bf16[2048,256]{0,1:T(8,128)(2,1)} %get-tuple-element.52) | copy-start | bytes 3145732 | tf_op jit(solution)/shard_map/cond
  125.5 0.7 copy-start.5
  125.5 0.7 copy-start.6
  125.5 111.0 %copy-start.1 = (bf16[512,1536]{1,0:T(8,128)(2,1)S(1)}, bf16[512,1536]{1,0:T(8,128)(2,1)}, u32[]{:S(2)}) copy-start(bf16[512,1536]{1,0:T(8,128)(2,1)} %param.17) | copy-start | bytes 4718596
  125.5 166.3 %all-reduce.4.cloned.1.call-start = ((), (), s32[]{:S(2)}) async-start(), calls=%async_computation.4 | async-start | bytes 3932160 | tf_op jit(solution)/shard_map/psum | solution.py:138
  126.4 115.8 %copy-start.7 = (bf16[1536]{0:T(1024)(128)(2,1)S(1)}, bf16[1536]{0:T(1024)(128)(2,1)}, u32[]{:S(2)}) copy-start(bf16[1536]{0:T(1024)(128)(2,1)} %param.19) | copy-start | bytes 9220
  241.9 174.4 %reduce-scatter.7.cloned.1.call-start = ((), (), s32[]{:S(2)}) async-start(), calls=%async_computation.7 | async-start | bytes 6758400
  291.8 2.5 copy-start.2
  295.0 7.8 %copy-start.3 = (bf16[640,1536]{1,0:T(8,128)(2,1)S(1)}, bf16[640,1536]{1,0:T(8,128)(2,1)}, u32[]{:S(2)}) copy-start(bf16[640,1536]{1,0:T(8,128)(2,1)} %all-reduce.4.cloned.1.call-done) | copy-start | bytes 5898244
  319.6 157.0 %all-gather.5.cloned.1.call-start = ((), (), s32[]{:S(2)}) async-start(), calls=%async_computation.5 | async-start | bytes 3276800 | tf_op jit(solution)/shard_map/all_gather | solution.py:167
  421.2 112.7 %all-reduce.6.cloned.1.call-start = ((), (), s32[]{:S(2)}) async-start(), calls=%async_computation.6 | async-start | bytes 3932160 | tf_op jit(solution)/shard_map/psum | solution.py:169
Sparse Core Ops, SparseCore 0:
  8.9 25.2 all-gather.2
  125.6 110.7 reduce-scatter.4
  242.0 49.7 all-reduce.3
  319.7 96.5 reduce-scatter.6
  421.3 55.2 all-gather.4
  485.8 48.0 all-reduce.5

commit v2 on v1

--- a/solution.py
+++ b/solution.py
@@ -1,8 +1,11 @@
+import functools
 import math
 
 import jax
 import jax.numpy as jnp
 from jax import lax
+from jax.experimental import pallas as pl
+from jax.experimental.pallas import tpu as pltpu
 from jax.sharding import PartitionSpec as P
 
 D = 6144
@@ -37,6 +40,61 @@
     )
     mixing = jax.nn.sigmoid(logit_value[:, 0] - partner_logit)
     return (jax.nn.silu(gate_value) * up_value * mixing[:, None]).astype(jnp.bfloat16)
+
+
+def attention_kernel(offset_ref, q_ref, k_ref, v_ref, o_ref, *, per_shared, block_q, scale):
+    seq = k_ref.shape[0]
+    first = offset_ref[0] + pl.program_id(1) * block_q
+    rows = first + lax.broadcasted_iota(jnp.int32, (block_q, seq), 0)
+    cols = lax.broadcasted_iota(jnp.int32, (block_q, seq), 1)
+    allowed = cols <= rows
+    keys = k_ref[...]
+    values = v_ref[...]
+    for head in range(per_shared):
+        query = q_ref[:, head * HEAD_SIZE : (head + 1) * HEAD_SIZE]
+        scores = (
+            lax.dot_general(
+                query, keys, (((1,), (1,)), ((), ())), preferred_element_type=jnp.float32
+            )
+            * scale
+        )
+        masked = jnp.where(allowed, scores, NEG_FILL)
+        row_max = jnp.max(masked, axis=1, keepdims=True)
+        weights = jnp.exp(masked - row_max)
+        total = jnp.sum(weights, axis=1, keepdims=True)
+        acc = jnp.dot(weights.astype(jnp.bfloat16), values, preferred_element_type=jnp.float32)
+        o_ref[:, head * HEAD_SIZE : (head + 1) * HEAD_SIZE] = (acc / total).astype(o_ref.dtype)
+
+
+def attend(queries, packed_kv, offset, shared_heads, per_shared, interpret=False):
+    rows_local = queries.shape[0]
+    seq = packed_kv.shape[0]
+    block_q = 256 if seq <= 2048 else 128
+    block_q = min(block_q, rows_local)
+    width = per_shared * HEAD_SIZE
+    kernel = functools.partial(
+        attention_kernel,
+        per_shared=per_shared,
+        block_q=block_q,
+        scale=1.0 / math.sqrt(HEAD_SIZE),
+    )
+    grid_spec = pltpu.PrefetchScalarGridSpec(
+        num_scalar_prefetch=1,
+        grid=(shared_heads, rows_local // block_q),
+        in_specs=[
+            pl.BlockSpec((block_q, width), lambda g, b, off: (b, g)),
+            pl.BlockSpec((seq, HEAD_SIZE), lambda g, b, off: (0, g)),
+            pl.BlockSpec((seq, HEAD_SIZE), lambda g, b, off: (0, shared_heads + g)),
+        ],
+        out_specs=pl.BlockSpec((block_q, width), lambda g, b, off: (b, g)),
+    )
+    return pl.pallas_call(
+        kernel,
+        grid_spec=grid_spec,
+        out_shape=jax.ShapeDtypeStruct((rows_local, shared_heads * width), jnp.bfloat16),
+        compiler_params=pltpu.CompilerParams(vmem_limit_bytes=48 * 1024 * 1024),
+        interpret=interpret,
+    )(offset, queries, packed_kv, packed_kv)
 
 
 def local(
@@ -68,57 +126,11 @@
     value_used = lax.dynamic_slice_in_dim(
         value_head_rows, first_shared * HEAD_SIZE, shared_heads * HEAD_SIZE, 1
     )
-    query_blocks = queries.reshape(rows_local, shared_heads, per_shared, HEAD_SIZE)
-    query_pos = ctx_index * rows_local + jnp.arange(rows_local, dtype=jnp.int32)
-    last_query = ctx_index * rows_local + rows_local - 1
-    scale_factor = 1.0 / math.sqrt(HEAD_SIZE)
-    start_state = (
-        jnp.full((shared_heads, per_shared, rows_local), -jnp.inf, jnp.float32),
-        jnp.zeros((shared_heads, per_shared, rows_local), jnp.float32),
-        jnp.zeros((shared_heads, per_shared, rows_local, HEAD_SIZE), jnp.float32),
-    )
     packed_kv = lax.all_gather(
         jnp.concatenate([key_used, value_used], axis=1), "ctx", axis=0, tiled=True
     )
-    pieces = (
-        packed_kv[:, : shared_heads * HEAD_SIZE],
-        packed_kv[:, shared_heads * HEAD_SIZE :],
-    )
-
-    def update(state):
-        running_max, running_sum, running_acc = state
-        key_piece = pieces[0].reshape(-1, shared_heads, HEAD_SIZE)
-        value_piece = pieces[1].reshape(-1, shared_heads, HEAD_SIZE)
-        scores = (
-            jnp.einsum(
-                "skqd,rkd->kqsr", query_blocks, key_piece, preferred_element_type=jnp.float32
-            )
-            * scale_factor
-        )
-        key_pos = jnp.arange(key_piece.shape[0], dtype=jnp.int32)
-        allowed = (key_pos[None, :] <= query_pos[:, None])[None, None, :, :]
-        masked = jnp.where(allowed, scores, NEG_FILL)
-        new_max = jnp.max(masked, axis=-1)
-        weights = jnp.where(allowed, jnp.exp(masked - new_max[..., None]), 0.0)
-        decay = jnp.exp(running_max - new_max)
-        new_sum = running_sum * decay + jnp.sum(weights, axis=-1)
-        added = jnp.einsum(
-            "kqsr,rkd->kqsd",
-            weights.astype(jnp.bfloat16),
-            value_piece,
-            preferred_element_type=jnp.float32,
-        )
-        return (new_max, new_sum, running_acc * decay[..., None] + added)
-
-    final_max, final_sum, final_acc = lax.cond(
-        jnp.int32(0) > last_query, lambda state: state, update, start_state
-    )
-    attended = final_acc / final_sum[..., None]
-    attended = (
-        jnp.transpose(attended, (2, 0, 1, 3))
-        .reshape(rows_local, heads_local * HEAD_SIZE)
-        .astype(jnp.bfloat16)
-    )
+    offset = jnp.reshape(ctx_index * rows_local, (1,)).astype(jnp.int32)
+    attended = attend(queries, packed_kv, offset, shared_heads, per_shared)
     partial_out = jnp.dot(attended, out_weight, preferred_element_type=jnp.float32)
     head_sum = lax.psum_scatter(
         partial_out.astype(jnp.bfloat16), "wide", scatter_dimension=1, tiled=True

time: 550 us -> 497 us (0.904)
  matrix products: 88.1 us -> 39.9 us
  other arithmetic: 35.6 us -> 12.2 us
  Pallas kernels: 0 us -> 23.3 us
    dot_general x2 -> x0, matrix products: 44.8 us -> none  [the longest x1 24.6 us: update(): jnp.einsum('kqsr,rkd->kqsd', weights.astype(jnp.bfloat16), value_piece, p...]
    pallas_call x0 -> x1, Pallas kernels: none -> 23.3 us  [attend(): pl.pallas_call(kernel, grid_spec=grid_spec, out_shape=jax.ShapeDtypeStruc...]
    reduce_sum x1 -> x0, other arithmetic: 22 us -> none  [update(): new_sum = running_sum * decay + jnp.sum(weights, axis=-1)]
where the time goes in v2:
time: 497 us
  waiting for transfers between devices  377 us (76%)
  matrix products  39.9 us (8%)
  local copies, waits for them, and re-layouts  29.6 us (6%)
  Pallas kernels  23.3 us (5%)
  between operations  13.7 us (3%)
  other arithmetic  12.2 us (2%)
    reduce_scatter x1, waiting for transfers between devices, local(): lax.psum_scatter(partial_out.astype(jnp.bfloat16), 'wide', scatter_dimens...  110 us
    unnamed x7, waiting for transfers between devices  88.6 us
    all_gather x1, waiting for transfers between devices, local(): hidden = lax.all_gather(hidden_chunk, 'wide', axis=0, tiled=True)  55.1 us
    psum x1, waiting for transfers between devices, local(): buffer = lax.psum(own_rows, 'ctx')  49.9 us
    psum x1, waiting for transfers between devices, local(): expert_sum = lax.psum(expert_part.astype(jnp.bfloat16), 'ctx')  48.1 us
    all_gather x1, waiting for transfers between devices, local(): lax.all_gather(jnp.concatenate([key_used, value_used], axis=1), 'ctx', ax...  25.6 us
    pallas_call x1, Pallas kernels, attend(): pl.pallas_call(kernel, grid_spec=grid_spec, out_shape=jax.ShapeDtypeStruc...  23.3 us
    dot_general x1, matrix products, local(): jnp.dot(attended, out_weight, preferred_element_type=jnp.float32)  15.4 us
  transfers between devices with their start and end apart: 6, of which 6 were waited for; matrix products, arithmetic and copies ran while one was open for 2% of the time, Pallas kernels for 0%

profile of v2, /device:TPU:0, one launch (start us, length us, event | category | flops | bytes accessed | tf_op | source)
XLA Modules:
  0.0 496.6 jit_solution(14408629881831844156)
XLA Ops:
  6.5 1.2 constant_dynamic-slice_fusion
  7.7 0.8 pad_maximum_fusion
  8.6 25.6 %all-gather.3.cloned.1.call-done.k_ref.v_ref = bf16[2048,512]{1,0:T(8,128)(2,1)} async-done(((bf16[512,512]{1,0:T(8,128)(2,1)}), bf16[2048,512]{1,0:T(8,128)(2,1)}) %all-gather.3.cloned.1.call-update) | async-done | bytes 2097168 | tf_op jit(solution)/shard_map/all_gather | solution.py:129
  34.2 1.6 copy-done.2
  35.8 23.3 %shard_map.118 = bf16[512,1536]{1,0:T(8,128)(2,1)S(1)} custom-call(s32[1]{0:T(128)} %bitcast.offset_ref, bf16[512,1536]{1,0:T(8,128)(2,1)S(1)} %copy-done.3, bf16[2048,512]{1,0:T(8,128)(2,1)S(1)} %copy-done.2, bf16[2048,512]{1,0:T(8,128)(2,1)S(1)} %copy-done.2), custom_call_target="tpu_custom_call" | custom-call | tf_op jit(solution)/shard_map/pallas_call | solution.py:91
  59.1 15.4 %convolution_convert_fusion = bf16[512,6144]{1,0:T(8,128)(2,1)} fusion(bf16[512,1536]{1,0:T(8,128)(2,1)S(1)} %shard_map.118, bf16[1536,6144]{1,0:T(8,128)(2,1)} %param.16), kind=kOutput, calls=%fused_computation.3 | convolution fusion | flops 9666822144 | bytes 26738688 | tf_op jit(solution)/shard_map/dot_general | solution.py:134
  74.6 0.2 all-reduce.4.cloned.1.call-start
  74.8 0.5 copy-done.7
  75.5 110.1 %reduce-scatter.5.cloned.1.call-done = bf16[512,1536]{1,0:T(8,128)(2,1)} async-done(((bf16[512,6144]{1,0:T(8,128)(2,1)}), bf16[512,1536]{1,0:T(8,128)(2,1)}) %reduce-scatter.5.cloned.1.call-update) | async-done | bytes 1572880 | tf_op jit(solution)/shard_map/reduce_scatter | solution.py:135
  185.6 5.4 %scatter_custom_fusion = bf16[640,1536]{1,0:T(8,128)(2,1)} fusion(s32[512]{0:T(512)S(1)} %compare_select_fusion.2, bf16[]{:T(256)} %constant.35.clone.1, bf16[512,1536]{1,0:T(8,128)(2,1)} %reduce-scatter.5.cloned.1.call-done, bf16[512,1536]{1,0:T(8,128)(2,1)S(1)} %copy-done.4), kind=kCustom, calls=%fused_computation.20 | custom fusion | flops 3145728 | bytes 5111810 | tf_op jit(solution)/shard_map/scatter | solution.py:147
  191.0 49.9 %all-reduce.4.cloned.1.call-done = bf16[640,1536]{1,0:T(8,128)(2,1)} async-done(((bf16[640,1536]{1,0:T(8,128)(2,1)}), bf16[640,1536]{1,0:T(8,128)(2,1)}) %all-reduce.4.cloned.1.call-update) | async-done | bytes 1966096 | tf_op jit(solution)/shard_map/psum | solution.py:150
  240.9 2.3 fusion.9
  243.2 0.2 copy.22
  243.4 0.5 fusion.1
  243.9 0.2 broadcast_in_dim.63
  244.1 0.9 copy-done.6
  245.0 7.5 %convolution_convert_fusion.2 = bf16[640,2048]{1,0:T(8,128)(2,1)S(1)} fusion(bf16[1536,2048]{1,0:T(8,128)(2,1)} %param.20, bf16[640,1536]{1,0:T(8,128)(2,1)S(1)} %copy-done.6, f32[1536]{0:T(1024)S(1)} %convert_element_type.46), kind=kOutput, calls=%fused_computation.9 | convolution fusion | flops 4030791680 | bytes 10885120 | tf_op jit(solution)/shard_map/dot_general | solution.py:155
  252.5 5.6 %convolution_convert_fusion.3 = bf16[640,2048]{1,0:T(8,128)(2,1)} fusion(bf16[1536,2048]{1,0:T(8,128)(2,1)S(1)} %bitcast.23, bf16[640,1536]{1,0:T(8,128)(2,1)S(1)} %copy-done.6, f32[1536]{0:T(1024)S(1)} %convert_element_type.46), kind=kOutput, calls=%fused_computation.10 | convolution fusion | flops 4030791680 | bytes 10885120 | tf_op jit(solution)/shard_map/dot_general | solution.py:154
  258.1 8.5 %concatenate.11 = bf16[640,4224]{1,0:T(8,128)(2,1)} concatenate(bf16[640,2048]{1,0:T(8,128)(2,1)} %convolution_convert_fusion.3, bf16[640,2048]{1,0:T(8,128)(2,1)S(1)} %convolution_convert_fusion.2, bf16[640,8]{1,0:T(8,128)(2,1)S(1)} %copy.22, bf16[640,1]{1,0:T(8,128)(2,1)S(1)} %broadcast_in_dim.63, bf16[640,119]{1,0:T(8,128)(2,1)S(1)} %broadcast_in_dim.57), dimensions={1} | concatenate | bytes 10813440 | tf_op jit(solution)/shard_map/concatenate | solution.py:160
  266.8 8.0 %scatter_custom_fusion.1 = s32[640]{0:T(1024)S(1)} fusion(s32[2048]{0:T(1024)S(1)} %bitcast.19, s32[2048]{0:T(1024)S(1)} %get-tuple-element.5, s32[]{:T(128)} %constant.23.clone.1), kind=kCustom, calls=%fused_computation.34 | custom fusion | bytes 2564 | tf_op jit(solution)/shard_map/scatter | solution.py:29
  274.9 88.5 %reduce-scatter.7.cloned.1.call-done = bf16[160,4224]{1,0:T(8,128)(2,1)} async-done(((bf16[640,4224]{1,0:T(8,128)(2,1)}), bf16[160,4224]{1,0:T(8,128)(2,1)}) %reduce-scatter.7.cloned.1.call-update) | async-done | bytes 1351696
  363.4 2.6 copy.27
  365.9 0.3 convert_element_type.48
  366.3 0.7 fusion.4
  367.0 1.2 copy.25
  368.2 0.3 all-reduce.6.cloned.1.call-start
  368.5 55.1 %all-gather.5.cloned.1.call-done = bf16[640,2048]{1,0:T(8,128)(2,1)} async-done(((bf16[160,2048]{1,0:T(8,128)(2,1)}), bf16[640,2048]{1,0:T(8,128)(2,1)}) %all-gather.5.cloned.1.call-update) | async-done | bytes 2621456 | tf_op jit(solution)/shard_map/all_gather | solution.py:179
  423.6 9.1 %convolution_convert_fusion.1 = bf16[640,1536]{1,0:T(8,128)(2,1)} fusion(bf16[640,2048]{1,0:T(8,128)(2,1)} %all-gather.5.cloned.1.call-done, bf16[2048,1536]{1,0:T(8,128)(2,1)} %param.21), kind=kOutput, calls=%fused_computation.8 | convolution fusion | flops 4027514880 | bytes 10878976 | tf_op jit(solution)/shard_map/dot_general | solution.py:180
  432.8 48.1 %all-reduce.6.cloned.1.call-done = bf16[640,1536]{1,0:T(8,128)(2,1)} async-done(((bf16[640,1536]{1,0:T(8,128)(2,1)}), bf16[640,1536]{1,0:T(8,128)(2,1)}) %all-reduce.6.cloned.1.call-update) | async-done | bytes 1966096 | tf_op jit(solution)/shard_map/psum | solution.py:181
  480.9 1.7 concatenate.12
  482.6 2.9 gather_fusion
  485.6 4.2 add_convert_fusion
  (43 shorter events, 0.7 us)
Async XLA Ops:
  6.5 234.4 %copy-start = (bf16[1536,8]{0,1:T(8,128)(2,1)S(1)}, bf16[1536,8]{0,1:T(8,128)(2,1)}, u32[]{:S(2)}) copy-start(bf16[1536,8]{0,1:T(8,128)(2,1)} %param.18) | copy-start | bytes 73732
  6.5 27.7 %copy-start.3 = (bf16[512,1536]{1,0:T(8,128)(2,1)S(1)}, bf16[512,1536]{1,0:T(8,128)(2,1)}, u32[]{:S(2)}) copy-start(bf16[512,1536]{1,0:T(8,128)(2,1)} %q_ref.1) | copy-start | bytes 4718596
  6.5 27.7 %all-gather.3.cloned.1.call-start = ((), (), s32[]{:S(2)}) async-start(), calls=%async_computation.2 | async-start | bytes 2621440 | tf_op jit(solution)/shard_map/all_gather | solution.py:129
  8.6 177.0 %reduce-scatter.5.cloned.1.call-start = ((), (), s32[]{:S(2)}) async-start(), calls=%async_computation.3 | async-start | bytes 7864320 | tf_op jit(solution)/shard_map/reduce_scatter | solution.py:135
  34.2 1.6 copy-start.2
  74.6 0.7 copy-start.7
  74.6 0.7 copy-start.8
  74.6 111.0 %copy-start.4 = (bf16[512,1536]{1,0:T(8,128)(2,1)S(1)}, bf16[512,1536]{1,0:T(8,128)(2,1)}, u32[]{:S(2)}) copy-start(bf16[512,1536]{1,0:T(8,128)(2,1)} %param.15) | copy-start | bytes 4718596
  74.6 166.3 %all-reduce.4.cloned.1.call-start = ((), (), s32[]{:S(2)}) async-start(), calls=%async_computation.4 | async-start | bytes 3932160 | tf_op jit(solution)/shard_map/psum | solution.py:150
  75.5 115.6 %copy-start.9 = (bf16[1536]{0:T(1024)(128)(2,1)S(1)}, bf16[1536]{0:T(1024)(128)(2,1)}, u32[]{:S(2)}) copy-start(bf16[1536]{0:T(1024)(128)(2,1)} %param.17) | copy-start | bytes 9220
  191.0 172.4 %reduce-scatter.7.cloned.1.call-start = ((), (), s32[]{:S(2)}) async-start(), calls=%async_computation.7 | async-start | bytes 6758400
  240.9 2.5 copy-start.5
  243.4 1.5 copy-start.6
  243.4 9.1 %slice-start = ((s8[6291456]{0:T(1024)(128)(4,1)}), s8[4194304]{0:T(1024)(128)(4,1)S(1)}, s32[]{:S(2)}) async-start(s8[6291456]{0:T(1024)(128)(4,1)} %bitcast.22), calls=%async_computation.8 | async-start | bytes 8388608
  245.0 7.5 %slice-start.1 = ((s8[6291456]{0:T(1024)(128)(4,1)}), s8[2097152]{0:T(1024)(128)(4,1)S(1)}, s32[]{:S(2)}) async-start(s8[6291456]{0:T(1024)(128)(4,1)} %bitcast.22), calls=%async_computation.9 | async-start | bytes 4194304
  266.7 157.0 %all-gather.5.cloned.1.call-start = ((), (), s32[]{:S(2)}) async-start(), calls=%async_computation.5 | async-start | bytes 3276800 | tf_op jit(solution)/shard_map/all_gather | solution.py:179
  368.2 112.7 %all-reduce.6.cloned.1.call-start = ((), (), s32[]{:S(2)}) async-start(), calls=%async_computation.6 | async-start | bytes 3932160 | tf_op jit(solution)/shard_map/psum | solution.py:181
  485.5 4.2 copy-start.1
Sparse Core Ops, SparseCore 0:
  8.9 25.2 all-gather.2
  74.7 110.7 reduce-scatter.4
  191.1 49.7 all-reduce.3
  266.8 96.5 reduce-scatter.6
  368.4 55.2 all-gather.4
  432.9 48.0 all-reduce.5

commit v3 on v2

--- a/solution.py
+++ b/solution.py
@@ -142,11 +142,11 @@
     wide_count = lax.axis_size("wide")
     chunk = capacity // wide_count
     slot_of_token = token_slots(expert_ids, slot_ids, capacity)
-    slot_other = other_experts(expert_ids, slot_of_token, capacity)
+    partner = jnp.sum(expert_ids, axis=1)
     slot_local = lax.dynamic_slice_in_dim(slot_of_token, ctx_index * rows_local, rows_local)
-    own_rows = jnp.zeros((capacity, width_local), jnp.bfloat16).at[slot_local].set(
-        resid, mode="drop"
-    )
+    slot_ids_all = jnp.arange(capacity, dtype=jnp.int32)
+    place = (slot_ids_all[:, None] == slot_local[None, :]).astype(jnp.bfloat16)
+    own_rows = jnp.dot(place, resid, preferred_element_type=jnp.float32).astype(jnp.bfloat16)
     buffer = lax.psum(own_rows, "ctx")
     buffer_wide = buffer.astype(jnp.float32)
     square_part = jnp.sum(buffer_wide * buffer_wide, axis=1)
@@ -154,35 +154,28 @@
     gate_part = jnp.dot(scaled, gate_weight, preferred_element_type=jnp.float32)
     up_part = jnp.dot(scaled, up_weight, preferred_element_type=jnp.float32)
     logit_part = jnp.dot(scaled, router_weight, preferred_element_type=jnp.float32)
-    hidden_local = gate_part.shape[1]
     experts = logit_part.shape[1]
     pad = 128 - (experts + 1) % 128
-    packed = jnp.concatenate(
-        [
-            gate_part,
-            up_part,
-            logit_part,
-            square_part[:, None],
-            jnp.zeros((capacity, pad), jnp.float32),
-        ],
-        axis=1,
-    ).astype(jnp.bfloat16)
-    reduced = lax.psum_scatter(packed, "wide", scatter_dimension=0, tiled=True).astype(
-        jnp.float32
+    small = jnp.concatenate(
+        [logit_part, square_part[:, None], jnp.zeros((capacity, pad), jnp.float32)], axis=1
     )
-    gate_sum = reduced[:, :hidden_local]
-    up_sum = reduced[:, hidden_local : 2 * hidden_local]
-    logit_sum = reduced[:, 2 * hidden_local : 2 * hidden_local + experts]
-    square_sum = reduced[:, 2 * hidden_local + experts]
-    other_chunk = lax.dynamic_slice_in_dim(slot_other, wide_index * chunk, chunk)
+    gate_sum, up_sum, small_sum = (
+        lax.psum_scatter(part.astype(jnp.bfloat16), "wide", scatter_dimension=0, tiled=True)
+        .astype(jnp.float32)
+        for part in (gate_part, up_part, small)
+    )
+    logit_sum = small_sum[:, :experts]
+    square_sum = small_sum[:, experts]
+    chunk_slots = wide_index * chunk + jnp.arange(chunk, dtype=jnp.int32)
+    other_chunk = jnp.sum(
+        jnp.where(chunk_slots[:, None] == slot_of_token[None, :], partner[None, :], 0), axis=1
+    )
     hidden_chunk = expert_hidden(gate_sum, up_sum, square_sum, logit_sum, other_chunk, D)
     hidden = lax.all_gather(hidden_chunk, "wide", axis=0, tiled=True)
     expert_part = jnp.dot(hidden, down_weight, preferred_element_type=jnp.float32)
     expert_sum = lax.psum(expert_part.astype(jnp.bfloat16), "ctx")
-    expert_pad = jnp.concatenate(
-        [expert_sum, jnp.zeros((1, width_local), jnp.bfloat16)], axis=0
-    )
-    moe_rows = jnp.take(expert_pad, slot_local, axis=0).astype(jnp.float32)
+    pick = (slot_local[:, None] == slot_ids_all[None, :]).astype(jnp.bfloat16)
+    moe_rows = jnp.dot(pick, expert_sum, preferred_element_type=jnp.float32)
     return (resid.astype(jnp.float32) + moe_rows).astype(jnp.bfloat16)
 
 

time: 497 us -> 496 us (level)
  local copies, waits for them, and re-layouts: 29.6 us -> 5.75 us
  waiting for transfers between devices: 377 us -> 396 us
  matrix products: 39.9 us -> 50.4 us
  other arithmetic: 12.2 us -> 6.16 us
    reduce_scatter x0 -> x2, waiting for transfers between devices: none -> 106 us  [local(): lax.psum_scatter(part.astype(jnp.bfloat16), 'wide', scatter_dimension=0,...]
    unnamed x7 -> x9, waiting for transfers between devices: 88.6 us -> 2.82 us
    concatenate x2 -> x1, local copies, waits for them, and re-layouts: 10.2 us -> 0.08 us  [local(): jnp.concatenate([logit_part, square_part[:, None], jnp.zeros((capacity, p...]
    dot_general x0 -> x2, matrix products: none -> 8.18 us  [the longest x1 4.2 us: local(): moe_rows = jnp.dot(pick, expert_sum, preferred_element_type=jnp.float32)]
    scatter x1 -> x0, local copies, waits for them, and re-layouts: 8.04 us -> none  [other_experts(): jnp.zeros((capacity,), jnp.int32).at[slot_of_token]]
    scatter x1 -> x0, other arithmetic: 5.4 us -> none  [local(): jnp.zeros((capacity, width_local), jnp.bfloat16).at[slot_local]]
  transfers between devices with their start and end apart: 6 -> 8, of which waited for: 6 -> 8; matrix products, arithmetic and copies ran while one was open for 2% -> 4% of each run, Pallas kernels for 0% -> 0%
where the time goes in v3:
time: 496 us
  waiting for transfers between devices  396 us (80%)
  matrix products  50.4 us (10%)
  Pallas kernels  23.3 us (5%)
  between operations  13.6 us (3%)
  other arithmetic  6.16 us (1%)
  local copies, waits for them, and re-layouts  5.75 us (1%)
    reduce_scatter x1, waiting for transfers between devices, local(): lax.psum_scatter(partial_out.astype(jnp.bfloat16), 'wide', scatter_dimens...  110 us
    reduce_scatter x2, waiting for transfers between devices, local(): lax.psum_scatter(part.astype(jnp.bfloat16), 'wide', scatter_dimension=0,...  106 us
    all_gather x1, waiting for transfers between devices, local(): hidden = lax.all_gather(hidden_chunk, 'wide', axis=0, tiled=True)  54.4 us
    psum x1, waiting for transfers between devices, local(): buffer = lax.psum(own_rows, 'ctx')  49.2 us
    psum x1, waiting for transfers between devices, local(): expert_sum = lax.psum(expert_part.astype(jnp.bfloat16), 'ctx')  48.2 us
    all_gather x1, waiting for transfers between devices, local(): lax.all_gather(jnp.concatenate([key_used, value_used], axis=1), 'ctx', ax...  25.6 us
    pallas_call x1, Pallas kernels, attend(): pl.pallas_call(kernel, grid_spec=grid_spec, out_shape=jax.ShapeDtypeStruc...  23.3 us
    dot_general x1, matrix products, local(): jnp.dot(attended, out_weight, preferred_element_type=jnp.float32)  15.8 us
  transfers between devices with their start and end apart: 8, of which 8 were waited for; matrix products, arithmetic and copies ran while one was open for 4% of the time, Pallas kernels for 0%

profile of v3, /device:TPU:0, one launch (start us, length us, event | category | flops | bytes accessed | tf_op | source)
XLA Modules:
  0.0 495.5 jit_solution(3837534889072734277)
XLA Ops:
  6.5 1.2 constant_dynamic-slice_fusion
  7.7 0.8 pad_maximum_fusion
  8.6 25.6 %all-gather.3.cloned.1.call-done.k_ref.v_ref = bf16[2048,512]{1,0:T(8,128)(2,1)} async-done(((bf16[512,512]{1,0:T(8,128)(2,1)}), bf16[2048,512]{1,0:T(8,128)(2,1)}) %all-gather.3.cloned.1.call-update) | async-done | bytes 2097168 | tf_op jit(solution)/shard_map/all_gather | solution.py:129
  34.2 1.6 copy-done.2
  35.8 23.3 %shard_map.118 = bf16[512,1536]{1,0:T(8,128)(2,1)S(1)} custom-call(s32[1]{0:T(128)} %bitcast.offset_ref, bf16[512,1536]{1,0:T(8,128)(2,1)S(1)} %copy-done.3, bf16[2048,512]{1,0:T(8,128)(2,1)S(1)} %copy-done.2, bf16[2048,512]{1,0:T(8,128)(2,1)S(1)} %copy-done.2), custom_call_target="tpu_custom_call" | custom-call | tf_op jit(solution)/shard_map/pallas_call | solution.py:91
  59.1 15.8 %convolution_convert_fusion = bf16[512,6144]{1,0:T(8,128)(2,1)} fusion(bf16[512,1536]{1,0:T(8,128)(2,1)S(1)} %shard_map.118, bf16[1536,6144]{1,0:T(8,128)(2,1)} %param.16), kind=kOutput, calls=%fused_computation | convolution fusion | flops 9666822144 | bytes 26738688 | tf_op jit(solution)/shard_map/dot_general | solution.py:134
  75.0 0.6 copy-done.5
  75.7 0.1 fusion.16
  75.7 0.1 dynamic_slice.11
  75.8 110.1 %reduce-scatter.7.cloned.1.call-done = bf16[512,1536]{1,0:T(8,128)(2,1)} async-done(((bf16[512,6144]{1,0:T(8,128)(2,1)}), bf16[512,1536]{1,0:T(8,128)(2,1)}) %reduce-scatter.7.cloned.1.call-update) | async-done | bytes 1572880 | tf_op jit(solution)/shard_map/reduce_scatter | solution.py:135
  185.9 4.0 convolution_convert_fusion.4
  189.9 0.2 reduce-scatter.13.cloned.1.call-start
  190.1 0.4 copy-done.7
  190.6 0.1 pad.2.clone
  190.6 49.2 %all-reduce.3.cloned.1.call-done = bf16[640,1536]{1,0:T(8,128)(2,1)} async-done(((bf16[640,1536]{1,0:T(8,128)(2,1)}), bf16[640,1536]{1,0:T(8,128)(2,1)}) %all-reduce.3.cloned.1.call-update) | async-done | bytes 1966096 | tf_op jit(solution)/shard_map/psum | solution.py:150
  239.8 2.1 fusion.1
  242.0 0.6 fusion.7
  242.6 0.1 maximum_maximum_fusion
  242.7 0.8 copy.14
  243.6 8.3 %convolution_convert_fusion.2 = bf16[640,2048]{1,0:T(8,128)(2,1)} fusion(bf16[1536,2048]{1,0:T(8,128)(2,1)} %param.20, bf16[640,1536]{1,0:T(8,128)(2,1)S(1)} %copy-done.4, f32[1536]{0:T(1024)S(1)} %convert_element_type.61), kind=kOutput, calls=%fused_computation.7 | convolution fusion | flops 4030791680 | bytes 10885120 | tf_op jit(solution)/shard_map/dot_general | solution.py:155
  252.0 8.3 %convolution_convert_fusion.3 = bf16[640,2048]{1,0:T(8,128)(2,1)} fusion(bf16[1536,2048]{1,0:T(8,128)(2,1)} %param.19, bf16[640,1536]{1,0:T(8,128)(2,1)S(1)} %copy-done.4, f32[1536]{0:T(1024)S(1)} %convert_element_type.61), kind=kOutput, calls=%fused_computation.8 | convolution fusion | flops 4030791680 | bytes 10885120 | tf_op jit(solution)/shard_map/dot_general | solution.py:154
  260.3 0.0 all-gather.5.cloned.1.call-start
  260.4 0.3 select_reduce_fusion
  260.7 2.7 reduce-scatter.13.cloned.1.call-done
  263.4 0.9 copy.15
  264.3 51.6 %reduce-scatter.11.cloned.1.call-done = bf16[160,2048]{1,0:T(8,128)(2,1)} async-done(((bf16[640,2048]{1,0:T(8,128)(2,1)}), bf16[160,2048]{1,0:T(8,128)(2,1)}) %reduce-scatter.11.cloned.1.call-update) | async-done | bytes 655376 | tf_op jit(solution)/shard_map/reduce_scatter | solution.py:163
  315.9 54.0 %reduce-scatter.9.cloned.1.call-done = bf16[160,2048]{1,0:T(8,128)(2,1)} async-done(((bf16[640,2048]{1,0:T(8,128)(2,1)}), bf16[160,2048]{1,0:T(8,128)(2,1)}) %reduce-scatter.9.cloned.1.call-update) | async-done | bytes 655376 | tf_op jit(solution)/shard_map/reduce_scatter | solution.py:163
  369.9 2.7 multiply_convert_fusion
  372.6 54.4 %all-gather.5.cloned.1.call-done = bf16[640,2048]{1,0:T(8,128)(2,1)} async-done(((bf16[160,2048]{1,0:T(8,128)(2,1)}), bf16[640,2048]{1,0:T(8,128)(2,1)}) %all-gather.5.cloned.1.call-update) | async-done | bytes 2621456 | tf_op jit(solution)/shard_map/all_gather | solution.py:174
  427.0 9.2 %convolution_convert_fusion.1 = bf16[640,1536]{1,0:T(8,128)(2,1)} fusion(bf16[640,2048]{1,0:T(8,128)(2,1)} %all-gather.5.cloned.1.call-done, bf16[2048,1536]{1,0:T(8,128)(2,1)} %param.21), kind=kOutput, calls=%fused_computation.6 | convolution fusion | flops 4027514880 | bytes 10878976 | tf_op jit(solution)/shard_map/dot_general | solution.py:175
  436.3 48.2 %all-reduce.5.cloned.1.call-done = bf16[640,1536]{1,0:T(8,128)(2,1)} async-done(((bf16[640,1536]{1,0:T(8,128)(2,1)}), bf16[640,1536]{1,0:T(8,128)(2,1)}) %all-reduce.5.cloned.1.call-update) | async-done | bytes 1966096 | tf_op jit(solution)/shard_map/psum | solution.py:176
  484.5 4.2 fusion.2
  (42 shorter events, 0.5 us)
Async XLA Ops:
  6.5 235.4 %copy-start = (bf16[1536,8]{0,1:T(8,128)(2,1)S(1)}, bf16[1536,8]{0,1:T(8,128)(2,1)}, u32[]{:S(2)}) copy-start(bf16[1536,8]{0,1:T(8,128)(2,1)} %param.18) | copy-start | bytes 73732
  6.5 27.7 %copy-start.3 = (bf16[512,1536]{1,0:T(8,128)(2,1)S(1)}, bf16[512,1536]{1,0:T(8,128)(2,1)}, u32[]{:S(2)}) copy-start(bf16[512,1536]{1,0:T(8,128)(2,1)} %q_ref.1) | copy-start | bytes 4718596
  6.5 27.7 %all-gather.3.cloned.1.call-start = ((), (), s32[]{:S(2)}) async-start(), calls=%async_computation.4 | async-start | bytes 2621440 | tf_op jit(solution)/shard_map/all_gather | solution.py:129
  8.6 177.3 %reduce-scatter.7.cloned.1.call-start = ((), (), s32[]{:S(2)}) async-start(), calls=%async_computation.5 | async-start | bytes 7864320 | tf_op jit(solution)/shard_map/reduce_scatter | solution.py:135
  34.2 1.6 copy-start.2
  74.9 0.7 copy-start.5
  74.9 0.7 copy-start.6
  74.9 111.0 %copy-start.8 = (bf16[512,1536]{1,0:T(8,128)(2,1)S(1)}, bf16[512,1536]{1,0:T(8,128)(2,1)}, u32[]{:S(2)}) copy-start(bf16[512,1536]{1,0:T(8,128)(2,1)} %param.15) | copy-start | bytes 4718596
  75.0 164.9 %all-reduce.3.cloned.1.call-start = ((), (), s32[]{:S(2)}) async-start(), calls=%async_computation.6 | async-start | bytes 3932160 | tf_op jit(solution)/shard_map/psum | solution.py:150
  189.9 0.7 copy-start.7
  189.9 73.5 %reduce-scatter.13.cloned.1.call-start = ((), (), s32[]{:S(2)}) async-start(), calls=%async_computation.11 | async-start | bytes 204800
  239.8 2.2 copy-start.4
  243.5 72.3 %reduce-scatter.11.cloned.1.call-start = ((), (), s32[]{:S(2)}) async-start(), calls=%async_computation.8 | async-start | bytes 3276800 | tf_op jit(solution)/shard_map/reduce_scatter | solution.py:163
  251.9 117.9 %reduce-scatter.9.cloned.1.call-start = ((), (), s32[]{:S(2)}) async-start(), calls=%async_computation.7 | async-start | bytes 3276800 | tf_op jit(solution)/shard_map/reduce_scatter | solution.py:163
  260.3 166.7 %all-gather.5.cloned.1.call-start = ((), (), s32[]{:S(2)}) async-start(), calls=%async_computation.9 | async-start | bytes 3276800 | tf_op jit(solution)/shard_map/all_gather | solution.py:174
  372.6 111.9 %all-reduce.5.cloned.1.call-start = ((), (), s32[]{:S(2)}) async-start(), calls=%async_computation.10 | async-start | bytes 3932160 | tf_op jit(solution)/shard_map/psum | solution.py:176
  427.0 57.4 %copy-start.10 = (bf16[512,1536]{1,0:T(8,128)(2,1)S(1)}, bf16[512,1536]{1,0:T(8,128)(2,1)}, u32[]{:S(2)}) copy-start(bf16[512,1536]{1,0:T(8,128)(2,1)} %reduce-scatter.7.cloned.1.call-done) | copy-start | bytes 4718596
  436.2 48.2 %copy-start.9 = (bf16[512,1536]{1,0:T(8,128)(2,1)S(1)}, bf16[512,1536]{1,0:T(8,128)(2,1)}, u32[]{:S(2)}) copy-start(bf16[512,1536]{1,0:T(8,128)(2,1)} %param.15) | copy-start | bytes 4718596
  484.5 4.2 copy-start.1
Sparse Core Ops, SparseCore 0:
  8.9 25.2 all-gather.2
  75.1 110.7 reduce-scatter.6
  190.0 49.7 all-reduce.2
  243.7 19.6 reduce-scatter.12
  265.5 50.3 reduce-scatter.10
  318.0 51.7 reduce-scatter.8
  372.7 54.2 all-gather.4
  436.4 48.0 all-reduce.4

commit v4 on v3

--- a/solution.py
+++ b/solution.py
@@ -95,6 +95,56 @@
         compiler_params=pltpu.CompilerParams(vmem_limit_bytes=48 * 1024 * 1024),
         interpret=interpret,
     )(offset, queries, packed_kv, packed_kv)
+
+
+def pair_exchange(x, axis, count, bit):
+    return lax.ppermute(x, axis, perm=[(i, i ^ bit) for i in range(count)])
+
+
+def gather_rows(x, axis):
+    count = lax.axis_size(axis)
+    if count & (count - 1):
+        return lax.all_gather(x, axis, axis=0, tiled=True)
+    index = lax.axis_index(axis)
+    out = x
+    bit = 1
+    while bit < count:
+        other = pair_exchange(out, axis, count, bit)
+        upper = (index // bit) % 2
+        size = out.shape[0]
+        both = jnp.zeros((2 * size,) + out.shape[1:], out.dtype)
+        both = lax.dynamic_update_slice_in_dim(both, out, upper * size, 0)
+        out = lax.dynamic_update_slice_in_dim(both, other, (1 - upper) * size, 0)
+        bit *= 2
+    return out
+
+
+def sum_rows(x, axis):
+    count = lax.axis_size(axis)
+    if count & (count - 1) or x.shape[0] % count:
+        return lax.psum(x.astype(jnp.bfloat16), axis)
+    index = lax.axis_index(axis)
+    acc = x.astype(jnp.float32)
+    bit = 1
+    while bit < count:
+        half = acc.shape[0] // 2
+        upper = (index // bit) % 2
+        keep = lax.dynamic_slice_in_dim(acc, upper * half, half, 0)
+        send = lax.dynamic_slice_in_dim(acc, (1 - upper) * half, half, 0)
+        other = pair_exchange(send.astype(jnp.bfloat16), axis, count, bit)
+        acc = keep + other.astype(jnp.float32)
+        bit *= 2
+    out = acc.astype(jnp.bfloat16)
+    bit = count // 2
+    while bit >= 1:
+        other = pair_exchange(out, axis, count, bit)
+        upper = (index // bit) % 2
+        size = out.shape[0]
+        both = jnp.zeros((2 * size,) + out.shape[1:], out.dtype)
+        both = lax.dynamic_update_slice_in_dim(both, out, upper * size, 0)
+        out = lax.dynamic_update_slice_in_dim(both, other, (1 - upper) * size, 0)
+        bit //= 2
+    return out
 
 
 def local(
@@ -126,9 +176,7 @@
     value_used = lax.dynamic_slice_in_dim(
         value_head_rows, first_shared * HEAD_SIZE, shared_heads * HEAD_SIZE, 1
     )
-    packed_kv = lax.all_gather(
-        jnp.concatenate([key_used, value_used], axis=1), "ctx", axis=0, tiled=True
-    )
+    packed_kv = gather_rows(jnp.concatenate([key_used, value_used], axis=1), "ctx")
     offset = jnp.reshape(ctx_index * rows_local, (1,)).astype(jnp.int32)
     attended = attend(queries, packed_kv, offset, shared_heads, per_shared)
     partial_out = jnp.dot(attended, out_weight, preferred_element_type=jnp.float32)
@@ -146,8 +194,8 @@
     slot_local = lax.dynamic_slice_in_dim(slot_of_token, ctx_index * rows_local, rows_local)
     slot_ids_all = jnp.arange(capacity, dtype=jnp.int32)
     place = (slot_ids_all[:, None] == slot_local[None, :]).astype(jnp.bfloat16)
-    own_rows = jnp.dot(place, resid, preferred_element_type=jnp.float32).astype(jnp.bfloat16)
-    buffer = lax.psum(own_rows, "ctx")
+    own_rows = jnp.dot(place, resid, preferred_element_type=jnp.float32)
+    buffer = sum_rows(own_rows, "ctx")
     buffer_wide = buffer.astype(jnp.float32)
     square_part = jnp.sum(buffer_wide * buffer_wide, axis=1)
     scaled = (buffer_wide * norm_gain.astype(jnp.float32)[None, :]).astype(jnp.bfloat16)
@@ -173,7 +221,7 @@
     hidden_chunk = expert_hidden(gate_sum, up_sum, square_sum, logit_sum, other_chunk, D)
     hidden = lax.all_gather(hidden_chunk, "wide", axis=0, tiled=True)
     expert_part = jnp.dot(hidden, down_weight, preferred_element_type=jnp.float32)
-    expert_sum = lax.psum(expert_part.astype(jnp.bfloat16), "ctx")
+    expert_sum = sum_rows(expert_part, "ctx")
     pick = (slot_local[:, None] == slot_ids_all[None, :]).astype(jnp.bfloat16)
     moe_rows = jnp.dot(pick, expert_sum, preferred_element_type=jnp.float32)
     return (resid.astype(jnp.float32) + moe_rows).astype(jnp.bfloat16)

time: 496 us -> 460 us (0.927)
  waiting for transfers between devices: 396 us -> 355 us
  starting transfers between devices: 0.48 us -> 10.4 us
  matrix products: 50.4 us -> 45.1 us
    psum x2 -> x0, waiting for transfers between devices: 97.4 us -> none  [the longest x1 49.2 us: local(): buffer = lax.psum(own_rows, 'ctx')]
    ppermute x0 -> x10, waiting for transfers between devices: none -> 79.8 us  [pair_exchange(): return lax.ppermute(x, axis, perm=[(i, i ^ bit) for i in range(count)])]
    all_gather x1 -> x0, waiting for transfers between devices: 25.6 us -> none  [local(): lax.all_gather(jnp.concatenate([key_used, value_used], axis=1), 'ctx', ax...]
    ppermute x0 -> x10, starting transfers between devices: none -> 9.87 us  [pair_exchange(): return lax.ppermute(x, axis, perm=[(i, i ^ bit) for i in range(count)])]
  transfers between devices with their start and end apart: 8 -> 15, of which waited for: 8 -> 15; matrix products, arithmetic and copies ran while one was open for 4% -> 4% of each run, Pallas kernels for 0% -> 0%
where the time goes in v4:
time: 460 us
  waiting for transfers between devices  355 us (77%)
  matrix products  45.1 us (10%)
  Pallas kernels  23.4 us (5%)
  between operations  13.5 us (3%)
  starting transfers between devices  10.4 us (2%)
  local copies, waits for them, and re-layouts  6.98 us (2%)
  other arithmetic  6 us (1%)
    reduce_scatter x1, waiting for transfers between devices, local(): lax.psum_scatter(partial_out.astype(jnp.bfloat16), 'wide', scatter_dimens...  112 us
    reduce_scatter x2, waiting for transfers between devices, local(): lax.psum_scatter(part.astype(jnp.bfloat16), 'wide', scatter_dimension=0,...  106 us
    ppermute x10, waiting for transfers between devices, pair_exchange(): return lax.ppermute(x, axis, perm=[(i, i ^ bit) for i in range(count)])  79.8 us
    all_gather x1, waiting for transfers between devices, local(): hidden = lax.all_gather(hidden_chunk, 'wide', axis=0, tiled=True)  54.4 us
    pallas_call x1, Pallas kernels, attend(): pl.pallas_call(kernel, grid_spec=grid_spec, out_shape=jax.ShapeDtypeStruc...  23.4 us
    dot_general x1, matrix products, local(): jnp.dot(attended, out_weight, preferred_element_type=jnp.float32)  15.5 us
    ppermute x10, starting transfers between devices, pair_exchange(): return lax.ppermute(x, axis, perm=[(i, i ^ bit) for i in range(count)])  9.87 us
  transfers between devices with their start and end apart: 15, of which 15 were waited for; matrix products, arithmetic and copies ran while one was open for 4% of the time, Pallas kernels for 0%

profile of v4, /device:TPU:0, one launch (start us, length us, event | category | flops | bytes accessed | tf_op | source)
XLA Modules:
  0.0 460.0 jit_solution(14446871406151381160)
XLA Ops:
  6.5 1.1 constant_dynamic-slice_fusion
  8.3 1.5 collective-permute-done
  9.9 2.9 collective-permute-start.1
  13.1 23.2 %collective-permute-done.1 = bf16[1024,512]{1,0:T(8,128)(2,1)S(1)} collective-permute-done((bf16[1024,512]{1,0:T(8,128)(2,1)S(1)}, bf16[1024,512]{1,0:T(8,128)(2,1)S(1)}, u32[]{:S(2)}, u32[]{:S(2)}) %collective-permute-start.1) | collective-permute-done | bytes 1048608 | tf_op jit(solution)/shard_map/ppermute | solution.py:101
  36.4 23.4 %shard_map.118 = bf16[512,1536]{1,0:T(8,128)(2,1)S(1)} custom-call(s32[1]{0:T(128)} %bitcast.offset_ref, bf16[512,1536]{1,0:T(8,128)(2,1)S(1)} %copy-done.2, bf16[2048,512]{1,0:T(8,128)(2,1)S(1)} %constant_dynamic-update-slice_fusion.8.k_ref.v_ref, bf16[2048,512]{1,0:T(8,128)(2,1)S(1)} %constant_dynamic-update-slice_fusion.8.k_ref.v_ref), custom_call_target="tpu_custom_call" | custom-call | tf_op jit(solution)/shard_map/pallas_call | solution.py:91
  59.8 15.5 %convolution_convert_fusion = bf16[512,6144]{1,0:T(8,128)(2,1)} fusion(bf16[512,1536]{1,0:T(8,128)(2,1)S(1)} %shard_map.118, bf16[1536,6144]{1,0:T(8,128)(2,1)} %param.16), kind=kOutput, calls=%fused_computation | convolution fusion | flops 9666822144 | bytes 26738688 | tf_op jit(solution)/shard_map/dot_general | solution.py:182
  76.1 111.6 %reduce-scatter.7.cloned.1.call-done = bf16[512,1536]{1,0:T(8,128)(2,1)} async-done(((bf16[512,6144]{1,0:T(8,128)(2,1)}), bf16[512,1536]{1,0:T(8,128)(2,1)}) %reduce-scatter.7.cloned.1.call-update) | async-done | bytes 1572880 | tf_op jit(solution)/shard_map/reduce_scatter | solution.py:183
  187.7 2.7 fusion.7
  190.4 1.9 copy-done.3
  192.5 2.5 collective-permute-done.2
  195.1 1.8 convert_add_fusion.1
  196.9 1.5 collective-permute-start.3
  198.5 11.8 %collective-permute-done.3 = bf16[160,1536]{1,0:T(8,128)(2,1)S(1)} collective-permute-done((bf16[160,1536]{1,0:T(8,128)(2,1)S(1)}, bf16[160,1536]{1,0:T(8,128)(2,1)S(1)}, u32[]{:S(2)}, u32[]{:S(2)}) %collective-permute-start.3) | collective-permute-done | bytes 491552 | tf_op jit(solution)/shard_map/ppermute | solution.py:101
  210.5 1.5 collective-permute-start.4
  212.0 10.9 %collective-permute-done.4 = bf16[160,1536]{1,0:T(8,128)(2,1)S(1)} collective-permute-done((bf16[160,1536]{1,0:T(8,128)(2,1)S(1)}, bf16[160,1536]{1,0:T(8,128)(2,1)S(1)}, u32[]{:S(2)}, u32[]{:S(2)}) %collective-permute-start.4) | collective-permute-done | bytes 491552 | tf_op jit(solution)/shard_map/ppermute | solution.py:101
  223.4 2.2 collective-permute-done.5
  227.8 8.3 %convolution_convert_fusion.1 = bf16[640,2048]{1,0:T(8,128)(2,1)} fusion(bf16[1536,2048]{1,0:T(8,128)(2,1)} %param.20, bf16[640,1536]{1,0:T(8,128)(2,1)S(1)} %constant_dynamic-update-slice_fusion.4, f32[1536]{0:T(1024)S(1)} %convert_element_type.89), kind=kOutput, calls=%fused_computation.6 | convolution fusion | flops 4030791680 | bytes 10885120 | tf_op jit(solution)/shard_map/dot_general | solution.py:203
  236.2 8.3 %convolution_convert_fusion.2 = bf16[640,2048]{1,0:T(8,128)(2,1)} fusion(bf16[1536,2048]{1,0:T(8,128)(2,1)} %param.19, bf16[640,1536]{1,0:T(8,128)(2,1)S(1)} %constant_dynamic-update-slice_fusion.4, f32[1536]{0:T(1024)S(1)} %convert_element_type.89), kind=kOutput, calls=%fused_computation.7 | convolution fusion | flops 4030791680 | bytes 10885120 | tf_op jit(solution)/shard_map/dot_general | solution.py:202
  245.1 2.9 reduce-scatter.13.cloned.1.call-done
  248.0 0.9 copy.15
  248.9 51.8 %reduce-scatter.11.cloned.1.call-done = bf16[160,2048]{1,0:T(8,128)(2,1)} async-done(((bf16[640,2048]{1,0:T(8,128)(2,1)}), bf16[160,2048]{1,0:T(8,128)(2,1)}) %reduce-scatter.11.cloned.1.call-update) | async-done | bytes 655376 | tf_op jit(solution)/shard_map/reduce_scatter | solution.py:211
  300.8 54.0 %reduce-scatter.9.cloned.1.call-done = bf16[160,2048]{1,0:T(8,128)(2,1)} async-done(((bf16[640,2048]{1,0:T(8,128)(2,1)}), bf16[160,2048]{1,0:T(8,128)(2,1)}) %reduce-scatter.9.cloned.1.call-update) | async-done | bytes 655376 | tf_op jit(solution)/shard_map/reduce_scatter | solution.py:211
  354.8 2.7 multiply_convert_fusion
  357.5 54.4 %all-gather.2.cloned.1.call-done = bf16[640,2048]{1,0:T(8,128)(2,1)} async-done(((bf16[160,2048]{1,0:T(8,128)(2,1)}), bf16[640,2048]{1,0:T(8,128)(2,1)}) %all-gather.2.cloned.1.call-update) | async-done | bytes 2621456 | tf_op jit(solution)/shard_map/all_gather | solution.py:222
  411.9 7.1 %fusion.18 = f32[640,1536]{1,0:T(8,128)S(1)} fusion(bf16[640,2048]{1,0:T(8,128)(2,1)} %all-gather.2.cloned.1.call-done, bf16[2048,1536]{1,0:T(8,128)(2,1)} %param.21), kind=kOutput, calls=%fused_computation.57 | convolution fusion | flops 4026531840 | bytes 12845056 | tf_op jit(solution)/shard_map/dot_general | solution.py:223
  419.2 2.6 collective-permute-done.6
  422.1 1.5 collective-permute-start.7
  423.6 11.8 %collective-permute-done.7 = bf16[160,1536]{1,0:T(8,128)(2,1)S(1)} collective-permute-done((bf16[160,1536]{1,0:T(8,128)(2,1)S(1)}, bf16[160,1536]{1,0:T(8,128)(2,1)S(1)}, u32[]{:S(2)}, u32[]{:S(2)}) %collective-permute-start.7) | collective-permute-done | bytes 491552 | tf_op jit(solution)/shard_map/ppermute | solution.py:101
  435.6 1.5 collective-permute-start.8
  437.2 10.9 %collective-permute-done.8 = bf16[160,1536]{1,0:T(8,128)(2,1)S(1)} collective-permute-done((bf16[160,1536]{1,0:T(8,128)(2,1)S(1)}, bf16[160,1536]{1,0:T(8,128)(2,1)S(1)}, u32[]{:S(2)}, u32[]{:S(2)}) %collective-permute-start.8) | collective-permute-done | bytes 491552 | tf_op jit(solution)/shard_map/ppermute | solution.py:101
  448.5 2.3 collective-permute-done.9
  450.9 2.6 fusion.2
  (74 shorter events, 6.7 us)
Async XLA Ops:
  6.5 219.6 %copy-start = (bf16[1536,8]{0,1:T(8,128)(2,1)S(1)}, bf16[1536,8]{0,1:T(8,128)(2,1)}, u32[]{:S(2)}) copy-start(bf16[1536,8]{0,1:T(8,128)(2,1)} %param.18) | copy-start | bytes 73732
  6.5 181.2 %reduce-scatter.7.cloned.1.call-start = ((), (), s32[]{:S(2)}) async-start(), calls=%async_computation.4 | async-start | bytes 7864320 | tf_op jit(solution)/shard_map/reduce_scatter | solution.py:183
  7.8 2.1 collective-permute-start
  9.9 26.4 %collective-permute-start.1 = (bf16[1024,512]{1,0:T(8,128)(2,1)S(1)}, bf16[1024,512]{1,0:T(8,128)(2,1)S(1)}, u32[]{:S(2)}, u32[]{:S(2)}) collective-permute-start(bf16[1024,512]{1,0:T(8,128)(2,1)S(1)} %constant_dynamic-update-slice_fusion.10), channel_id=1, source_target_pairs={{0,2},{1,3},{2,0},{3,1},{4,6},{5,7},{6,4},{7,5},{8,10},{9,11},{10,... | collective-permute-start | bytes 3145736 | tf_op jit(solution)/shard_map/ppermute | solution.py:101
  13.0 23.4 %copy-start.2 = (bf16[512,1536]{1,0:T(8,128)(2,1)S(1)}, bf16[512,1536]{1,0:T(8,128)(2,1)}, u32[]{:S(2)}) copy-start(bf16[512,1536]{1,0:T(8,128)(2,1)} %q_ref.1) | copy-start | bytes 4718596
  75.2 0.7 copy-start.4
  75.2 0.7 copy-start.5
  75.3 112.5 %copy-start.7 = (bf16[512,1536]{1,0:T(8,128)(2,1)S(1)}, bf16[512,1536]{1,0:T(8,128)(2,1)}, u32[]{:S(2)}) copy-start(bf16[512,1536]{1,0:T(8,128)(2,1)} %param.15) | copy-start | bytes 4718596
  75.3 172.7 %reduce-scatter.13.cloned.1.call-start = ((), (), s32[]{:S(2)}) async-start(), calls=%async_computation.8 | async-start | bytes 204800
  190.4 1.9 copy-start.3
  192.4 2.6 collective-permute-start.2
  196.9 13.3 %collective-permute-start.3 = (bf16[160,1536]{1,0:T(8,128)(2,1)S(1)}, bf16[160,1536]{1,0:T(8,128)(2,1)S(1)}, u32[]{:S(2)}, u32[]{:S(2)}) collective-permute-start(bf16[160,1536]{1,0:T(8,128)(2,1)S(1)} %dynamic-slice_convert_fusion.3), channel_id=1, source_target_pairs={{0,2},{1,3},{2,0},{3,1},{4,6},{5,7},{6,4},{7,5},{8,10},{9,11},{10,... | collective-permute-start | bytes 1474568 | tf_op jit(solution)/shard_map/ppermute | solution.py:101
  210.3 12.7 %copy-start.6 = (bf16[1536]{0:T(1024)(128)(2,1)S(1)}, bf16[1536]{0:T(1024)(128)(2,1)}, u32[]{:S(2)}) copy-start(bf16[1536]{0:T(1024)(128)(2,1)} %param.17) | copy-start | bytes 9220
  210.5 12.5 %collective-permute-start.4 = (bf16[160,1536]{1,0:T(8,128)(2,1)S(1)}, bf16[160,1536]{1,0:T(8,128)(2,1)S(1)}, u32[]{:S(2)}, u32[]{:S(2)}) collective-permute-start(bf16[160,1536]{1,0:T(8,128)(2,1)S(1)} %get-tuple-element.12), channel_id=1, source_target_pairs={{0,2},{1,3},{2,0},{3,1},{4,6},{5,7},{6,4},{7,5},{8,10},{9,11},{10,... | collective-permute-start | bytes 1474568 | tf_op jit(solution)/shard_map/ppermute | solution.py:101
  223.0 2.6 collective-permute-start.5
  227.7 73.0 %reduce-scatter.11.cloned.1.call-start = ((), (), s32[]{:S(2)}) async-start(), calls=%async_computation.6 | async-start | bytes 3276800 | tf_op jit(solution)/shard_map/reduce_scatter | solution.py:211
  236.1 118.6 %reduce-scatter.9.cloned.1.call-start = ((), (), s32[]{:S(2)}) async-start(), calls=%async_computation.5 | async-start | bytes 3276800 | tf_op jit(solution)/shard_map/reduce_scatter | solution.py:211
  244.5 167.4 %all-gather.2.cloned.1.call-start = ((), (), s32[]{:S(2)}) async-start(), calls=%async_computation.7 | async-start | bytes 3276800 | tf_op jit(solution)/shard_map/all_gather | solution.py:222
  419.1 2.6 collective-permute-start.6
  422.1 13.3 %collective-permute-start.7 = (bf16[160,1536]{1,0:T(8,128)(2,1)S(1)}, bf16[160,1536]{1,0:T(8,128)(2,1)S(1)}, u32[]{:S(2)}, u32[]{:S(2)}) collective-permute-start(bf16[160,1536]{1,0:T(8,128)(2,1)S(1)} %dynamic-slice_convert_fusion.2), channel_id=1, source_target_pairs={{0,2},{1,3},{2,0},{3,1},{4,6},{5,7},{6,4},{7,5},{8,10},{9,11},{10,... | collective-permute-start | bytes 1474568 | tf_op jit(solution)/shard_map/ppermute | solution.py:101
  435.6 12.5 %collective-permute-start.8 = (bf16[160,1536]{1,0:T(8,128)(2,1)S(1)}, bf16[160,1536]{1,0:T(8,128)(2,1)S(1)}, u32[]{:S(2)}, u32[]{:S(2)}) collective-permute-start(bf16[160,1536]{1,0:T(8,128)(2,1)S(1)} %get-tuple-element.8), channel_id=1, source_target_pairs={{0,2},{1,3},{2,0},{3,1},{4,6},{5,7},{6,4},{7,5},{8,10},{9,11},{10,... | collective-permute-start | bytes 1474568 | tf_op jit(solution)/shard_map/ppermute | solution.py:101
  448.1 2.6 collective-permute-start.9
  448.4 2.5 copy-start.8
  448.4 2.5 copy-start.9
  450.9 2.6 copy-start.1
Sparse Core Ops, SparseCore 0:
  75.4 112.2 reduce-scatter.6
  227.9 20.0 reduce-scatter.12
  250.3 50.4 reduce-scatter.10
  302.9 51.7 reduce-scatter.8
  357.6 54.2 all-gather.1

commit v5 on v4

--- a/solution.py
+++ b/solution.py
@@ -177,53 +177,75 @@
         value_head_rows, first_shared * HEAD_SIZE, shared_heads * HEAD_SIZE, 1
     )
     packed_kv = gather_rows(jnp.concatenate([key_used, value_used], axis=1), "ctx")
-    offset = jnp.reshape(ctx_index * rows_local, (1,)).astype(jnp.int32)
-    attended = attend(queries, packed_kv, offset, shared_heads, per_shared)
-    partial_out = jnp.dot(attended, out_weight, preferred_element_type=jnp.float32)
-    head_sum = lax.psum_scatter(
-        partial_out.astype(jnp.bfloat16), "wide", scatter_dimension=1, tiled=True
-    ).astype(jnp.float32)
-    resid = (residual.astype(jnp.float32) + head_sum).astype(jnp.bfloat16)
+    halves = 2 if rows_local % 256 == 0 else 1
+    half_rows = rows_local // halves
+    resid_parts = []
+    for half in range(halves):
+        offset = jnp.reshape(ctx_index * rows_local + half * half_rows, (1,)).astype(jnp.int32)
+        query_part = lax.slice_in_dim(queries, half * half_rows, (half + 1) * half_rows, axis=0)
+        attended = attend(query_part, packed_kv, offset, shared_heads, per_shared)
+        partial_out = jnp.dot(attended, out_weight, preferred_element_type=jnp.float32)
+        head_sum = lax.psum_scatter(
+            partial_out.astype(jnp.bfloat16), "wide", scatter_dimension=1, tiled=True
+        ).astype(jnp.float32)
+        residual_part = lax.slice_in_dim(residual, half * half_rows, (half + 1) * half_rows, axis=0)
+        resid_parts.append((residual_part.astype(jnp.float32) + head_sum).astype(jnp.bfloat16))
+    resid = jnp.concatenate(resid_parts, axis=0)
     seq_len = rows_local * ctx_count
     capacity = seq_len * 5 // 16
     width_local = resid.shape[1]
     wide_count = lax.axis_size("wide")
-    chunk = capacity // wide_count
+    pieces = 2 if capacity % (16 * max(wide_count, ctx_count)) == 0 else 1
+    piece_slots = capacity // pieces
+    chunk = piece_slots // wide_count
     slot_of_token = token_slots(expert_ids, slot_ids, capacity)
     partner = jnp.sum(expert_ids, axis=1)
     slot_local = lax.dynamic_slice_in_dim(slot_of_token, ctx_index * rows_local, rows_local)
-    slot_ids_all = jnp.arange(capacity, dtype=jnp.int32)
-    place = (slot_ids_all[:, None] == slot_local[None, :]).astype(jnp.bfloat16)
-    own_rows = jnp.dot(place, resid, preferred_element_type=jnp.float32)
-    buffer = sum_rows(own_rows, "ctx")
-    buffer_wide = buffer.astype(jnp.float32)
-    square_part = jnp.sum(buffer_wide * buffer_wide, axis=1)
-    scaled = (buffer_wide * norm_gain.astype(jnp.float32)[None, :]).astype(jnp.bfloat16)
-    gate_part = jnp.dot(scaled, gate_weight, preferred_element_type=jnp.float32)
-    up_part = jnp.dot(scaled, up_weight, preferred_element_type=jnp.float32)
-    logit_part = jnp.dot(scaled, router_weight, preferred_element_type=jnp.float32)
-    experts = logit_part.shape[1]
-    pad = 128 - (experts + 1) % 128
-    small = jnp.concatenate(
-        [logit_part, square_part[:, None], jnp.zeros((capacity, pad), jnp.float32)], axis=1
-    )
-    gate_sum, up_sum, small_sum = (
-        lax.psum_scatter(part.astype(jnp.bfloat16), "wide", scatter_dimension=0, tiled=True)
-        .astype(jnp.float32)
-        for part in (gate_part, up_part, small)
-    )
-    logit_sum = small_sum[:, :experts]
-    square_sum = small_sum[:, experts]
-    chunk_slots = wide_index * chunk + jnp.arange(chunk, dtype=jnp.int32)
-    other_chunk = jnp.sum(
-        jnp.where(chunk_slots[:, None] == slot_of_token[None, :], partner[None, :], 0), axis=1
-    )
-    hidden_chunk = expert_hidden(gate_sum, up_sum, square_sum, logit_sum, other_chunk, D)
-    hidden = lax.all_gather(hidden_chunk, "wide", axis=0, tiled=True)
-    expert_part = jnp.dot(hidden, down_weight, preferred_element_type=jnp.float32)
-    expert_sum = sum_rows(expert_part, "ctx")
-    pick = (slot_local[:, None] == slot_ids_all[None, :]).astype(jnp.bfloat16)
-    moe_rows = jnp.dot(pick, expert_sum, preferred_element_type=jnp.float32)
+    gain = norm_gain.astype(jnp.float32)[None, :]
+    moe_rows = jnp.zeros((rows_local, width_local), jnp.float32)
+    after_sums = None
+    after_down = None
+    for piece in range(pieces):
+        slot_ids_piece = piece * piece_slots + jnp.arange(piece_slots, dtype=jnp.int32)
+        place = (slot_ids_piece[:, None] == slot_local[None, :]).astype(jnp.bfloat16)
+        own_rows = jnp.dot(place, resid, preferred_element_type=jnp.float32)
+        if after_sums is not None:
+            own_rows, _ = lax.optimization_barrier((own_rows, after_sums))
+        buffer = sum_rows(own_rows, "ctx")
+        buffer_wide = buffer.astype(jnp.float32)
+        square_part = jnp.sum(buffer_wide * buffer_wide, axis=1)
+        scaled = (buffer_wide * gain).astype(jnp.bfloat16)
+        gate_part = jnp.dot(scaled, gate_weight, preferred_element_type=jnp.float32)
+        up_part = jnp.dot(scaled, up_weight, preferred_element_type=jnp.float32)
+        logit_part = jnp.dot(scaled, router_weight, preferred_element_type=jnp.float32)
+        experts = logit_part.shape[1]
+        pad = 128 - (experts + 1) % 128
+        small = jnp.concatenate(
+            [logit_part, square_part[:, None], jnp.zeros((piece_slots, pad), jnp.float32)],
+            axis=1,
+        )
+        sent = tuple(part.astype(jnp.bfloat16) for part in (gate_part, up_part, small))
+        after_sums = sent
+        gate_sum, up_sum, small_sum = (
+            lax.psum_scatter(part, "wide", scatter_dimension=0, tiled=True).astype(jnp.float32)
+            for part in sent
+        )
+        logit_sum = small_sum[:, :experts]
+        square_sum = small_sum[:, experts]
+        chunk_slots = piece * piece_slots + wide_index * chunk + jnp.arange(chunk, dtype=jnp.int32)
+        other_chunk = jnp.sum(
+            jnp.where(chunk_slots[:, None] == slot_of_token[None, :], partner[None, :], 0),
+            axis=1,
+        )
+        hidden_chunk = expert_hidden(gate_sum, up_sum, square_sum, logit_sum, other_chunk, D)
+        if after_down is not None:
+            hidden_chunk, _ = lax.optimization_barrier((hidden_chunk, after_down))
+        hidden = lax.all_gather(hidden_chunk, "wide", axis=0, tiled=True)
+        expert_part = jnp.dot(hidden, down_weight, preferred_element_type=jnp.float32)
+        after_down = expert_part
+        expert_sum = sum_rows(expert_part, "ctx")
+        pick = (slot_local[:, None] == slot_ids_piece[None, :]).astype(jnp.bfloat16)
+        moe_rows = moe_rows + jnp.dot(pick, expert_sum, preferred_element_type=jnp.float32)
     return (resid.astype(jnp.float32) + moe_rows).astype(jnp.bfloat16)
 
 

time: 460 us -> 506 us (1.10); the launches traced: 460 us -> 498 us
  matrix products: 45.1 us -> 68.8 us
  waiting for transfers between devices: 355 us -> 347 us
  local copies, waits for them, and re-layouts: 6.98 us -> 14.5 us
  starting transfers between devices: 10.4 us -> 17.3 us
  other arithmetic: 6 us -> 12.1 us
    unnamed x6 -> x12, waiting for transfers between devices: 2.96 us -> 17.9 us
    reduce_scatter x1 -> x2, waiting for transfers between devices: 112 us -> 98.8 us  [local(): lax.psum_scatter(partial_out.astype(jnp.bfloat16), 'wide', scatter_dimens...]
    reduce_scatter x2 -> x4, waiting for transfers between devices: 106 us -> 95.1 us  [local(): lax.psum_scatter(part, 'wide', scatter_dimension=0, tiled=True)]
    dot_general x1 -> x2, matrix products: 15.5 us -> 25.7 us  [local(): jnp.dot(attended, out_weight, preferred_element_type=jnp.float32)]
    all_gather x1 -> x2, waiting for transfers between devices: 54.4 us -> 61.1 us  [local(): hidden = lax.all_gather(hidden_chunk, 'wide', axis=0, tiled=True)]
    ppermute x10 -> x18, starting transfers between devices: 9.87 us -> 16.3 us  [pair_exchange(): return lax.ppermute(x, axis, perm=[(i, i ^ bit) for i in range(count)])]
    ppermute x10 -> x18, waiting for transfers between devices: 79.8 us -> 74.3 us  [pair_exchange(): return lax.ppermute(x, axis, perm=[(i, i ^ bit) for i in range(count)])]
    dot_general x1 -> x2, matrix products: 7.12 us -> 12.2 us  [local(): jnp.dot(hidden, down_weight, preferred_element_type=jnp.float32)]
  transfers between devices with their start and end apart: 15 -> 28, of which waited for: 15 -> 24; matrix products, arithmetic and copies ran while one was open for 4% -> 12% of each run, Pallas kernels for 0% -> 2%
where the time goes in v5:
time: 506 us; the launch traced here: 498 us
  waiting for transfers between devices  347 us (69%)
  matrix products  68.8 us (14%)
  Pallas kernels  23.7 us (5%)
  starting transfers between devices  17.3 us (3%)
  between operations  14.6 us (3%)
  local copies, waits for them, and re-layouts  14.5 us (3%)
  other arithmetic  12.1 us (2%)
    reduce_scatter x2, waiting for transfers between devices, local(): lax.psum_scatter(partial_out.astype(jnp.bfloat16), 'wide', scatter_dimens...  98.8 us
    reduce_scatter x4, waiting for transfers between devices, local(): lax.psum_scatter(part, 'wide', scatter_dimension=0, tiled=True)  95.1 us
    ppermute x18, waiting for transfers between devices, pair_exchange(): return lax.ppermute(x, axis, perm=[(i, i ^ bit) for i in range(count)])  74.3 us
    all_gather x2, waiting for transfers between devices, local(): hidden = lax.all_gather(hidden_chunk, 'wide', axis=0, tiled=True)  61.1 us
    dot_general x2, matrix products, local(): jnp.dot(attended, out_weight, preferred_element_type=jnp.float32)  25.7 us
    pallas_call x2, Pallas kernels, attend(): pl.pallas_call(kernel, grid_spec=grid_spec, out_shape=jax.ShapeDtypeStruc...  23.7 us
    unnamed x12, waiting for transfers between devices  17.9 us
    ppermute x18, starting transfers between devices, pair_exchange(): return lax.ppermute(x, axis, perm=[(i, i ^ bit) for i in range(count)])  16.3 us
  transfers between devices with their start and end apart: 28, of which 24 were waited for; matrix products, arithmetic and copies ran while one was open for 12% of the time, Pallas kernels for 2%

profile of v5, /device:TPU:0, one launch (start us, length us, event | category | flops | bytes accessed | tf_op | source)
XLA Modules:
  0.0 498.2 jit_solution(12448615321211739711)
XLA Ops:
  12.4 2.8 collective-permute-start.1
  16.8 22.2 %collective-permute-done.1 = bf16[1024,512]{1,0:T(8,128)(2,1)} collective-permute-done((bf16[1024,512]{1,0:T(8,128)(2,1)}, bf16[1024,512]{1,0:T(8,128)(2,1)}, u32[]{:S(2)}, u32[]{:S(2)}) %collective-permute-start.1) | collective-permute-done | bytes 1048608 | tf_op jit(solution)/shard_map/ppermute | solution.py:101
  40.3 11.9 %shard_map.119 = bf16[256,1536]{1,0:T(8,128)(2,1)S(1)} custom-call(s32[1]{0:T(128)} %bitcast.1.offset_ref, bf16[256,1536]{1,0:T(8,128)(2,1)S(1)} %get-tuple-element.28.q_ref, bf16[2048,512]{1,0:T(8,128)(2,1)S(1)} %constant_dynamic-update-slice_fusion.16.k_ref.v_ref, bf16[2048,512]{1,0:T(8,128)(2,1)S(1)} %constant_dynamic-update-slice_fusion.16.k_ref.v_ref), custom_call_target="tpu_custom_call" | custom-call | tf_op jit(solution)/shard_map/pallas_call | solution.py:91
  52.2 12.8 %convolution_convert_fusion = bf16[256,6144]{1,0:T(8,128)(2,1)} fusion(bf16[256,1536]{1,0:T(8,128)(2,1)S(1)} %shard_map.119, bf16[1536,6144]{1,0:T(8,128)(2,1)} %param.16), kind=kOutput, calls=%fused_computation | convolution fusion | flops 4833411072 | bytes 22806528 | tf_op jit(solution)/shard_map/dot_general | solution.py:187
  65.2 11.9 %shard_map.118 = bf16[256,1536]{1,0:T(8,128)(2,1)S(1)} custom-call(s32[1]{0:T(128)} %bitcast.offset_ref, bf16[256,1536]{1,0:T(8,128)(2,1)S(1)} %get-tuple-element.27.q_ref, bf16[2048,512]{1,0:T(8,128)(2,1)S(1)} %constant_dynamic-update-slice_fusion.16.k_ref.v_ref, bf16[2048,512]{1,0:T(8,128)(2,1)S(1)} %constant_dynamic-update-slice_fusion.16.k_ref.v_ref), custom_call_target="tpu_custom_call" | custom-call | tf_op jit(solution)/shard_map/pallas_call | solution.py:91
  77.1 12.9 %convolution_convert_fusion.1 = bf16[256,6144]{1,0:T(8,128)(2,1)} fusion(bf16[256,1536]{1,0:T(8,128)(2,1)S(1)} %shard_map.118, bf16[1536,6144]{1,0:T(8,128)(2,1)} %param.16), kind=kOutput, calls=%fused_computation.1 | convolution fusion | flops 4833411072 | bytes 22806528 | tf_op jit(solution)/shard_map/dot_general | solution.py:187
  90.9 36.2 %reduce-scatter.15.cloned.1.call-done = bf16[256,1536]{1,0:T(8,128)(2,1)} async-done(((bf16[256,6144]{1,0:T(8,128)(2,1)}), bf16[256,1536]{1,0:T(8,128)(2,1)}) %reduce-scatter.15.cloned.1.call-update) | async-done | bytes 786448 | tf_op jit(solution)/shard_map/reduce_scatter | solution.py:188
  127.1 62.6 %reduce-scatter.13.cloned.1.call-done = bf16[256,1536]{1,0:T(8,128)(2,1)} async-done(((bf16[256,6144]{1,0:T(8,128)(2,1)}), bf16[256,1536]{1,0:T(8,128)(2,1)}) %reduce-scatter.13.cloned.1.call-update) | async-done | bytes 786448 | tf_op jit(solution)/shard_map/reduce_scatter | solution.py:188
  198.1 6.5 %collective-permute-done.3 = bf16[80,1536]{1,0:T(8,128)(2,1)S(1)} collective-permute-done((bf16[80,1536]{1,0:T(8,128)(2,1)S(1)}, bf16[80,1536]{1,0:T(8,128)(2,1)S(1)}, u32[]{:S(2)}, u32[]{:S(2)}) %collective-permute-start.3) | collective-permute-done | bytes 245792 | tf_op jit(solution)/shard_map/ppermute | solution.py:101
  207.3 5.7 %collective-permute-done.4 = bf16[80,1536]{1,0:T(8,128)(2,1)S(1)} collective-permute-done((bf16[80,1536]{1,0:T(8,128)(2,1)S(1)}, bf16[80,1536]{1,0:T(8,128)(2,1)S(1)}, u32[]{:S(2)}, u32[]{:S(2)}) %collective-permute-start.4) | collective-permute-done | bytes 245792 | tf_op jit(solution)/shard_map/ppermute | solution.py:101
  216.9 6.1 %convolution_convert_fusion.5 = bf16[320,2048]{1,0:T(8,128)(2,1)} fusion(bf16[1536,2048]{1,0:T(8,128)(2,1)} %param.19, bf16[320,1536]{1,0:T(8,128)(2,1)S(1)} %constant_dynamic-update-slice_fusion.12, f32[1536]{0:T(1024)S(1)} %convert_element_type.162), kind=kOutput, calls=%fused_computation.8 | convolution fusion | flops 2015395840 | bytes 8591360 | tf_op jit(solution)/shard_map/dot_general | solution.py:218
  223.0 2.0 fusion.15
  225.0 6.1 %convolution_convert_fusion.4 = bf16[320,2048]{1,0:T(8,128)(2,1)} fusion(bf16[1536,2048]{1,0:T(8,128)(2,1)} %param.20, bf16[320,1536]{1,0:T(8,128)(2,1)S(1)} %constant_dynamic-update-slice_fusion.12, f32[1536]{0:T(1024)S(1)} %convert_element_type.162), kind=kOutput, calls=%fused_computation.7 | convolution fusion | flops 2015395840 | bytes 8591360 | tf_op jit(solution)/shard_map/dot_general | solution.py:219
  237.2 6.5 %collective-permute-done.11 = bf16[80,1536]{1,0:T(8,128)(2,1)S(1)} collective-permute-done((bf16[80,1536]{1,0:T(8,128)(2,1)S(1)}, bf16[80,1536]{1,0:T(8,128)(2,1)S(1)}, u32[]{:S(2)}, u32[]{:S(2)}) %collective-permute-start.11) | collective-permute-done | bytes 245792 | tf_op jit(solution)/shard_map/ppermute | solution.py:101
  245.3 5.7 %collective-permute-done.12 = bf16[80,1536]{1,0:T(8,128)(2,1)S(1)} collective-permute-done((bf16[80,1536]{1,0:T(8,128)(2,1)S(1)}, bf16[80,1536]{1,0:T(8,128)(2,1)S(1)}, u32[]{:S(2)}, u32[]{:S(2)}) %collective-permute-start.12) | collective-permute-done | bytes 245792 | tf_op jit(solution)/shard_map/ppermute | solution.py:101
  254.6 6.1 %convolution_convert_fusion.3 = bf16[320,2048]{1,0:T(8,128)(2,1)} fusion(bf16[1536,2048]{1,0:T(8,128)(2,1)} %param.19, bf16[320,1536]{1,0:T(8,128)(2,1)S(1)} %constant_dynamic-update-slice_fusion.3, f32[1536]{0:T(1024)S(1)} %convert_element_type.162), kind=kOutput, calls=%fused_computation.6 | convolution fusion | flops 2015395840 | bytes 8591360 | tf_op jit(solution)/shard_map/dot_general | solution.py:218
  260.8 6.1 %convolution_convert_fusion.2 = bf16[320,2048]{1,0:T(8,128)(2,1)} fusion(bf16[1536,2048]{1,0:T(8,128)(2,1)} %param.20, bf16[320,1536]{1,0:T(8,128)(2,1)S(1)} %constant_dynamic-update-slice_fusion.3, f32[1536]{0:T(1024)S(1)} %convert_element_type.162), kind=kOutput, calls=%fused_computation.5 | convolution fusion | flops 2015395840 | bytes 8591360 | tf_op jit(solution)/shard_map/dot_general | solution.py:219
  268.2 31.8 %reduce-scatter.19.cloned.1.call-done = bf16[80,2048]{1,0:T(8,128)(2,1)} async-done(((bf16[320,2048]{1,0:T(8,128)(2,1)}), bf16[80,2048]{1,0:T(8,128)(2,1)}) %reduce-scatter.19.cloned.1.call-update) | async-done | bytes 327696 | tf_op jit(solution)/shard_map/reduce_scatter | solution.py:230
  300.0 2.1 multiply_convert_fusion.1
  302.4 17.7 %reduce-scatter.27.cloned.1.call-done = bf16[80,128]{1,0:T(8,128)(2,1)} async-done(((bf16[320,128]{1,0:T(8,128)(2,1)}), bf16[80,128]{1,0:T(8,128)(2,1)}) %reduce-scatter.27.cloned.1.call-update) | async-done | bytes 20496
  321.0 31.0 %reduce-scatter.21.cloned.1.call-done = bf16[80,2048]{1,0:T(8,128)(2,1)} async-done(((bf16[320,2048]{1,0:T(8,128)(2,1)}), bf16[80,2048]{1,0:T(8,128)(2,1)}) %reduce-scatter.21.cloned.1.call-update) | async-done | bytes 327696 | tf_op jit(solution)/shard_map/reduce_scatter | solution.py:230
  352.0 32.4 %reduce-scatter.23.cloned.1.call-done = bf16[80,2048]{1,0:T(8,128)(2,1)} async-done(((bf16[320,2048]{1,0:T(8,128)(2,1)}), bf16[80,2048]{1,0:T(8,128)(2,1)}) %reduce-scatter.23.cloned.1.call-update) | async-done | bytes 327696 | tf_op jit(solution)/shard_map/reduce_scatter | solution.py:230
  384.4 2.1 multiply_convert_fusion
  386.5 30.7 %all-gather.3.cloned.1.call-done = bf16[320,2048]{1,0:T(8,128)(2,1)} async-done(((bf16[80,2048]{1,0:T(8,128)(2,1)}), bf16[320,2048]{1,0:T(8,128)(2,1)}) %all-gather.3.cloned.1.call-update) | async-done | bytes 1310736 | tf_op jit(solution)/shard_map/all_gather | solution.py:243
  417.2 6.7 %fusion.38 = f32[320,1536]{1,0:T(8,128)} fusion(bf16[320,2048]{1,0:T(8,128)(2,1)} %all-gather.3.cloned.1.call-done, bf16[2048,1536]{1,0:T(8,128)(2,1)} %param.21), kind=kOutput, calls=%fused_computation.112 | convolution fusion | flops 2013265920 | bytes 9568256 | tf_op jit(solution)/shard_map/dot_general | solution.py:244
  425.2 30.4 %all-gather.5.cloned.1.call-done = bf16[320,2048]{1,0:T(8,128)(2,1)} async-done(((bf16[80,2048]{1,0:T(8,128)(2,1)}), bf16[320,2048]{1,0:T(8,128)(2,1)}) %all-gather.5.cloned.1.call-update) | async-done | bytes 1310736 | tf_op jit(solution)/shard_map/all_gather | solution.py:243
  455.7 5.5 %fusion.39 = f32[320,1536]{1,0:T(8,128)S(1)} fusion(bf16[320,2048]{1,0:T(8,128)(2,1)} %all-gather.5.cloned.1.call-done, bf16[2048,1536]{1,0:T(8,128)(2,1)} %param.21), kind=kOutput, calls=%fused_computation.113 | convolution fusion | flops 2013265920 | bytes 9568256 | tf_op jit(solution)/shard_map/dot_general | solution.py:244
  464.9 5.5 %collective-permute-done.7 = bf16[80,1536]{1,0:T(8,128)(2,1)S(1)} collective-permute-done((bf16[80,1536]{1,0:T(8,128)(2,1)S(1)}, bf16[80,1536]{1,0:T(8,128)(2,1)S(1)}, u32[]{:S(2)}, u32[]{:S(2)}) %collective-permute-start.7) | collective-permute-done | bytes 245792 | tf_op jit(solution)/shard_map/ppermute | solution.py:101
  472.0 3.6 collective-permute-done.15
  477.3 3.6 collective-permute-done.8
  481.0 4.7 collective-permute-done.16
  488.7 2.2 fusion.1
  (145 shorter events, 49.6 us)
Async XLA Ops:
  6.5 208.8 %copy-start = (bf16[1536,8]{0,1:T(8,128)(2,1)S(1)}, bf16[1536,8]{0,1:T(8,128)(2,1)}, u32[]{:S(2)}) copy-start(bf16[1536,8]{0,1:T(8,128)(2,1)} %param.18) | copy-start | bytes 73732
  6.5 120.5 %reduce-scatter.15.cloned.1.call-start = ((), (), s32[]{:S(2)}) async-start(), calls=%async_computation.9 | async-start | bytes 3932160 | tf_op jit(solution)/shard_map/reduce_scatter | solution.py:188
  7.6 7.6 %copy-start.4 = (bf16[512,1536]{1,0:T(8,128)(2,1)S(1)}, bf16[512,1536]{1,0:T(8,128)(2,1)}, u32[]{:S(2)}) copy-start(bf16[512,1536]{1,0:T(8,128)(2,1)} %param.12) | copy-start | bytes 4718596
  9.5 2.0 collective-permute-start
  12.4 26.6 %collective-permute-start.1 = (bf16[1024,512]{1,0:T(8,128)(2,1)}, bf16[1024,512]{1,0:T(8,128)(2,1)}, u32[]{:S(2)}, u32[]{:S(2)}) collective-permute-start(bf16[1024,512]{1,0:T(8,128)(2,1)} %constant_dynamic-update-slice_fusion.18), channel_id=1, source_target_pairs={{0,2},{1,3},{2,0},{3,1},{4,6},{5,7},{6,4},{7,5},{8,10},{9,11},{10,... | collective-permute-start | bytes 3145736 | tf_op jit(solution)/shard_map/ppermute | solution.py:101
  65.0 124.7 %reduce-scatter.13.cloned.1.call-start = ((), (), s32[]{:S(2)}) async-start(), calls=%async_computation.8 | async-start | bytes 3932160 | tf_op jit(solution)/shard_map/reduce_scatter | solution.py:188
  90.0 99.7 %copy-start.5 = (bf16[512,1536]{1,0:T(8,128)(2,1)S(1)}, bf16[512,1536]{1,0:T(8,128)(2,1)}, u32[]{:S(2)}) copy-start(bf16[512,1536]{1,0:T(8,128)(2,1)} %param.15) | copy-start | bytes 4718596
  90.0 177.2 %reduce-scatter.25.cloned.1.call-start = ((), (), s32[]{:S(2)}) async-start(), calls=%async_computation.16 | async-start | bytes 102400
  192.4 2.1 collective-permute-start.2
  196.6 16.5 %copy-start.9 = (bf16[1536]{0:T(1024)(128)(2,1)S(1)}, bf16[1536]{0:T(1024)(128)(2,1)}, u32[]{:S(2)}) copy-start(bf16[1536]{0:T(1024)(128)(2,1)} %param.17) | copy-start | bytes 9220
  196.6 8.1 %collective-permute-start.3 = (bf16[80,1536]{1,0:T(8,128)(2,1)S(1)}, bf16[80,1536]{1,0:T(8,128)(2,1)S(1)}, u32[]{:S(2)}, u32[]{:S(2)}) collective-permute-start(bf16[80,1536]{1,0:T(8,128)(2,1)S(1)} %dynamic-slice_convert_fusion.7), channel_id=1, source_target_pairs={{0,2},{1,3},{2,0},{3,1},{4,6},{5,7},{6,4},{7,5},{8,10},{9,11},{10,... | collective-permute-start | bytes 737288 | tf_op jit(solution)/shard_map/ppermute | solution.py:101
  205.8 7.2 %collective-permute-start.4 = (bf16[80,1536]{1,0:T(8,128)(2,1)S(1)}, bf16[80,1536]{1,0:T(8,128)(2,1)S(1)}, u32[]{:S(2)}, u32[]{:S(2)}) collective-permute-start(bf16[80,1536]{1,0:T(8,128)(2,1)S(1)} %get-tuple-element.24), channel_id=1, source_target_pairs={{0,2},{1,3},{2,0},{3,1},{4,6},{5,7},{6,4},{7,5},{8,10},{9,11},{10,... | collective-permute-start | bytes 737288 | tf_op jit(solution)/shard_map/ppermute | solution.py:101
  213.0 1.9 collective-permute-start.5
  216.6 51.6 %reduce-scatter.17.cloned.1.call-start = ((), (), s32[]{:S(2)}) async-start(), calls=%async_computation.10 | async-start | bytes 1638400 | tf_op jit(solution)/shard_map/reduce_scatter | solution.py:230
  222.9 77.0 %reduce-scatter.19.cloned.1.call-start = ((), (), s32[]{:S(2)}) async-start(), calls=%async_computation.11 | async-start | bytes 1638400 | tf_op jit(solution)/shard_map/reduce_scatter | solution.py:230
  232.3 1.9 collective-permute-start.10
  232.6 87.5 %reduce-scatter.27.cloned.1.call-start = ((), (), s32[]{:S(2)}) async-start(), calls=%async_computation.17 | async-start | bytes 102400
  235.7 8.1 %collective-permute-start.11 = (bf16[80,1536]{1,0:T(8,128)(2,1)S(1)}, bf16[80,1536]{1,0:T(8,128)(2,1)S(1)}, u32[]{:S(2)}, u32[]{:S(2)}) collective-permute-start(bf16[80,1536]{1,0:T(8,128)(2,1)S(1)} %dynamic-slice_convert_fusion.5), channel_id=1, source_target_pairs={{0,2},{1,3},{2,0},{3,1},{4,6},{5,7},{6,4},{7,5},{8,10},{9,11},{10,... | collective-permute-start | bytes 737288 | tf_op jit(solution)/shard_map/ppermute | solution.py:101
  243.8 7.2 %collective-permute-start.12 = (bf16[80,1536]{1,0:T(8,128)(2,1)S(1)}, bf16[80,1536]{1,0:T(8,128)(2,1)S(1)}, u32[]{:S(2)}, u32[]{:S(2)}) collective-permute-start(bf16[80,1536]{1,0:T(8,128)(2,1)S(1)} %get-tuple-element.22), channel_id=1, source_target_pairs={{0,2},{1,3},{2,0},{3,1},{4,6},{5,7},{6,4},{7,5},{8,10},{9,11},{10,... | collective-permute-start | bytes 737288 | tf_op jit(solution)/shard_map/ppermute | solution.py:101
  251.0 1.9 collective-permute-start.13
  254.6 97.4 %reduce-scatter.21.cloned.1.call-start = ((), (), s32[]{:S(2)}) async-start(), calls=%async_computation.13 | async-start | bytes 1638400 | tf_op jit(solution)/shard_map/reduce_scatter | solution.py:230
  260.7 123.6 %reduce-scatter.23.cloned.1.call-start = ((), (), s32[]{:S(2)}) async-start(), calls=%async_computation.14 | async-start | bytes 1638400 | tf_op jit(solution)/shard_map/reduce_scatter | solution.py:230
  266.9 150.3 %all-gather.3.cloned.1.call-start = ((), (), s32[]{:S(2)}) async-start(), calls=%async_computation.12 | async-start | bytes 1638400 | tf_op jit(solution)/shard_map/all_gather | solution.py:243
  302.1 153.5 %all-gather.5.cloned.1.call-start = ((), (), s32[]{:S(2)}) async-start(), calls=%async_computation.15 | async-start | bytes 1638400 | tf_op jit(solution)/shard_map/all_gather | solution.py:243
  425.1 36.2 %collective-permute-start.6 = (bf16[160,1536]{1,0:T(8,128)(2,1)S(1)}, bf16[160,1536]{1,0:T(8,128)(2,1)S(1)}, u32[]{:S(2)}, u32[]{:S(2)}) collective-permute-start(bf16[160,1536]{1,0:T(8,128)(2,1)S(1)} %dynamic-slice_convert_fusion.2), channel_id=1, source_target_pairs={{0,1},{1,0},{2,3},{3,2},{4,5},{5,4},{6,7},{7,6},{8,9},{9,8},{10,11... | collective-permute-start | bytes 1474568 | tf_op jit(solution)/shard_map/ppermute | solution.py:101
  461.2 1.9 collective-permute-start.14
  461.5 8.9 %collective-permute-start.7 = (bf16[80,1536]{1,0:T(8,128)(2,1)S(1)}, bf16[80,1536]{1,0:T(8,128)(2,1)S(1)}, u32[]{:S(2)}, u32[]{:S(2)}) collective-permute-start(bf16[80,1536]{1,0:T(8,128)(2,1)S(1)} %dynamic-slice_convert_fusion.6), channel_id=1, source_target_pairs={{0,2},{1,3},{2,0},{3,1},{4,6},{5,7},{6,4},{7,5},{8,10},{9,11},{10,... | collective-permute-start | bytes 737288 | tf_op jit(solution)/shard_map/ppermute | solution.py:101
  463.3 12.3 %collective-permute-start.15 = (bf16[80,1536]{1,0:T(8,128)(2,1)S(1)}, bf16[80,1536]{1,0:T(8,128)(2,1)S(1)}, u32[]{:S(2)}, u32[]{:S(2)}) collective-permute-start(bf16[80,1536]{1,0:T(8,128)(2,1)S(1)} %dynamic-slice_convert_fusion.4), channel_id=1, source_target_pairs={{0,2},{1,3},{2,0},{3,1},{4,6},{5,7},{6,4},{7,5},{8,10},{9,11},{10,... | collective-permute-start | bytes 737288 | tf_op jit(solution)/shard_map/ppermute | solution.py:101
  470.5 10.4 %collective-permute-start.8 = (bf16[80,1536]{1,0:T(8,128)(2,1)S(1)}, bf16[80,1536]{1,0:T(8,128)(2,1)S(1)}, u32[]{:S(2)}, u32[]{:S(2)}) collective-permute-start(bf16[80,1536]{1,0:T(8,128)(2,1)S(1)} %get-tuple-element.14), channel_id=1, source_target_pairs={{0,2},{1,3},{2,0},{3,1},{4,6},{5,7},{6,4},{7,5},{8,10},{9,11},{10,... | collective-permute-start | bytes 737288 | tf_op jit(solution)/shard_map/ppermute | solution.py:101
  475.8 9.9 %collective-permute-start.16 = (bf16[80,1536]{1,0:T(8,128)(2,1)S(1)}, bf16[80,1536]{1,0:T(8,128)(2,1)S(1)}, u32[]{:S(2)}, u32[]{:S(2)}) collective-permute-start(bf16[80,1536]{1,0:T(8,128)(2,1)S(1)} %get-tuple-element.16), channel_id=1, source_target_pairs={{0,2},{1,3},{2,0},{3,1},{4,6},{5,7},{6,4},{7,5},{8,10},{9,11},{10,... | collective-permute-start | bytes 737288 | tf_op jit(solution)/shard_map/ppermute | solution.py:101
  481.0 5.0 %collective-permute-start.9 = (bf16[160,1536]{1,0:T(8,128)(2,1)S(1)}, bf16[160,1536]{1,0:T(8,128)(2,1)S(1)}, u32[]{:S(2)}, u32[]{:S(2)}) collective-permute-start(bf16[160,1536]{1,0:T(8,128)(2,1)S(1)} %constant_dynamic-update-slice_fusion.9), channel_id=1, source_target_pairs={{0,1},{1,0},{2,3},{3,2},{4,5},{5,4},{6,7},{7,6},{8,9},{9,8},{10,11... | collective-permute-start | bytes 1474568 | tf_op jit(solution)/shard_map/ppermute | solution.py:101
  485.7 1.9 collective-permute-start.17
  (6 other events, 15.4 us)
Sparse Core Ops, SparseCore 0:
  65.1 61.8 reduce-scatter.14
  129.4 60.2 reduce-scatter.12
  216.7 19.2 reduce-scatter.24
  238.1 29.5 reduce-scatter.16
  269.9 30.0 reduce-scatter.18
  302.1 18.0 reduce-scatter.26
  322.4 29.5 reduce-scatter.20
  354.3 30.0 reduce-scatter.22
  385.9 31.1 all-gather.2
  424.0 31.6 all-gather.4

commit v6 on v4

--- a/solution.py
+++ b/solution.py
@@ -116,6 +116,27 @@
         both = lax.dynamic_update_slice_in_dim(both, out, upper * size, 0)
         out = lax.dynamic_update_slice_in_dim(both, other, (1 - upper) * size, 0)
         bit *= 2
+    return out
+
+
+def gather_causal(x, axis):
+    count = lax.axis_size(axis)
+    if count != 4:
+        return gather_rows(x, axis)
+    index = lax.axis_index(axis)
+    rows = x.shape[0]
+    lower = lax.ppermute(x, axis, perm=[(0, 2), (1, 3)])
+    pair = jnp.concatenate([x, lower], axis=0)
+    other = pair_exchange(pair, axis, count, 1)
+    partner = index ^ 1
+    out = jnp.zeros((count * rows,) + x.shape[1:], x.dtype)
+    for block, at in (
+        (x, index),
+        (lower, (index + 2) % 4),
+        (other[:rows], partner),
+        (other[rows:], (partner + 2) % 4),
+    ):
+        out = lax.dynamic_update_slice_in_dim(out, block, at * rows, 0)
     return out
 
 
@@ -176,7 +197,7 @@
     value_used = lax.dynamic_slice_in_dim(
         value_head_rows, first_shared * HEAD_SIZE, shared_heads * HEAD_SIZE, 1
     )
-    packed_kv = gather_rows(jnp.concatenate([key_used, value_used], axis=1), "ctx")
+    packed_kv = gather_causal(jnp.concatenate([key_used, value_used], axis=1), "ctx")
     offset = jnp.reshape(ctx_index * rows_local, (1,)).astype(jnp.int32)
     attended = attend(queries, packed_kv, offset, shared_heads, per_shared)
     partial_out = jnp.dot(attended, out_weight, preferred_element_type=jnp.float32)
@@ -202,18 +223,26 @@
     gate_part = jnp.dot(scaled, gate_weight, preferred_element_type=jnp.float32)
     up_part = jnp.dot(scaled, up_weight, preferred_element_type=jnp.float32)
     logit_part = jnp.dot(scaled, router_weight, preferred_element_type=jnp.float32)
+    hidden_local = gate_part.shape[1]
     experts = logit_part.shape[1]
     pad = 128 - (experts + 1) % 128
-    small = jnp.concatenate(
-        [logit_part, square_part[:, None], jnp.zeros((capacity, pad), jnp.float32)], axis=1
-    )
-    gate_sum, up_sum, small_sum = (
-        lax.psum_scatter(part.astype(jnp.bfloat16), "wide", scatter_dimension=0, tiled=True)
-        .astype(jnp.float32)
-        for part in (gate_part, up_part, small)
-    )
-    logit_sum = small_sum[:, :experts]
-    square_sum = small_sum[:, experts]
+    packed = jnp.concatenate(
+        [
+            gate_part,
+            up_part,
+            logit_part,
+            square_part[:, None],
+            jnp.zeros((capacity, pad), jnp.float32),
+        ],
+        axis=1,
+    ).astype(jnp.bfloat16)
+    reduced = lax.psum_scatter(packed, "wide", scatter_dimension=0, tiled=True).astype(
+        jnp.float32
+    )
+    gate_sum = reduced[:, :hidden_local]
+    up_sum = reduced[:, hidden_local : 2 * hidden_local]
+    logit_sum = reduced[:, 2 * hidden_local : 2 * hidden_local + experts]
+    square_sum = reduced[:, 2 * hidden_local + experts]
     chunk_slots = wide_index * chunk + jnp.arange(chunk, dtype=jnp.int32)
     other_chunk = jnp.sum(
         jnp.where(chunk_slots[:, None] == slot_of_token[None, :], partner[None, :], 0), axis=1

time: 460 us -> 449 us (0.976)
  waiting for transfers between devices: 355 us -> 334 us
  local copies, waits for them, and re-layouts: 6.98 us -> 19.7 us
    reduce_scatter x2 -> x0, waiting for transfers between devices: 106 us -> none  [local(): lax.psum_scatter(part.astype(jnp.bfloat16), 'wide', scatter_dimension=0,...]
    unnamed x6 -> x4, waiting for transfers between devices: 2.96 us -> 96.6 us
    ppermute x10 -> x9, waiting for transfers between devices: 79.8 us -> 58.1 us  [pair_exchange(): return lax.ppermute(x, axis, perm=[(i, i ^ bit) for i in range(count)])]
    ppermute x0 -> x1, waiting for transfers between devices: none -> 11.1 us  [gather_causal(): lower = lax.ppermute(x, axis, perm=[(0, 2), (1, 3)])]
    concatenate x1, local copies, waits for them, and re-layouts: 0.08 us -> 8.51 us  [local(): jnp.concatenate([gate_part, up_part, logit_part, square_part[:, None], jn...]
    ppermute x0 -> x1, starting transfers between devices: none -> 4.9 us  [gather_causal(): lower = lax.ppermute(x, axis, perm=[(0, 2), (1, 3)])]
    ppermute x10 -> x9, starting transfers between devices: 9.87 us -> 6.44 us  [pair_exchange(): return lax.ppermute(x, axis, perm=[(i, i ^ bit) for i in range(count)])]
  transfers between devices with their start and end apart: 15 -> 13, of which waited for: 15 -> 13; matrix products, arithmetic and copies ran while one was open for 4% -> 0% of each run, Pallas kernels for 0% -> 0%
where the time goes in v6:
time: 449 us
  waiting for transfers between devices  334 us (74%)
  matrix products  41.6 us (9%)
  Pallas kernels  23.4 us (5%)
  local copies, waits for them, and re-layouts  19.7 us (4%)
  between operations  13.5 us (3%)
  starting transfers between devices  11.8 us (3%)
  other arithmetic  5.28 us (1%)
    reduce_scatter x1, waiting for transfers between devices, local(): lax.psum_scatter(partial_out.astype(jnp.bfloat16), 'wide', scatter_dimens...  112 us
    unnamed x4, waiting for transfers between devices  96.6 us
    ppermute x9, waiting for transfers between devices, pair_exchange(): return lax.ppermute(x, axis, perm=[(i, i ^ bit) for i in range(count)])  58.1 us
    all_gather x1, waiting for transfers between devices, local(): hidden = lax.all_gather(hidden_chunk, 'wide', axis=0, tiled=True)  55.4 us
    pallas_call x1, Pallas kernels, attend(): pl.pallas_call(kernel, grid_spec=grid_spec, out_shape=jax.ShapeDtypeStruc...  23.4 us
    dot_general x1, matrix products, local(): jnp.dot(attended, out_weight, preferred_element_type=jnp.float32)  15.5 us
    ppermute x1, waiting for transfers between devices, gather_causal(): lower = lax.ppermute(x, axis, perm=[(0, 2), (1, 3)])  11.1 us
  transfers between devices with their start and end apart: 13, of which 13 were waited for; matrix products, arithmetic and copies ran while one was open for 0% of the time, Pallas kernels for 0%

profile of v6, /device:TPU:0, one launch (start us, length us, event | category | flops | bytes accessed | tf_op | source)
XLA Modules:
  0.0 448.8 jit_solution(961931113690962303)
XLA Ops:
  6.5 1.1 constant_dynamic-slice_fusion
  7.9 4.9 %collective-permute-start = (bf16[512,512]{1,0:T(8,128)(2,1)S(1)}, bf16[512,512]{1,0:T(8,128)(2,1)S(1)}, u32[]{:S(2)}, u32[]{:S(2)}) collective-permute-start(bf16[512,512]{1,0:T(8,128)(2,1)S(1)} %get-tuple-element.13), channel_id=1, source_target_pairs={{0,2},{1,3},{4,6},{5,7},{8,10},{9,11},{12,14},{13,15},{16,18},{17,... | collective-permute-start | bytes 1572872 | tf_op jit(solution)/shard_map/ppermute | solution.py:128
  12.8 11.1 %collective-permute-done = bf16[512,512]{1,0:T(8,128)(2,1)S(1)} collective-permute-done((bf16[512,512]{1,0:T(8,128)(2,1)S(1)}, bf16[512,512]{1,0:T(8,128)(2,1)S(1)}, u32[]{:S(2)}, u32[]{:S(2)}) %collective-permute-start) | collective-permute-done | bytes 524320 | tf_op jit(solution)/shard_map/ppermute | solution.py:128
  25.0 3.0 collective-permute-done.1
  29.0 1.1 slice_dynamic-update-slice_fusion.k_ref.v_ref
  30.1 23.4 %shard_map.118 = bf16[512,1536]{1,0:T(8,128)(2,1)S(1)} custom-call(s32[1]{0:T(128)} %bitcast.offset_ref, bf16[512,1536]{1,0:T(8,128)(2,1)S(1)} %copy-done.1, bf16[2048,512]{1,0:T(8,128)(2,1)S(1)} %slice_dynamic-update-slice_fusion.k_ref.v_ref, bf16[2048,512]{1,0:T(8,128)(2,1)S(1)} %slice_dynamic-update-slice_fusion.k_ref.v_ref), custom_call_target="tpu_custom_call" | custom-call | tf_op jit(solution)/shard_map/pallas_call | solution.py:91
  53.5 15.5 %convolution_convert_fusion = bf16[512,6144]{1,0:T(8,128)(2,1)} fusion(bf16[512,1536]{1,0:T(8,128)(2,1)S(1)} %shard_map.118, bf16[1536,6144]{1,0:T(8,128)(2,1)} %param.16), kind=kOutput, calls=%fused_computation | convolution fusion | flops 9666822144 | bytes 26738688 | tf_op jit(solution)/shard_map/dot_general | solution.py:203
  69.9 112.3 %reduce-scatter.5.cloned.1.call-done = bf16[512,1536]{1,0:T(8,128)(2,1)} async-done(((bf16[512,6144]{1,0:T(8,128)(2,1)}), bf16[512,1536]{1,0:T(8,128)(2,1)}) %reduce-scatter.5.cloned.1.call-update) | async-done | bytes 1572880 | tf_op jit(solution)/shard_map/reduce_scatter | solution.py:204
  182.2 2.7 fusion.10
  184.9 1.8 copy-done.2
  187.0 2.5 collective-permute-done.2
  189.5 1.8 convert_add_fusion.1
  191.3 1.5 collective-permute-start.3
  192.9 11.8 %collective-permute-done.3 = bf16[160,1536]{1,0:T(8,128)(2,1)S(1)} collective-permute-done((bf16[160,1536]{1,0:T(8,128)(2,1)S(1)}, bf16[160,1536]{1,0:T(8,128)(2,1)S(1)}, u32[]{:S(2)}, u32[]{:S(2)}) %collective-permute-start.3) | collective-permute-done | bytes 491552 | tf_op jit(solution)/shard_map/ppermute | solution.py:101
  204.9 1.5 collective-permute-start.4
  206.4 10.9 %collective-permute-done.4 = bf16[160,1536]{1,0:T(8,128)(2,1)S(1)} collective-permute-done((bf16[160,1536]{1,0:T(8,128)(2,1)S(1)}, bf16[160,1536]{1,0:T(8,128)(2,1)S(1)}, u32[]{:S(2)}, u32[]{:S(2)}) %collective-permute-start.4) | collective-permute-done | bytes 491552 | tf_op jit(solution)/shard_map/ppermute | solution.py:101
  217.7 2.3 collective-permute-done.5
  220.6 7.5 %convolution_convert_fusion.1 = bf16[640,2048]{1,0:T(8,128)(2,1)S(1)} fusion(bf16[1536,2048]{1,0:T(8,128)(2,1)} %param.20, bf16[640,1536]{1,0:T(8,128)(2,1)S(1)} %constant_dynamic-update-slice_fusion.4, f32[1536]{0:T(1024)S(1)} %convert_element_type.77), kind=kOutput, calls=%fused_computation.6 | convolution fusion | flops 4030791680 | bytes 10885120 | tf_op jit(solution)/shard_map/dot_general | solution.py:224
  228.1 5.6 %convolution_convert_fusion.2 = bf16[640,2048]{1,0:T(8,128)(2,1)} fusion(bf16[1536,2048]{1,0:T(8,128)(2,1)S(1)} %bitcast.18, bf16[640,1536]{1,0:T(8,128)(2,1)S(1)} %constant_dynamic-update-slice_fusion.4, f32[1536]{0:T(1024)S(1)} %convert_element_type.77), kind=kOutput, calls=%fused_computation.7 | convolution fusion | flops 4030791680 | bytes 10885120 | tf_op jit(solution)/shard_map/dot_general | solution.py:223
  234.7 8.5 %concatenate.12 = bf16[640,4224]{1,0:T(8,128)(2,1)} concatenate(bf16[640,2048]{1,0:T(8,128)(2,1)} %convolution_convert_fusion.2, bf16[640,2048]{1,0:T(8,128)(2,1)S(1)} %convolution_convert_fusion.1, bf16[640,8]{1,0:T(8,128)(2,1)S(1)} %copy.22, bf16[640,1]{1,0:T(8,128)(2,1)S(1)} %broadcast_in_dim.56, bf16[640,119]{1,0:T(8,128)(2,1)S(1)} %broadcast_in_dim.52), dimensions={1} | concatenate | bytes 10813440 | tf_op jit(solution)/shard_map/concatenate | solution.py:229
  243.8 96.6 %reduce-scatter.7.cloned.1.call-done = bf16[160,4224]{1,0:T(8,128)(2,1)} async-done(((bf16[640,4224]{1,0:T(8,128)(2,1)}), bf16[160,4224]{1,0:T(8,128)(2,1)}) %reduce-scatter.7.cloned.1.call-update) | async-done | bytes 1351696
  340.4 2.6 copy.27
  344.0 1.2 copy.25
  345.2 55.4 %all-gather.2.cloned.1.call-done = bf16[640,2048]{1,0:T(8,128)(2,1)} async-done(((bf16[160,2048]{1,0:T(8,128)(2,1)}), bf16[640,2048]{1,0:T(8,128)(2,1)}) %all-gather.2.cloned.1.call-update) | async-done | bytes 2621456 | tf_op jit(solution)/shard_map/all_gather | solution.py:251
  400.7 7.1 %fusion.21 = f32[640,1536]{1,0:T(8,128)S(1)} fusion(bf16[640,2048]{1,0:T(8,128)(2,1)} %all-gather.2.cloned.1.call-done, bf16[2048,1536]{1,0:T(8,128)(2,1)} %param.21), kind=kOutput, calls=%fused_computation.61 | convolution fusion | flops 4026531840 | bytes 12845056 | tf_op jit(solution)/shard_map/dot_general | solution.py:252
  408.0 2.6 collective-permute-done.6
  410.9 1.5 collective-permute-start.7
  412.4 11.8 %collective-permute-done.7 = bf16[160,1536]{1,0:T(8,128)(2,1)S(1)} collective-permute-done((bf16[160,1536]{1,0:T(8,128)(2,1)S(1)}, bf16[160,1536]{1,0:T(8,128)(2,1)S(1)}, u32[]{:S(2)}, u32[]{:S(2)}) %collective-permute-start.7) | collective-permute-done | bytes 491552 | tf_op jit(solution)/shard_map/ppermute | solution.py:101
  424.4 1.5 collective-permute-start.8
  425.9 10.9 %collective-permute-done.8 = bf16[160,1536]{1,0:T(8,128)(2,1)S(1)} collective-permute-done((bf16[160,1536]{1,0:T(8,128)(2,1)S(1)}, bf16[160,1536]{1,0:T(8,128)(2,1)S(1)}, u32[]{:S(2)}, u32[]{:S(2)}) %collective-permute-start.8) | collective-permute-done | bytes 491552 | tf_op jit(solution)/shard_map/ppermute | solution.py:101
  437.3 2.3 collective-permute-done.9
  439.7 2.6 fusion.2
  (71 shorter events, 8.3 us)
Async XLA Ops:
  6.5 227.2 %copy-start = (bf16[1536,8]{0,1:T(8,128)(2,1)S(1)}, bf16[1536,8]{0,1:T(8,128)(2,1)}, u32[]{:S(2)}) copy-start(bf16[1536,8]{0,1:T(8,128)(2,1)} %param.18) | copy-start | bytes 73732
  6.5 175.7 %reduce-scatter.5.cloned.1.call-start = ((), (), s32[]{:S(2)}) async-start(), calls=%async_computation.2 | async-start | bytes 7864320 | tf_op jit(solution)/shard_map/reduce_scatter | solution.py:204
  7.9 16.0 %collective-permute-start = (bf16[512,512]{1,0:T(8,128)(2,1)S(1)}, bf16[512,512]{1,0:T(8,128)(2,1)S(1)}, u32[]{:S(2)}, u32[]{:S(2)}) collective-permute-start(bf16[512,512]{1,0:T(8,128)(2,1)S(1)} %get-tuple-element.13), channel_id=1, source_target_pairs={{0,2},{1,3},{4,6},{5,7},{8,10},{9,11},{12,14},{13,15},{16,18},{17,... | collective-permute-start | bytes 1572872 | tf_op jit(solution)/shard_map/ppermute | solution.py:128
  25.0 3.0 collective-permute-start.1
  25.0 5.2 %copy-start.1 = (bf16[512,1536]{1,0:T(8,128)(2,1)S(1)}, bf16[512,1536]{1,0:T(8,128)(2,1)}, u32[]{:S(2)}) copy-start(bf16[512,1536]{1,0:T(8,128)(2,1)} %q_ref.1) | copy-start | bytes 4718596
  69.0 0.7 copy-start.3
  69.0 0.7 copy-start.4
  69.0 113.2 %copy-start.6 = (bf16[512,1536]{1,0:T(8,128)(2,1)S(1)}, bf16[512,1536]{1,0:T(8,128)(2,1)}, u32[]{:S(2)}) copy-start(bf16[512,1536]{1,0:T(8,128)(2,1)} %param.15) | copy-start | bytes 4718596
  69.0 271.3 %reduce-scatter.7.cloned.1.call-start = ((), (), s32[]{:S(2)}) async-start(), calls=%async_computation.4 | async-start | bytes 6758400
  184.9 1.9 copy-start.2
  186.8 2.6 collective-permute-start.2
  191.3 13.3 %collective-permute-start.3 = (bf16[160,1536]{1,0:T(8,128)(2,1)S(1)}, bf16[160,1536]{1,0:T(8,128)(2,1)S(1)}, u32[]{:S(2)}, u32[]{:S(2)}) collective-permute-start(bf16[160,1536]{1,0:T(8,128)(2,1)S(1)} %dynamic-slice_convert_fusion.3), channel_id=1, source_target_pairs={{0,2},{1,3},{2,0},{3,1},{4,6},{5,7},{6,4},{7,5},{8,10},{9,11},{10,... | collective-permute-start | bytes 1474568 | tf_op jit(solution)/shard_map/ppermute | solution.py:101
  192.9 24.6 %copy-start.5 = (bf16[1536]{0:T(1024)(128)(2,1)S(1)}, bf16[1536]{0:T(1024)(128)(2,1)}, u32[]{:S(2)}) copy-start(bf16[1536]{0:T(1024)(128)(2,1)} %param.17) | copy-start | bytes 9220
  204.9 12.5 %collective-permute-start.4 = (bf16[160,1536]{1,0:T(8,128)(2,1)S(1)}, bf16[160,1536]{1,0:T(8,128)(2,1)S(1)}, u32[]{:S(2)}, u32[]{:S(2)}) collective-permute-start(bf16[160,1536]{1,0:T(8,128)(2,1)S(1)} %get-tuple-element.12), channel_id=1, source_target_pairs={{0,2},{1,3},{2,0},{3,1},{4,6},{5,7},{6,4},{7,5},{8,10},{9,11},{10,... | collective-permute-start | bytes 1474568 | tf_op jit(solution)/shard_map/ppermute | solution.py:101
  217.4 2.6 collective-permute-start.5
  220.1 8.0 %slice-start = ((s8[6291456]{0:T(1024)(128)(4,1)}), s8[4194304]{0:T(1024)(128)(4,1)S(1)}, s32[]{:S(2)}) async-start(s8[6291456]{0:T(1024)(128)(4,1)} %bitcast.17), calls=%async_computation.5 | async-start | bytes 8388608
  220.6 7.5 %slice-start.1 = ((s8[6291456]{0:T(1024)(128)(4,1)}), s8[2097152]{0:T(1024)(128)(4,1)S(1)}, s32[]{:S(2)}) async-start(s8[6291456]{0:T(1024)(128)(4,1)} %bitcast.17), calls=%async_computation.6 | async-start | bytes 4194304
  243.2 157.4 %all-gather.2.cloned.1.call-start = ((), (), s32[]{:S(2)}) async-start(), calls=%async_computation.3 | async-start | bytes 3276800 | tf_op jit(solution)/shard_map/all_gather | solution.py:251
  407.9 2.6 collective-permute-start.6
  410.9 13.3 %collective-permute-start.7 = (bf16[160,1536]{1,0:T(8,128)(2,1)S(1)}, bf16[160,1536]{1,0:T(8,128)(2,1)S(1)}, u32[]{:S(2)}, u32[]{:S(2)}) collective-permute-start(bf16[160,1536]{1,0:T(8,128)(2,1)S(1)} %dynamic-slice_convert_fusion.2), channel_id=1, source_target_pairs={{0,2},{1,3},{2,0},{3,1},{4,6},{5,7},{6,4},{7,5},{8,10},{9,11},{10,... | collective-permute-start | bytes 1474568 | tf_op jit(solution)/shard_map/ppermute | solution.py:101
  424.4 12.5 %collective-permute-start.8 = (bf16[160,1536]{1,0:T(8,128)(2,1)S(1)}, bf16[160,1536]{1,0:T(8,128)(2,1)S(1)}, u32[]{:S(2)}, u32[]{:S(2)}) collective-permute-start(bf16[160,1536]{1,0:T(8,128)(2,1)S(1)} %get-tuple-element.8), channel_id=1, source_target_pairs={{0,2},{1,3},{2,0},{3,1},{4,6},{5,7},{6,4},{7,5},{8,10},{9,11},{10,... | collective-permute-start | bytes 1474568 | tf_op jit(solution)/shard_map/ppermute | solution.py:101
  436.9 2.6 collective-permute-start.9
  437.1 2.5 copy-start.7
  437.1 2.5 copy-start.8
Sparse Core Ops, SparseCore 0:
  69.1 113.0 reduce-scatter.4
  243.4 96.9 reduce-scatter.6
  345.4 55.2 all-gather.1

commit v7 on v5

--- a/solution.py
+++ b/solution.py
@@ -116,6 +116,27 @@
         both = lax.dynamic_update_slice_in_dim(both, out, upper * size, 0)
         out = lax.dynamic_update_slice_in_dim(both, other, (1 - upper) * size, 0)
         bit *= 2
+    return out
+
+
+def gather_causal(x, axis):
+    count = lax.axis_size(axis)
+    if count != 4:
+        return gather_rows(x, axis)
+    index = lax.axis_index(axis)
+    rows = x.shape[0]
+    lower = lax.ppermute(x, axis, perm=[(0, 2), (1, 3)])
+    pair = jnp.concatenate([x, lower], axis=0)
+    other = pair_exchange(pair, axis, count, 1)
+    partner = index ^ 1
+    out = jnp.zeros((count * rows,) + x.shape[1:], x.dtype)
+    for block, at in (
+        (x, index),
+        (lower, (index + 2) % 4),
+        (other[:rows], partner),
+        (other[rows:], (partner + 2) % 4),
+    ):
+        out = lax.dynamic_update_slice_in_dim(out, block, at * rows, 0)
     return out
 
 
@@ -176,31 +197,24 @@
     value_used = lax.dynamic_slice_in_dim(
         value_head_rows, first_shared * HEAD_SIZE, shared_heads * HEAD_SIZE, 1
     )
-    packed_kv = gather_rows(jnp.concatenate([key_used, value_used], axis=1), "ctx")
-    halves = 2 if rows_local % 256 == 0 else 1
-    half_rows = rows_local // halves
-    resid_parts = []
-    for half in range(halves):
-        offset = jnp.reshape(ctx_index * rows_local + half * half_rows, (1,)).astype(jnp.int32)
-        query_part = lax.slice_in_dim(queries, half * half_rows, (half + 1) * half_rows, axis=0)
-        attended = attend(query_part, packed_kv, offset, shared_heads, per_shared)
-        partial_out = jnp.dot(attended, out_weight, preferred_element_type=jnp.float32)
-        head_sum = lax.psum_scatter(
-            partial_out.astype(jnp.bfloat16), "wide", scatter_dimension=1, tiled=True
-        ).astype(jnp.float32)
-        residual_part = lax.slice_in_dim(residual, half * half_rows, (half + 1) * half_rows, axis=0)
-        resid_parts.append((residual_part.astype(jnp.float32) + head_sum).astype(jnp.bfloat16))
-    resid = jnp.concatenate(resid_parts, axis=0)
+    packed_kv = gather_causal(jnp.concatenate([key_used, value_used], axis=1), "ctx")
+    offset = jnp.reshape(ctx_index * rows_local, (1,)).astype(jnp.int32)
+    attended = attend(queries, packed_kv, offset, shared_heads, per_shared)
+    partial_out = jnp.dot(attended, out_weight, preferred_element_type=jnp.float32)
+    head_sum = lax.psum_scatter(
+        partial_out.astype(jnp.bfloat16), "wide", scatter_dimension=1, tiled=True
+    ).astype(jnp.float32)
+    resid = (residual.astype(jnp.float32) + head_sum).astype(jnp.bfloat16)
     seq_len = rows_local * ctx_count
     capacity = seq_len * 5 // 16
     width_local = resid.shape[1]
     wide_count = lax.axis_size("wide")
+    slot_of_token = token_slots(expert_ids, slot_ids, capacity)
+    partner = jnp.sum(expert_ids, axis=1)
+    slot_local = lax.dynamic_slice_in_dim(slot_of_token, ctx_index * rows_local, rows_local)
     pieces = 2 if capacity % (16 * max(wide_count, ctx_count)) == 0 else 1
     piece_slots = capacity // pieces
     chunk = piece_slots // wide_count
-    slot_of_token = token_slots(expert_ids, slot_ids, capacity)
-    partner = jnp.sum(expert_ids, axis=1)
-    slot_local = lax.dynamic_slice_in_dim(slot_of_token, ctx_index * rows_local, rows_local)
     gain = norm_gain.astype(jnp.float32)[None, :]
     moe_rows = jnp.zeros((rows_local, width_local), jnp.float32)
     after_sums = None
@@ -218,20 +232,27 @@
         gate_part = jnp.dot(scaled, gate_weight, preferred_element_type=jnp.float32)
         up_part = jnp.dot(scaled, up_weight, preferred_element_type=jnp.float32)
         logit_part = jnp.dot(scaled, router_weight, preferred_element_type=jnp.float32)
+        hidden_local = gate_part.shape[1]
         experts = logit_part.shape[1]
         pad = 128 - (experts + 1) % 128
-        small = jnp.concatenate(
-            [logit_part, square_part[:, None], jnp.zeros((piece_slots, pad), jnp.float32)],
+        packed = jnp.concatenate(
+            [
+                gate_part,
+                up_part,
+                logit_part,
+                square_part[:, None],
+                jnp.zeros((piece_slots, pad), jnp.float32),
+            ],
             axis=1,
+        ).astype(jnp.bfloat16)
+        after_sums = packed
+        reduced = lax.psum_scatter(packed, "wide", scatter_dimension=0, tiled=True).astype(
+            jnp.float32
         )
-        sent = tuple(part.astype(jnp.bfloat16) for part in (gate_part, up_part, small))
-        after_sums = sent
-        gate_sum, up_sum, small_sum = (
-            lax.psum_scatter(part, "wide", scatter_dimension=0, tiled=True).astype(jnp.float32)
-            for part in sent
-        )
-        logit_sum = small_sum[:, :experts]
-        square_sum = small_sum[:, experts]
+        gate_sum = reduced[:, :hidden_local]
+        up_sum = reduced[:, hidden_local : 2 * hidden_local]
+        logit_sum = reduced[:, 2 * hidden_local : 2 * hidden_local + experts]
+        square_sum = reduced[:, 2 * hidden_local + experts]
         chunk_slots = piece * piece_slots + wide_index * chunk + jnp.arange(chunk, dtype=jnp.int32)
         other_chunk = jnp.sum(
             jnp.where(chunk_slots[:, None] == slot_of_token[None, :], partner[None, :], 0),

time: 506 us -> 450 us (0.89); the launches traced: 498 us -> 449 us
  waiting for transfers between devices: 347 us -> 296 us
  local copies, waits for them, and re-layouts: 14.5 us -> 29.8 us
  matrix products: 68.8 us -> 57.4 us
    reduce_scatter x4 -> x0, waiting for transfers between devices: 95.1 us -> none  [local(): lax.psum_scatter(part, 'wide', scatter_dimension=0, tiled=True)]
    unnamed x12 -> x7, waiting for transfers between devices: 17.9 us -> 59.8 us
    ppermute x18 -> x17, waiting for transfers between devices: 74.3 us -> 54.5 us  [pair_exchange(): return lax.ppermute(x, axis, perm=[(i, i ^ bit) for i in range(count)])]
    reduce_scatter x2 -> x1, waiting for transfers between devices: 98.8 us -> 112 us  [local(): lax.psum_scatter(partial_out.astype(jnp.bfloat16), 'wide', scatter_dimens...]
    ppermute x0 -> x1, waiting for transfers between devices: none -> 11.1 us  [gather_causal(): lower = lax.ppermute(x, axis, perm=[(0, 2), (1, 3)])]
    concatenate x1 -> x2, local copies, waits for them, and re-layouts: 0.08 us -> 10.2 us  [local(): jnp.concatenate([gate_part, up_part, logit_part, square_part[:, None], jn...]
    dot_general x2 -> x1, matrix products: 25.7 us -> 15.8 us  [local(): jnp.dot(attended, out_weight, preferred_element_type=jnp.float32)]
    ppermute x18 -> x17, starting transfers between devices: 16.3 us -> 12 us  [pair_exchange(): return lax.ppermute(x, axis, perm=[(i, i ^ bit) for i in range(count)])]
  transfers between devices with their start and end apart: 28 -> 23, of which waited for: 24 -> 20; matrix products, arithmetic and copies ran while one was open for 12% -> 10% of each run, Pallas kernels for 2% -> 0%
where the time goes in v7:
time: 450 us; the launch traced here: 449 us
  waiting for transfers between devices  296 us (66%)
  matrix products  57.4 us (13%)
  local copies, waits for them, and re-layouts  29.8 us (7%)
  Pallas kernels  23.4 us (5%)
  starting transfers between devices  17.5 us (4%)
  between operations  13.8 us (3%)
  other arithmetic  11.3 us (3%)
    reduce_scatter x1, waiting for transfers between devices, local(): lax.psum_scatter(partial_out.astype(jnp.bfloat16), 'wide', scatter_dimens...  112 us
    unnamed x7, waiting for transfers between devices  59.8 us
    all_gather x2, waiting for transfers between devices, local(): hidden = lax.all_gather(hidden_chunk, 'wide', axis=0, tiled=True)  58.5 us
    ppermute x17, waiting for transfers between devices, pair_exchange(): return lax.ppermute(x, axis, perm=[(i, i ^ bit) for i in range(count)])  54.5 us
    pallas_call x1, Pallas kernels, attend(): pl.pallas_call(kernel, grid_spec=grid_spec, out_shape=jax.ShapeDtypeStruc...  23.4 us
    dot_general x1, matrix products, local(): jnp.dot(attended, out_weight, preferred_element_type=jnp.float32)  15.8 us
    dot_general x2, matrix products, local(): jnp.dot(hidden, down_weight, preferred_element_type=jnp.float32)  12.2 us
    ppermute x17, starting transfers between devices, pair_exchange(): return lax.ppermute(x, axis, perm=[(i, i ^ bit) for i in range(count)])  12 us
  transfers between devices with their start and end apart: 23, of which 20 were waited for; matrix products, arithmetic and copies ran while one was open for 10% of the time, Pallas kernels for 0%

profile of v7, /device:TPU:0, one launch (start us, length us, event | category | flops | bytes accessed | tf_op | source)
XLA Modules:
  0.0 449.4 jit_solution(658273083420580922)
XLA Ops:
  7.8 4.9 %collective-permute-start = (bf16[512,512]{1,0:T(8,128)(2,1)S(1)}, bf16[512,512]{1,0:T(8,128)(2,1)S(1)}, u32[]{:S(2)}, u32[]{:S(2)}) collective-permute-start(bf16[512,512]{1,0:T(8,128)(2,1)S(1)} %get-tuple-element.25), channel_id=1, source_target_pairs={{0,2},{1,3},{4,6},{5,7},{8,10},{9,11},{12,14},{13,15},{16,18},{17,... | collective-permute-start | bytes 1572872 | tf_op jit(solution)/shard_map/ppermute | solution.py:128
  12.8 11.1 %collective-permute-done = bf16[512,512]{1,0:T(8,128)(2,1)S(1)} collective-permute-done((bf16[512,512]{1,0:T(8,128)(2,1)S(1)}, bf16[512,512]{1,0:T(8,128)(2,1)S(1)}, u32[]{:S(2)}, u32[]{:S(2)}) %collective-permute-start) | collective-permute-done | bytes 524320 | tf_op jit(solution)/shard_map/ppermute | solution.py:128
  25.0 3.0 collective-permute-done.1
  30.1 23.4 %shard_map.118 = bf16[512,1536]{1,0:T(8,128)(2,1)S(1)} custom-call(s32[1]{0:T(128)} %bitcast.offset_ref, bf16[512,1536]{1,0:T(8,128)(2,1)S(1)} %copy-done.2, bf16[2048,512]{1,0:T(8,128)(2,1)S(1)} %slice_dynamic-update-slice_fusion.k_ref.v_ref, bf16[2048,512]{1,0:T(8,128)(2,1)S(1)} %slice_dynamic-update-slice_fusion.k_ref.v_ref), custom_call_target="tpu_custom_call" | custom-call | tf_op jit(solution)/shard_map/pallas_call | solution.py:91
  53.5 15.8 %convolution_convert_fusion = bf16[512,6144]{1,0:T(8,128)(2,1)} fusion(bf16[512,1536]{1,0:T(8,128)(2,1)S(1)} %shard_map.118, bf16[1536,6144]{1,0:T(8,128)(2,1)} %param.16), kind=kOutput, calls=%fused_computation | convolution fusion | flops 9666822144 | bytes 26738688 | tf_op jit(solution)/shard_map/dot_general | solution.py:203
  70.1 112.3 %reduce-scatter.8.cloned.1.call-done = bf16[512,1536]{1,0:T(8,128)(2,1)} async-done(((bf16[512,6144]{1,0:T(8,128)(2,1)}), bf16[512,1536]{1,0:T(8,128)(2,1)}) %reduce-scatter.8.cloned.1.call-update) | async-done | bytes 1572880 | tf_op jit(solution)/shard_map/reduce_scatter | solution.py:204
  182.5 3.5 fusion.20
  192.0 6.5 %collective-permute-done.3 = bf16[80,1536]{1,0:T(8,128)(2,1)S(1)} collective-permute-done((bf16[80,1536]{1,0:T(8,128)(2,1)S(1)}, bf16[80,1536]{1,0:T(8,128)(2,1)S(1)}, u32[]{:S(2)}, u32[]{:S(2)}) %collective-permute-start.3) | collective-permute-done | bytes 245792 | tf_op jit(solution)/shard_map/ppermute | solution.py:101
  200.2 5.7 %collective-permute-done.4 = bf16[80,1536]{1,0:T(8,128)(2,1)S(1)} collective-permute-done((bf16[80,1536]{1,0:T(8,128)(2,1)S(1)}, bf16[80,1536]{1,0:T(8,128)(2,1)S(1)}, u32[]{:S(2)}, u32[]{:S(2)}) %collective-permute-start.4) | collective-permute-done | bytes 245792 | tf_op jit(solution)/shard_map/ppermute | solution.py:101
  208.1 5.2 %convolution_convert_fusion.3 = bf16[320,2048]{1,0:T(8,128)(2,1)S(1)} fusion(bf16[1536,2048]{1,0:T(8,128)(2,1)} %param.20, bf16[320,1536]{1,0:T(8,128)(2,1)S(1)} %constant_dynamic-update-slice_fusion.12, f32[1536]{0:T(1024)S(1)} %convert_element_type.122), kind=kOutput, calls=%fused_computation.7 | convolution fusion | flops 2015395840 | bytes 8591360 | tf_op jit(solution)/shard_map/dot_general | solution.py:233
  213.3 3.3 convolution_convert_fusion.4
  217.3 4.9 %concatenate.16 = bf16[320,4224]{1,0:T(8,128)(2,1)} concatenate(bf16[320,2048]{1,0:T(8,128)(2,1)} %convolution_convert_fusion.4, bf16[320,2048]{1,0:T(8,128)(2,1)S(1)} %convolution_convert_fusion.3, bf16[320,8]{1,0:T(8,128)(2,1)S(1)} %copy.33, bf16[320,1]{1,0:T(8,128)(2,1)S(1)} %broadcast_in_dim.75, bf16[320,119]{1,0:T(8,128)(2,1)S(1)} %broadcast.77), dimensions={1} | concatenate | bytes 5406720 | tf_op jit(solution)/shard_map/concatenate | solution.py:238
  228.1 6.5 %collective-permute-done.11 = bf16[80,1536]{1,0:T(8,128)(2,1)S(1)} collective-permute-done((bf16[80,1536]{1,0:T(8,128)(2,1)S(1)}, bf16[80,1536]{1,0:T(8,128)(2,1)S(1)}, u32[]{:S(2)}, u32[]{:S(2)}) %collective-permute-start.11) | collective-permute-done | bytes 245792 | tf_op jit(solution)/shard_map/ppermute | solution.py:101
  236.3 5.8 %collective-permute-done.12 = bf16[80,1536]{1,0:T(8,128)(2,1)S(1)} collective-permute-done((bf16[80,1536]{1,0:T(8,128)(2,1)S(1)}, bf16[80,1536]{1,0:T(8,128)(2,1)S(1)}, u32[]{:S(2)}, u32[]{:S(2)}) %collective-permute-start.12) | collective-permute-done | bytes 245792 | tf_op jit(solution)/shard_map/ppermute | solution.py:101
  247.2 6.5 %convolution_convert_fusion.1 = bf16[320,2048]{1,0:T(8,128)(2,1)} fusion(bf16[1536,2048]{1,0:T(8,128)(2,1)} %param.20, bf16[320,1536]{1,0:T(8,128)(2,1)} %copy-done.5, f32[1536]{0:T(1024)S(1)} %convert_element_type.122), kind=kOutput, calls=%fused_computation.5 | convolution fusion | flops 2015395840 | bytes 8591360 | tf_op jit(solution)/shard_map/dot_general | solution.py:233
  253.7 6.1 %convolution_convert_fusion.2 = bf16[320,2048]{1,0:T(8,128)(2,1)} fusion(bf16[1536,2048]{1,0:T(8,128)(2,1)} %param.19, bf16[320,1536]{1,0:T(8,128)(2,1)S(1)} %copy-done.6, f32[1536]{0:T(1024)S(1)} %convert_element_type.122), kind=kOutput, calls=%fused_computation.6 | convolution fusion | flops 2015395840 | bytes 8591360 | tf_op jit(solution)/shard_map/dot_general | solution.py:232
  259.8 5.3 %concatenate.17 = bf16[320,4224]{1,0:T(8,128)(2,1)} concatenate(bf16[320,2048]{1,0:T(8,128)(2,1)} %convolution_convert_fusion.2, bf16[320,2048]{1,0:T(8,128)(2,1)} %convolution_convert_fusion.1, bf16[320,8]{1,0:T(8,128)(2,1)S(1)} %copy.37, bf16[320,1]{1,0:T(8,128)(2,1)S(1)} %broadcast_in_dim.76, bf16[320,119]{1,0:T(8,128)(2,1)S(1)} %broadcast.77), dimensions={1} | concatenate | bytes 5406720 | tf_op jit(solution)/shard_map/concatenate | solution.py:238
  265.7 10.9 %reduce-scatter.10.cloned.1.call-done = bf16[80,4224]{1,0:T(8,128)(2,1)} async-done(((bf16[320,4224]{1,0:T(8,128)(2,1)}), bf16[80,4224]{1,0:T(8,128)(2,1)}) %reduce-scatter.10.cloned.1.call-update) | async-done | bytes 675856
  276.6 2.3 copy.42
  281.5 2.0 copy.36
  283.5 48.8 %reduce-scatter.12.cloned.1.call-done = bf16[80,4224]{1,0:T(8,128)(2,1)} async-done(((bf16[320,4224]{1,0:T(8,128)(2,1)}), bf16[80,4224]{1,0:T(8,128)(2,1)}) %reduce-scatter.12.cloned.1.call-update) | async-done | bytes 675856
  332.3 2.3 copy.44
  337.1 28.7 %all-gather.3.cloned.1.call-done = bf16[320,2048]{1,0:T(8,128)(2,1)} async-done(((bf16[80,2048]{1,0:T(8,128)(2,1)}), bf16[320,2048]{1,0:T(8,128)(2,1)}) %all-gather.3.cloned.1.call-update) | async-done | bytes 1310736 | tf_op jit(solution)/shard_map/all_gather | solution.py:264
  365.9 6.7 %fusion.41 = f32[320,1536]{1,0:T(8,128)} fusion(bf16[320,2048]{1,0:T(8,128)(2,1)} %all-gather.3.cloned.1.call-done, bf16[2048,1536]{1,0:T(8,128)(2,1)} %param.21), kind=kOutput, calls=%fused_computation.113 | convolution fusion | flops 2013265920 | bytes 9568256 | tf_op jit(solution)/shard_map/dot_general | solution.py:265
  374.6 2.0 dynamic-slice_convert_fusion.2
  376.6 29.7 %all-gather.5.cloned.1.call-done = bf16[320,2048]{1,0:T(8,128)(2,1)} async-done(((bf16[80,2048]{1,0:T(8,128)(2,1)}), bf16[320,2048]{1,0:T(8,128)(2,1)}) %all-gather.5.cloned.1.call-update) | async-done | bytes 1310736 | tf_op jit(solution)/shard_map/all_gather | solution.py:264
  406.3 5.5 %fusion.42 = f32[320,1536]{1,0:T(8,128)S(1)} fusion(bf16[320,2048]{1,0:T(8,128)(2,1)} %all-gather.5.cloned.1.call-done, bf16[2048,1536]{1,0:T(8,128)(2,1)} %param.21), kind=kOutput, calls=%fused_computation.114 | convolution fusion | flops 2013265920 | bytes 9568256 | tf_op jit(solution)/shard_map/dot_general | solution.py:265
  415.5 6.6 %collective-permute-done.7 = bf16[80,1536]{1,0:T(8,128)(2,1)S(1)} collective-permute-done((bf16[80,1536]{1,0:T(8,128)(2,1)S(1)}, bf16[80,1536]{1,0:T(8,128)(2,1)S(1)}, u32[]{:S(2)}, u32[]{:S(2)}) %collective-permute-start.7) | collective-permute-done | bytes 245792 | tf_op jit(solution)/shard_map/ppermute | solution.py:101
  423.7 3.6 collective-permute-done.15
  429.0 3.6 collective-permute-done.8
  432.7 4.7 %collective-permute-done.16 = bf16[80,1536]{1,0:T(8,128)(2,1)S(1)} collective-permute-done((bf16[80,1536]{1,0:T(8,128)(2,1)S(1)}, bf16[80,1536]{1,0:T(8,128)(2,1)S(1)}, u32[]{:S(2)}, u32[]{:S(2)}) %collective-permute-start.16) | collective-permute-done | bytes 245792 | tf_op jit(solution)/shard_map/ppermute | solution.py:101
  440.4 2.4 fusion.1
  (134 shorter events, 46.1 us)
Async XLA Ops:
  6.5 210.1 %copy-start = (bf16[1536,8]{0,1:T(8,128)(2,1)S(1)}, bf16[1536,8]{0,1:T(8,128)(2,1)}, u32[]{:S(2)}) copy-start(bf16[1536,8]{0,1:T(8,128)(2,1)} %param.18) | copy-start | bytes 73732
  6.5 175.9 %reduce-scatter.8.cloned.1.call-start = ((), (), s32[]{:S(2)}) async-start(), calls=%async_computation.3 | async-start | bytes 7864320 | tf_op jit(solution)/shard_map/reduce_scatter | solution.py:204
  7.8 16.0 %collective-permute-start = (bf16[512,512]{1,0:T(8,128)(2,1)S(1)}, bf16[512,512]{1,0:T(8,128)(2,1)S(1)}, u32[]{:S(2)}, u32[]{:S(2)}) collective-permute-start(bf16[512,512]{1,0:T(8,128)(2,1)S(1)} %get-tuple-element.25), channel_id=1, source_target_pairs={{0,2},{1,3},{4,6},{5,7},{8,10},{9,11},{12,14},{13,15},{16,18},{17,... | collective-permute-start | bytes 1572872 | tf_op jit(solution)/shard_map/ppermute | solution.py:128
  24.9 3.0 collective-permute-start.1
  24.9 5.2 %copy-start.2 = (bf16[512,1536]{1,0:T(8,128)(2,1)S(1)}, bf16[512,1536]{1,0:T(8,128)(2,1)}, u32[]{:S(2)}) copy-start(bf16[512,1536]{1,0:T(8,128)(2,1)} %q_ref.1) | copy-start | bytes 4718596
  69.3 113.2 %copy-start.3 = (bf16[512,1536]{1,0:T(8,128)(2,1)S(1)}, bf16[512,1536]{1,0:T(8,128)(2,1)}, u32[]{:S(2)}) copy-start(bf16[512,1536]{1,0:T(8,128)(2,1)} %param.15) | copy-start | bytes 4718596
  69.3 207.3 %reduce-scatter.10.cloned.1.call-start = ((), (), s32[]{:S(2)}) async-start(), calls=%async_computation.6 | async-start | bytes 3379200
  187.2 1.9 collective-permute-start.2
  190.4 15.5 %copy-start.10 = (bf16[1536]{0:T(1024)(128)(2,1)S(1)}, bf16[1536]{0:T(1024)(128)(2,1)}, u32[]{:S(2)}) copy-start(bf16[1536]{0:T(1024)(128)(2,1)} %param.17) | copy-start | bytes 9220
  190.5 8.1 %collective-permute-start.3 = (bf16[80,1536]{1,0:T(8,128)(2,1)S(1)}, bf16[80,1536]{1,0:T(8,128)(2,1)S(1)}, u32[]{:S(2)}, u32[]{:S(2)}) collective-permute-start(bf16[80,1536]{1,0:T(8,128)(2,1)S(1)} %dynamic-slice_convert_fusion.7), channel_id=1, source_target_pairs={{0,2},{1,3},{2,0},{3,1},{4,6},{5,7},{6,4},{7,5},{8,10},{9,11},{10,... | collective-permute-start | bytes 737288 | tf_op jit(solution)/shard_map/ppermute | solution.py:101
  198.6 7.2 %collective-permute-start.4 = (bf16[80,1536]{1,0:T(8,128)(2,1)S(1)}, bf16[80,1536]{1,0:T(8,128)(2,1)S(1)}, u32[]{:S(2)}, u32[]{:S(2)}) collective-permute-start(bf16[80,1536]{1,0:T(8,128)(2,1)S(1)} %get-tuple-element.24), channel_id=1, source_target_pairs={{0,2},{1,3},{2,0},{3,1},{4,6},{5,7},{6,4},{7,5},{8,10},{9,11},{10,... | collective-permute-start | bytes 737288 | tf_op jit(solution)/shard_map/ppermute | solution.py:101
  205.9 1.9 collective-permute-start.5
  207.8 5.5 %slice-start = ((s8[6291456]{0:T(1024)(128)(4,1)}), s8[4194304]{0:T(1024)(128)(4,1)S(1)}, s32[]{:S(2)}) async-start(s8[6291456]{0:T(1024)(128)(4,1)} %bitcast.41), calls=%async_computation.8 | async-start | bytes 8388608
  208.1 5.2 %slice-start.1 = ((s8[6291456]{0:T(1024)(128)(4,1)}), s8[2097152]{0:T(1024)(128)(4,1)S(1)}, s32[]{:S(2)}) async-start(s8[6291456]{0:T(1024)(128)(4,1)} %bitcast.41), calls=%async_computation.9 | async-start | bytes 4194304
  222.2 110.0 %reduce-scatter.12.cloned.1.call-start = ((), (), s32[]{:S(2)}) async-start(), calls=%async_computation.7 | async-start | bytes 3379200
  224.5 1.9 collective-permute-start.10
  226.6 8.1 %collective-permute-start.11 = (bf16[80,1536]{1,0:T(8,128)(2,1)S(1)}, bf16[80,1536]{1,0:T(8,128)(2,1)S(1)}, u32[]{:S(2)}, u32[]{:S(2)}) collective-permute-start(bf16[80,1536]{1,0:T(8,128)(2,1)S(1)} %dynamic-slice_convert_fusion.5), channel_id=1, source_target_pairs={{0,2},{1,3},{2,0},{3,1},{4,6},{5,7},{6,4},{7,5},{8,10},{9,11},{10,... | collective-permute-start | bytes 737288 | tf_op jit(solution)/shard_map/ppermute | solution.py:101
  234.7 7.3 %collective-permute-start.12 = (bf16[80,1536]{1,0:T(8,128)(2,1)S(1)}, bf16[80,1536]{1,0:T(8,128)(2,1)S(1)}, u32[]{:S(2)}, u32[]{:S(2)}) collective-permute-start(bf16[80,1536]{1,0:T(8,128)(2,1)S(1)} %get-tuple-element.22), channel_id=1, source_target_pairs={{0,2},{1,3},{2,0},{3,1},{4,6},{5,7},{6,4},{7,5},{8,10},{9,11},{10,... | collective-permute-start | bytes 737288 | tf_op jit(solution)/shard_map/ppermute | solution.py:101
  242.1 1.9 collective-permute-start.13
  247.1 6.5 %copy-start.6 = (bf16[320,1536]{1,0:T(8,128)(2,1)S(1)}, bf16[320,1536]{1,0:T(8,128)(2,1)}, u32[]{:S(2)}) copy-start(bf16[320,1536]{1,0:T(8,128)(2,1)} %copy-done.5) | copy-start | bytes 2949124
  265.1 100.8 %all-gather.3.cloned.1.call-start = ((), (), s32[]{:S(2)}) async-start(), calls=%async_computation.4 | async-start | bytes 1638400 | tf_op jit(solution)/shard_map/all_gather | solution.py:264
  283.5 122.9 %all-gather.5.cloned.1.call-start = ((), (), s32[]{:S(2)}) async-start(), calls=%async_computation.5 | async-start | bytes 1638400 | tf_op jit(solution)/shard_map/all_gather | solution.py:264
  376.6 35.4 %collective-permute-start.6 = (bf16[160,1536]{1,0:T(8,128)(2,1)}, bf16[160,1536]{1,0:T(8,128)(2,1)}, u32[]{:S(2)}, u32[]{:S(2)}) collective-permute-start(bf16[160,1536]{1,0:T(8,128)(2,1)} %dynamic-slice_convert_fusion.2), channel_id=1, source_target_pairs={{0,1},{1,0},{2,3},{3,2},{4,5},{5,4},{6,7},{7,6},{8,9},{9,8},{10,11... | collective-permute-start | bytes 1474568 | tf_op jit(solution)/shard_map/ppermute | solution.py:101
  406.3 5.7 %copy-start.7 = (f32[320,1536]{1,0:T(8,128)S(1)}, f32[320,1536]{1,0:T(8,128)}, u32[]{:S(2)}) copy-start(f32[320,1536]{1,0:T(8,128)} %fusion.41) | copy-start | bytes 5898244
  411.9 2.8 collective-permute-start.14
  413.2 8.9 %collective-permute-start.7 = (bf16[80,1536]{1,0:T(8,128)(2,1)S(1)}, bf16[80,1536]{1,0:T(8,128)(2,1)S(1)}, u32[]{:S(2)}, u32[]{:S(2)}) collective-permute-start(bf16[80,1536]{1,0:T(8,128)(2,1)S(1)} %dynamic-slice_convert_fusion.6), channel_id=1, source_target_pairs={{0,2},{1,3},{2,0},{3,1},{4,6},{5,7},{6,4},{7,5},{8,10},{9,11},{10,... | collective-permute-start | bytes 737288 | tf_op jit(solution)/shard_map/ppermute | solution.py:101
  414.9 12.5 %collective-permute-start.15 = (bf16[80,1536]{1,0:T(8,128)(2,1)S(1)}, bf16[80,1536]{1,0:T(8,128)(2,1)S(1)}, u32[]{:S(2)}, u32[]{:S(2)}) collective-permute-start(bf16[80,1536]{1,0:T(8,128)(2,1)S(1)} %dynamic-slice_convert_fusion.4), channel_id=1, source_target_pairs={{0,2},{1,3},{2,0},{3,1},{4,6},{5,7},{6,4},{7,5},{8,10},{9,11},{10,... | collective-permute-start | bytes 737288 | tf_op jit(solution)/shard_map/ppermute | solution.py:101
  422.2 10.4 %collective-permute-start.8 = (bf16[80,1536]{1,0:T(8,128)(2,1)S(1)}, bf16[80,1536]{1,0:T(8,128)(2,1)S(1)}, u32[]{:S(2)}, u32[]{:S(2)}) collective-permute-start(bf16[80,1536]{1,0:T(8,128)(2,1)S(1)} %get-tuple-element.14), channel_id=1, source_target_pairs={{0,2},{1,3},{2,0},{3,1},{4,6},{5,7},{6,4},{7,5},{8,10},{9,11},{10,... | collective-permute-start | bytes 737288 | tf_op jit(solution)/shard_map/ppermute | solution.py:101
  427.5 9.9 %collective-permute-start.16 = (bf16[80,1536]{1,0:T(8,128)(2,1)S(1)}, bf16[80,1536]{1,0:T(8,128)(2,1)S(1)}, u32[]{:S(2)}, u32[]{:S(2)}) collective-permute-start(bf16[80,1536]{1,0:T(8,128)(2,1)S(1)} %get-tuple-element.16), channel_id=1, source_target_pairs={{0,2},{1,3},{2,0},{3,1},{4,6},{5,7},{6,4},{7,5},{8,10},{9,11},{10,... | collective-permute-start | bytes 737288 | tf_op jit(solution)/shard_map/ppermute | solution.py:101
  432.7 5.0 %collective-permute-start.9 = (bf16[160,1536]{1,0:T(8,128)(2,1)S(1)}, bf16[160,1536]{1,0:T(8,128)(2,1)S(1)}, u32[]{:S(2)}, u32[]{:S(2)}) collective-permute-start(bf16[160,1536]{1,0:T(8,128)(2,1)S(1)} %constant_dynamic-update-slice_fusion.9), channel_id=1, source_target_pairs={{0,1},{1,0},{2,3},{3,2},{4,5},{5,4},{6,7},{7,6},{8,9},{9,8},{10,11... | collective-permute-start | bytes 1474568 | tf_op jit(solution)/shard_map/ppermute | solution.py:101
  437.4 1.9 collective-permute-start.17
  440.4 2.4 copy-start.1
  (4 other events, 3.8 us)
Sparse Core Ops, SparseCore 0:
  69.4 113.0 reduce-scatter.7
  222.4 54.1 reduce-scatter.9
  278.9 53.3 reduce-scatter.11
  333.7 32.1 all-gather.2
  374.7 31.6 all-gather.4

commit v8 on v4

--- a/solution.py
+++ b/solution.py
@@ -116,6 +116,27 @@
         both = lax.dynamic_update_slice_in_dim(both, out, upper * size, 0)
         out = lax.dynamic_update_slice_in_dim(both, other, (1 - upper) * size, 0)
         bit *= 2
+    return out
+
+
+def gather_causal(x, axis):
+    count = lax.axis_size(axis)
+    if count != 4:
+        return gather_rows(x, axis)
+    index = lax.axis_index(axis)
+    rows = x.shape[0]
+    lower = lax.ppermute(x, axis, perm=[(0, 2), (1, 3)])
+    pair = jnp.concatenate([x, lower], axis=0)
+    other = pair_exchange(pair, axis, count, 1)
+    partner = index ^ 1
+    out = jnp.zeros((count * rows,) + x.shape[1:], x.dtype)
+    for block, at in (
+        (x, index),
+        (lower, (index + 2) % 4),
+        (other[:rows], partner),
+        (other[rows:], (partner + 2) % 4),
+    ):
+        out = lax.dynamic_update_slice_in_dim(out, block, at * rows, 0)
     return out
 
 
@@ -176,7 +197,7 @@
     value_used = lax.dynamic_slice_in_dim(
         value_head_rows, first_shared * HEAD_SIZE, shared_heads * HEAD_SIZE, 1
     )
-    packed_kv = gather_rows(jnp.concatenate([key_used, value_used], axis=1), "ctx")
+    packed_kv = gather_causal(jnp.concatenate([key_used, value_used], axis=1), "ctx")
     offset = jnp.reshape(ctx_index * rows_local, (1,)).astype(jnp.int32)
     attended = attend(queries, packed_kv, offset, shared_heads, per_shared)
     partial_out = jnp.dot(attended, out_weight, preferred_element_type=jnp.float32)
@@ -199,19 +220,25 @@
     buffer_wide = buffer.astype(jnp.float32)
     square_part = jnp.sum(buffer_wide * buffer_wide, axis=1)
     scaled = (buffer_wide * norm_gain.astype(jnp.float32)[None, :]).astype(jnp.bfloat16)
-    gate_part = jnp.dot(scaled, gate_weight, preferred_element_type=jnp.float32)
-    up_part = jnp.dot(scaled, up_weight, preferred_element_type=jnp.float32)
+    both_part = jnp.dot(
+        scaled,
+        jnp.concatenate([gate_weight, up_weight], axis=1),
+        preferred_element_type=jnp.float32,
+    )
     logit_part = jnp.dot(scaled, router_weight, preferred_element_type=jnp.float32)
+    hidden_local = gate_weight.shape[1]
     experts = logit_part.shape[1]
     pad = 128 - (experts + 1) % 128
     small = jnp.concatenate(
         [logit_part, square_part[:, None], jnp.zeros((capacity, pad), jnp.float32)], axis=1
     )
-    gate_sum, up_sum, small_sum = (
+    both_sum, small_sum = (
         lax.psum_scatter(part.astype(jnp.bfloat16), "wide", scatter_dimension=0, tiled=True)
         .astype(jnp.float32)
-        for part in (gate_part, up_part, small)
-    )
+        for part in (both_part, small)
+    )
+    gate_sum = both_sum[:, :hidden_local]
+    up_sum = both_sum[:, hidden_local:]
     logit_sum = small_sum[:, :experts]
     square_sum = small_sum[:, experts]
     chunk_slots = wide_index * chunk + jnp.arange(chunk, dtype=jnp.int32)

time: 460 us -> 444 us (0.965)
  waiting for transfers between devices: 355 us -> 335 us
    ppermute x10 -> x9, waiting for transfers between devices: 79.8 us -> 58 us  [pair_exchange(): return lax.ppermute(x, axis, perm=[(i, i ^ bit) for i in range(count)])]
    reduce_scatter x2 -> x1, waiting for transfers between devices: 106 us -> 93.4 us  [local(): lax.psum_scatter(part.astype(jnp.bfloat16), 'wide', scatter_dimension=0,...]
    ppermute x0 -> x1, waiting for transfers between devices: none -> 11.1 us  [gather_causal(): lower = lax.ppermute(x, axis, perm=[(0, 2), (1, 3)])]
    ppermute x0 -> x1, starting transfers between devices: none -> 4.9 us  [gather_causal(): lower = lax.ppermute(x, axis, perm=[(0, 2), (1, 3)])]
    ppermute x10 -> x9, starting transfers between devices: 9.87 us -> 6.43 us  [pair_exchange(): return lax.ppermute(x, axis, perm=[(i, i ^ bit) for i in range(count)])]
    dot_general x2 -> x1, matrix products: 16.6 us -> 15.3 us  [local(): jnp.dot(scaled, jnp.concatenate([gate_weight, up_weight], axis=1), prefer...]
  transfers between devices with their start and end apart: 15 -> 14, of which waited for: 15 -> 14; matrix products, arithmetic and copies ran while one was open for 4% -> 4% of each run, Pallas kernels for 0% -> 0%
where the time goes in v8:
time: 444 us
  waiting for transfers between devices  335 us (75%)
  matrix products  44.1 us (10%)
  Pallas kernels  23.4 us (5%)
  between operations  13.5 us (3%)
  starting transfers between devices  11.9 us (3%)
  local copies, waits for them, and re-layouts  8.85 us (2%)
  other arithmetic  7.27 us (2%)
    reduce_scatter x1, waiting for transfers between devices, local(): lax.psum_scatter(partial_out.astype(jnp.bfloat16), 'wide', scatter_dimens...  112 us
    reduce_scatter x1, waiting for transfers between devices, local(): lax.psum_scatter(part.astype(jnp.bfloat16), 'wide', scatter_dimension=0,...  93.4 us
    ppermute x9, waiting for transfers between devices, pair_exchange(): return lax.ppermute(x, axis, perm=[(i, i ^ bit) for i in range(count)])  58 us
    all_gather x1, waiting for transfers between devices, local(): hidden = lax.all_gather(hidden_chunk, 'wide', axis=0, tiled=True)  55.4 us
    pallas_call x1, Pallas kernels, attend(): pl.pallas_call(kernel, grid_spec=grid_spec, out_shape=jax.ShapeDtypeStruc...  23.4 us
    dot_general x1, matrix products, local(): jnp.dot(attended, out_weight, preferred_element_type=jnp.float32)  15.8 us
    dot_general x1, matrix products, local(): jnp.dot(scaled, jnp.concatenate([gate_weight, up_weight], axis=1), prefer...  15.3 us
    ppermute x1, waiting for transfers between devices, gather_causal(): lower = lax.ppermute(x, axis, perm=[(0, 2), (1, 3)])  11.1 us
  transfers between devices with their start and end apart: 14, of which 14 were waited for; matrix products, arithmetic and copies ran while one was open for 4% of the time, Pallas kernels for 0%

profile of v8, /device:TPU:0, one launch (start us, length us, event | category | flops | bytes accessed | tf_op | source)
XLA Modules:
  0.0 443.6 jit_solution(16701199009745944526)
XLA Ops:
  6.5 1.1 constant_dynamic-slice_fusion
  7.9 4.9 %collective-permute-start = (bf16[512,512]{1,0:T(8,128)(2,1)S(1)}, bf16[512,512]{1,0:T(8,128)(2,1)S(1)}, u32[]{:S(2)}, u32[]{:S(2)}) collective-permute-start(bf16[512,512]{1,0:T(8,128)(2,1)S(1)} %get-tuple-element.13), channel_id=1, source_target_pairs={{0,2},{1,3},{4,6},{5,7},{8,10},{9,11},{12,14},{13,15},{16,18},{17,... | collective-permute-start | bytes 1572872 | tf_op jit(solution)/shard_map/ppermute | solution.py:128
  12.8 11.1 %collective-permute-done = bf16[512,512]{1,0:T(8,128)(2,1)S(1)} collective-permute-done((bf16[512,512]{1,0:T(8,128)(2,1)S(1)}, bf16[512,512]{1,0:T(8,128)(2,1)S(1)}, u32[]{:S(2)}, u32[]{:S(2)}) %collective-permute-start) | collective-permute-done | bytes 524320 | tf_op jit(solution)/shard_map/ppermute | solution.py:128
  25.0 3.0 collective-permute-done.1
  28.0 1.1 slice_dynamic-update-slice_fusion.1
  29.0 1.1 slice_dynamic-update-slice_fusion.k_ref.v_ref
  30.1 23.4 %shard_map.118 = bf16[512,1536]{1,0:T(8,128)(2,1)S(1)} custom-call(s32[1]{0:T(128)} %bitcast.offset_ref, bf16[512,1536]{1,0:T(8,128)(2,1)S(1)} %copy-done.2, bf16[2048,512]{1,0:T(8,128)(2,1)S(1)} %slice_dynamic-update-slice_fusion.k_ref.v_ref, bf16[2048,512]{1,0:T(8,128)(2,1)S(1)} %slice_dynamic-update-slice_fusion.k_ref.v_ref), custom_call_target="tpu_custom_call" | custom-call | tf_op jit(solution)/shard_map/pallas_call | solution.py:91
  53.5 15.8 %convolution_convert_fusion = bf16[512,6144]{1,0:T(8,128)(2,1)} fusion(bf16[512,1536]{1,0:T(8,128)(2,1)S(1)} %shard_map.118, bf16[1536,6144]{1,0:T(8,128)(2,1)} %param.16), kind=kOutput, calls=%fused_computation.4 | convolution fusion | flops 9666822144 | bytes 26738688 | tf_op jit(solution)/shard_map/dot_general | solution.py:203
  70.1 112.3 %reduce-scatter.6.cloned.1.call-done = bf16[512,1536]{1,0:T(8,128)(2,1)} async-done(((bf16[512,6144]{1,0:T(8,128)(2,1)}), bf16[512,1536]{1,0:T(8,128)(2,1)}) %reduce-scatter.6.cloned.1.call-update) | async-done | bytes 1572880 | tf_op jit(solution)/shard_map/reduce_scatter | solution.py:204
  182.5 2.7 fusion.16
  185.1 1.9 copy-done.3
  187.3 2.5 collective-permute-done.2
  189.8 1.8 convert_add_fusion.1
  191.7 1.5 collective-permute-start.3
  193.2 11.8 %collective-permute-done.3 = bf16[160,1536]{1,0:T(8,128)(2,1)S(1)} collective-permute-done((bf16[160,1536]{1,0:T(8,128)(2,1)S(1)}, bf16[160,1536]{1,0:T(8,128)(2,1)S(1)}, u32[]{:S(2)}, u32[]{:S(2)}) %collective-permute-start.3) | collective-permute-done | bytes 491552 | tf_op jit(solution)/shard_map/ppermute | solution.py:101
  205.2 1.5 collective-permute-start.4
  206.7 10.9 %collective-permute-done.4 = bf16[160,1536]{1,0:T(8,128)(2,1)S(1)} collective-permute-done((bf16[160,1536]{1,0:T(8,128)(2,1)S(1)}, bf16[160,1536]{1,0:T(8,128)(2,1)S(1)}, u32[]{:S(2)}, u32[]{:S(2)}) %collective-permute-start.4) | collective-permute-done | bytes 491552 | tf_op jit(solution)/shard_map/ppermute | solution.py:101
  218.1 2.2 collective-permute-done.5
  222.5 15.3 %fusion.4 = bf16[640,4096]{1,0:T(8,128)(2,1)} fusion(bf16[1536,2048]{1,0:T(8,128)(2,1)} %param.20, bf16[1536,2048]{1,0:T(8,128)(2,1)} %param.19, bf16[640,1536]{1,0:T(8,128)(2,1)S(1)} %constant_dynamic-update-slice_fusion.4, f32[1536]{0:T(1024)S(1)} %convert_element_type.83), kind=kOutput, calls=%fused_computation.5 | convolution fusion | flops 8083800064 | bytes 19798016 | tf_op jit(solution)/shard_map/dot_general | solution.py:223
  238.4 4.3 reduce-scatter.10.cloned.1.call-done
  243.7 93.4 %reduce-scatter.8.cloned.1.call-done = bf16[160,4096]{1,0:T(8,128)(2,1)} async-done(((bf16[640,4096]{1,0:T(8,128)(2,1)}), bf16[160,4096]{1,0:T(8,128)(2,1)}) %reduce-scatter.8.cloned.1.call-update) | async-done | bytes 1310736 | tf_op jit(solution)/shard_map/reduce_scatter | solution.py:236
  337.0 1.6 convert_element_type.86
  338.6 1.3 fusion.15
  340.0 55.4 %all-gather.2.cloned.1.call-done = bf16[640,2048]{1,0:T(8,128)(2,1)} async-done(((bf16[160,2048]{1,0:T(8,128)(2,1)}), bf16[640,2048]{1,0:T(8,128)(2,1)}) %all-gather.2.cloned.1.call-update) | async-done | bytes 2621456 | tf_op jit(solution)/shard_map/all_gather | solution.py:249
  395.4 7.1 %fusion.28 = f32[640,1536]{1,0:T(8,128)S(1)} fusion(bf16[640,2048]{1,0:T(8,128)(2,1)} %all-gather.2.cloned.1.call-done, bf16[2048,1536]{1,0:T(8,128)(2,1)} %param.21), kind=kOutput, calls=%fused_computation.66 | convolution fusion | flops 4026531840 | bytes 12845056 | tf_op jit(solution)/shard_map/dot_general | solution.py:250
  402.7 2.6 collective-permute-done.6
  405.6 1.5 collective-permute-start.7
  407.1 11.8 %collective-permute-done.7 = bf16[160,1536]{1,0:T(8,128)(2,1)S(1)} collective-permute-done((bf16[160,1536]{1,0:T(8,128)(2,1)S(1)}, bf16[160,1536]{1,0:T(8,128)(2,1)S(1)}, u32[]{:S(2)}, u32[]{:S(2)}) %collective-permute-start.7) | collective-permute-done | bytes 491552 | tf_op jit(solution)/shard_map/ppermute | solution.py:101
  419.1 1.5 collective-permute-start.8
  420.6 10.9 %collective-permute-done.8 = bf16[160,1536]{1,0:T(8,128)(2,1)S(1)} collective-permute-done((bf16[160,1536]{1,0:T(8,128)(2,1)S(1)}, bf16[160,1536]{1,0:T(8,128)(2,1)S(1)}, u32[]{:S(2)}, u32[]{:S(2)}) %collective-permute-start.8) | collective-permute-done | bytes 491552 | tf_op jit(solution)/shard_map/ppermute | solution.py:101
  431.9 2.3 collective-permute-done.9
  434.4 2.7 fusion.9
  (71 shorter events, 7.7 us)
Async XLA Ops:
  6.5 214.4 %copy-start = (bf16[1536,8]{0,1:T(8,128)(2,1)S(1)}, bf16[1536,8]{0,1:T(8,128)(2,1)}, u32[]{:S(2)}) copy-start(bf16[1536,8]{0,1:T(8,128)(2,1)} %param.18) | copy-start | bytes 73732
  6.5 175.9 %reduce-scatter.6.cloned.1.call-start = ((), (), s32[]{:S(2)}) async-start(), calls=%async_computation.3 | async-start | bytes 7864320 | tf_op jit(solution)/shard_map/reduce_scatter | solution.py:204
  7.9 16.0 %collective-permute-start = (bf16[512,512]{1,0:T(8,128)(2,1)S(1)}, bf16[512,512]{1,0:T(8,128)(2,1)S(1)}, u32[]{:S(2)}, u32[]{:S(2)}) collective-permute-start(bf16[512,512]{1,0:T(8,128)(2,1)S(1)} %get-tuple-element.13), channel_id=1, source_target_pairs={{0,2},{1,3},{4,6},{5,7},{8,10},{9,11},{12,14},{13,15},{16,18},{17,... | collective-permute-start | bytes 1572872 | tf_op jit(solution)/shard_map/ppermute | solution.py:128
  25.0 3.0 collective-permute-start.1
  25.0 5.2 %copy-start.2 = (bf16[512,1536]{1,0:T(8,128)(2,1)S(1)}, bf16[512,1536]{1,0:T(8,128)(2,1)}, u32[]{:S(2)}) copy-start(bf16[512,1536]{1,0:T(8,128)(2,1)} %q_ref.1) | copy-start | bytes 4718596
  69.3 0.7 copy-start.4
  69.3 0.7 copy-start.5
  69.3 113.2 %copy-start.7 = (bf16[512,1536]{1,0:T(8,128)(2,1)S(1)}, bf16[512,1536]{1,0:T(8,128)(2,1)}, u32[]{:S(2)}) copy-start(bf16[512,1536]{1,0:T(8,128)(2,1)} %param.15) | copy-start | bytes 4718596
  69.3 173.4 %reduce-scatter.10.cloned.1.call-start = ((), (), s32[]{:S(2)}) async-start(), calls=%async_computation.6 | async-start | bytes 204800
  185.1 1.9 copy-start.3
  187.2 2.6 collective-permute-start.2
  191.7 13.3 %collective-permute-start.3 = (bf16[160,1536]{1,0:T(8,128)(2,1)S(1)}, bf16[160,1536]{1,0:T(8,128)(2,1)S(1)}, u32[]{:S(2)}, u32[]{:S(2)}) collective-permute-start(bf16[160,1536]{1,0:T(8,128)(2,1)S(1)} %dynamic-slice_convert_fusion.3), channel_id=1, source_target_pairs={{0,2},{1,3},{2,0},{3,1},{4,6},{5,7},{6,4},{7,5},{8,10},{9,11},{10,... | collective-permute-start | bytes 1474568 | tf_op jit(solution)/shard_map/ppermute | solution.py:101
  205.1 12.7 %copy-start.6 = (bf16[1536]{0:T(1024)(128)(2,1)S(1)}, bf16[1536]{0:T(1024)(128)(2,1)}, u32[]{:S(2)}) copy-start(bf16[1536]{0:T(1024)(128)(2,1)} %param.17) | copy-start | bytes 9220
  205.2 12.5 %collective-permute-start.4 = (bf16[160,1536]{1,0:T(8,128)(2,1)S(1)}, bf16[160,1536]{1,0:T(8,128)(2,1)S(1)}, u32[]{:S(2)}, u32[]{:S(2)}) collective-permute-start(bf16[160,1536]{1,0:T(8,128)(2,1)S(1)} %get-tuple-element.12), channel_id=1, source_target_pairs={{0,2},{1,3},{2,0},{3,1},{4,6},{5,7},{6,4},{7,5},{8,10},{9,11},{10,... | collective-permute-start | bytes 1474568 | tf_op jit(solution)/shard_map/ppermute | solution.py:101
  217.7 2.6 collective-permute-start.5
  222.5 114.6 %reduce-scatter.8.cloned.1.call-start = ((), (), s32[]{:S(2)}) async-start(), calls=%async_computation.4 | async-start | bytes 6553600 | tf_op jit(solution)/shard_map/reduce_scatter | solution.py:236
  237.8 157.5 %all-gather.2.cloned.1.call-start = ((), (), s32[]{:S(2)}) async-start(), calls=%async_computation.5 | async-start | bytes 3276800 | tf_op jit(solution)/shard_map/all_gather | solution.py:249
  402.6 2.6 collective-permute-start.6
  405.6 13.3 %collective-permute-start.7 = (bf16[160,1536]{1,0:T(8,128)(2,1)S(1)}, bf16[160,1536]{1,0:T(8,128)(2,1)S(1)}, u32[]{:S(2)}, u32[]{:S(2)}) collective-permute-start(bf16[160,1536]{1,0:T(8,128)(2,1)S(1)} %dynamic-slice_convert_fusion.2), channel_id=1, source_target_pairs={{0,2},{1,3},{2,0},{3,1},{4,6},{5,7},{6,4},{7,5},{8,10},{9,11},{10,... | collective-permute-start | bytes 1474568 | tf_op jit(solution)/shard_map/ppermute | solution.py:101
  419.1 12.5 %collective-permute-start.8 = (bf16[160,1536]{1,0:T(8,128)(2,1)S(1)}, bf16[160,1536]{1,0:T(8,128)(2,1)S(1)}, u32[]{:S(2)}, u32[]{:S(2)}) collective-permute-start(bf16[160,1536]{1,0:T(8,128)(2,1)S(1)} %get-tuple-element.8), channel_id=1, source_target_pairs={{0,2},{1,3},{2,0},{3,1},{4,6},{5,7},{6,4},{7,5},{8,10},{9,11},{10,... | collective-permute-start | bytes 1474568 | tf_op jit(solution)/shard_map/ppermute | solution.py:101
  431.6 2.6 collective-permute-start.9
  431.8 2.5 copy-start.8
  431.8 2.5 copy-start.9
  434.4 2.7 copy-start.1
Sparse Core Ops, SparseCore 0:
  69.4 113.0 reduce-scatter.5
  222.6 20.0 reduce-scatter.9
  245.0 91.9 reduce-scatter.7
  340.1 55.2 all-gather.1

commit v9 on v8

--- a/solution.py
+++ b/solution.py
@@ -232,11 +232,12 @@
     small = jnp.concatenate(
         [logit_part, square_part[:, None], jnp.zeros((capacity, pad), jnp.float32)], axis=1
     )
-    both_sum, small_sum = (
-        lax.psum_scatter(part.astype(jnp.bfloat16), "wide", scatter_dimension=0, tiled=True)
-        .astype(jnp.float32)
-        for part in (both_part, small)
-    )
+    both_sum = lax.psum_scatter(
+        both_part.astype(jnp.bfloat16), "wide", scatter_dimension=0, tiled=True
+    ).astype(jnp.float32)
+    small_sum = lax.dynamic_slice_in_dim(
+        sum_rows(small, "wide"), wide_index * chunk, chunk, 0
+    ).astype(jnp.float32)
     gate_sum = both_sum[:, :hidden_local]
     up_sum = both_sum[:, hidden_local:]
     logit_sum = small_sum[:, :experts]

time: 444 us -> 442 us (level)
  waiting for transfers between devices: 335 us -> 326 us
  starting transfers between devices: 11.9 us -> 17.4 us
    reduce_scatter x1, waiting for transfers between devices: 93.4 us -> 63.1 us  [local(): lax.psum_scatter(both_part.astype(jnp.bfloat16), 'wide', scatter_dimensio...]
    ppermute x9 -> x13, waiting for transfers between devices: 58 us -> 83.6 us  [pair_exchange(): return lax.ppermute(x, axis, perm=[(i, i ^ bit) for i in range(count)])]
    ppermute x9 -> x13, starting transfers between devices: 6.43 us -> 12 us  [pair_exchange(): return lax.ppermute(x, axis, perm=[(i, i ^ bit) for i in range(count)])]
  transfers between devices with their start and end apart: 14 -> 17, of which waited for: 14 -> 17; matrix products, arithmetic and copies ran while one was open for 4% -> 1% of each run, Pallas kernels for 0% -> 0%
where the time goes in v9:
time: 442 us
  waiting for transfers between devices  326 us (74%)
  matrix products  44.1 us (10%)
  Pallas kernels  23.4 us (5%)
  starting transfers between devices  17.4 us (4%)
  between operations  13.6 us (3%)
  local copies, waits for them, and re-layouts  10 us (2%)
  other arithmetic  7.57 us (2%)
    reduce_scatter x1, waiting for transfers between devices, local(): lax.psum_scatter(partial_out.astype(jnp.bfloat16), 'wide', scatter_dimens...  112 us
    ppermute x13, waiting for transfers between devices, pair_exchange(): return lax.ppermute(x, axis, perm=[(i, i ^ bit) for i in range(count)])  83.6 us
    reduce_scatter x1, waiting for transfers between devices, local(): lax.psum_scatter(both_part.astype(jnp.bfloat16), 'wide', scatter_dimensio...  63.1 us
    all_gather x1, waiting for transfers between devices, local(): hidden = lax.all_gather(hidden_chunk, 'wide', axis=0, tiled=True)  55.4 us
    pallas_call x1, Pallas kernels, attend(): pl.pallas_call(kernel, grid_spec=grid_spec, out_shape=jax.ShapeDtypeStruc...  23.4 us
    dot_general x1, matrix products, local(): jnp.dot(attended, out_weight, preferred_element_type=jnp.float32)  15.8 us
    dot_general x1, matrix products, local(): jnp.dot(scaled, jnp.concatenate([gate_weight, up_weight], axis=1), prefer...  15.3 us
    ppermute x13, starting transfers between devices, pair_exchange(): return lax.ppermute(x, axis, perm=[(i, i ^ bit) for i in range(count)])  12 us
  transfers between devices with their start and end apart: 17, of which 17 were waited for; matrix products, arithmetic and copies ran while one was open for 1% of the time, Pallas kernels for 0%

profile of v9, /device:TPU:0, one launch (start us, length us, event | category | flops | bytes accessed | tf_op | source)
XLA Modules:
  0.0 441.6 jit_solution(672975145378556149)
XLA Ops:
  7.9 4.9 %collective-permute-start = (bf16[512,512]{1,0:T(8,128)(2,1)S(1)}, bf16[512,512]{1,0:T(8,128)(2,1)S(1)}, u32[]{:S(2)}, u32[]{:S(2)}) collective-permute-start(bf16[512,512]{1,0:T(8,128)(2,1)S(1)} %get-tuple-element.13), channel_id=1, source_target_pairs={{0,2},{1,3},{4,6},{5,7},{8,10},{9,11},{12,14},{13,15},{16,18},{17,... | collective-permute-start | bytes 1572872 | tf_op jit(solution)/shard_map/ppermute | solution.py:128
  12.8 11.1 %collective-permute-done = bf16[512,512]{1,0:T(8,128)(2,1)S(1)} collective-permute-done((bf16[512,512]{1,0:T(8,128)(2,1)S(1)}, bf16[512,512]{1,0:T(8,128)(2,1)S(1)}, u32[]{:S(2)}, u32[]{:S(2)}) %collective-permute-start) | collective-permute-done | bytes 524320 | tf_op jit(solution)/shard_map/ppermute | solution.py:128
  25.0 3.0 collective-permute-done.1
  30.1 23.4 %shard_map.118 = bf16[512,1536]{1,0:T(8,128)(2,1)S(1)} custom-call(s32[1]{0:T(128)} %bitcast.offset_ref, bf16[512,1536]{1,0:T(8,128)(2,1)S(1)} %copy-done.1, bf16[2048,512]{1,0:T(8,128)(2,1)S(1)} %slice_dynamic-update-slice_fusion.k_ref.v_ref, bf16[2048,512]{1,0:T(8,128)(2,1)S(1)} %slice_dynamic-update-slice_fusion.k_ref.v_ref), custom_call_target="tpu_custom_call" | custom-call | tf_op jit(solution)/shard_map/pallas_call | solution.py:91
  53.5 15.8 %convolution_convert_fusion = bf16[512,6144]{1,0:T(8,128)(2,1)} fusion(bf16[512,1536]{1,0:T(8,128)(2,1)S(1)} %shard_map.118, bf16[1536,6144]{1,0:T(8,128)(2,1)} %param.16), kind=kOutput, calls=%fused_computation.4 | convolution fusion | flops 9666822144 | bytes 26738688 | tf_op jit(solution)/shard_map/dot_general | solution.py:203
  70.2 112.3 %reduce-scatter.3.cloned.1.call-done = bf16[512,1536]{1,0:T(8,128)(2,1)} async-done(((bf16[512,6144]{1,0:T(8,128)(2,1)}), bf16[512,1536]{1,0:T(8,128)(2,1)}) %reduce-scatter.3.cloned.1.call-update) | async-done | bytes 1572880 | tf_op jit(solution)/shard_map/reduce_scatter | solution.py:204
  182.5 2.7 fusion.16
  185.2 1.9 copy-done.2
  187.3 2.5 collective-permute-done.2
  189.8 1.8 convert_add_fusion.1
  191.7 1.5 collective-permute-start.3
  193.2 11.8 %collective-permute-done.3 = bf16[160,1536]{1,0:T(8,128)(2,1)S(1)} collective-permute-done((bf16[160,1536]{1,0:T(8,128)(2,1)S(1)}, bf16[160,1536]{1,0:T(8,128)(2,1)S(1)}, u32[]{:S(2)}, u32[]{:S(2)}) %collective-permute-start.3) | collective-permute-done | bytes 491552 | tf_op jit(solution)/shard_map/ppermute | solution.py:101
  205.2 1.5 collective-permute-start.4
  206.8 10.9 %collective-permute-done.4 = bf16[160,1536]{1,0:T(8,128)(2,1)S(1)} collective-permute-done((bf16[160,1536]{1,0:T(8,128)(2,1)S(1)}, bf16[160,1536]{1,0:T(8,128)(2,1)S(1)}, u32[]{:S(2)}, u32[]{:S(2)}) %collective-permute-start.4) | collective-permute-done | bytes 491552 | tf_op jit(solution)/shard_map/ppermute | solution.py:101
  218.1 2.3 collective-permute-done.5
  220.5 15.3 %fusion.4 = bf16[640,4096]{1,0:T(8,128)(2,1)} fusion(bf16[1536,2048]{1,0:T(8,128)(2,1)} %param.20, bf16[1536,2048]{1,0:T(8,128)(2,1)} %param.19, bf16[640,1536]{1,0:T(8,128)(2,1)S(1)} %constant_dynamic-update-slice_fusion.4, f32[1536]{0:T(1024)S(1)} %convert_element_type.97), kind=kOutput, calls=%fused_computation.5 | convolution fusion | flops 8083800064 | bytes 19798016 | tf_op jit(solution)/shard_map/dot_general | solution.py:223
  237.5 1.6 collective-permute-start.6
  239.0 3.3 collective-permute-done.6
  242.6 3.0 collective-permute-start.7
  245.6 8.2 %collective-permute-done.7 = bf16[160,128]{0,1:T(8,128)(2,1)S(1)} collective-permute-done((bf16[160,128]{0,1:T(8,128)(2,1)S(1)}, bf16[160,128]{0,1:T(8,128)(2,1)S(1)}, u32[]{:S(2)}, u32[]{:S(2)}) %collective-permute-start.7) | collective-permute-done | bytes 40992 | tf_op jit(solution)/shard_map/ppermute | solution.py:101
  254.6 8.1 %collective-permute-done.8 = bf16[160,128]{0,1:T(8,128)(2,1)S(1)} collective-permute-done((bf16[160,128]{0,1:T(8,128)(2,1)S(1)}, bf16[160,128]{0,1:T(8,128)(2,1)S(1)}, u32[]{:S(2)}, u32[]{:S(2)}) %collective-permute-start.8) | collective-permute-done | bytes 40992 | tf_op jit(solution)/shard_map/ppermute | solution.py:101
  265.3 5.9 %collective-permute-done.9 = bf16[320,128]{0,1:T(8,128)(2,1)S(1)} collective-permute-done((bf16[320,128]{0,1:T(8,128)(2,1)S(1)}, bf16[320,128]{0,1:T(8,128)(2,1)S(1)}, u32[]{:S(2)}, u32[]{:S(2)}) %collective-permute-start.9) | collective-permute-done | bytes 81952 | tf_op jit(solution)/shard_map/ppermute | solution.py:101
  272.1 63.1 %reduce-scatter.5.cloned.1.call-done = bf16[160,4096]{1,0:T(8,128)(2,1)} async-done(((bf16[640,4096]{1,0:T(8,128)(2,1)}), bf16[160,4096]{1,0:T(8,128)(2,1)}) %reduce-scatter.5.cloned.1.call-update) | async-done | bytes 1310736 | tf_op jit(solution)/shard_map/reduce_scatter | solution.py:235
  335.2 1.6 convert_element_type.100
  338.1 55.4 %all-gather.2.cloned.1.call-done = bf16[640,2048]{1,0:T(8,128)(2,1)} async-done(((bf16[160,2048]{1,0:T(8,128)(2,1)}), bf16[640,2048]{1,0:T(8,128)(2,1)}) %all-gather.2.cloned.1.call-update) | async-done | bytes 2621456 | tf_op jit(solution)/shard_map/all_gather | solution.py:250
  393.5 7.1 %fusion.25 = f32[640,1536]{1,0:T(8,128)S(1)} fusion(bf16[640,2048]{1,0:T(8,128)(2,1)} %all-gather.2.cloned.1.call-done, bf16[2048,1536]{1,0:T(8,128)(2,1)} %param.21), kind=kOutput, calls=%fused_computation.70 | convolution fusion | flops 4026531840 | bytes 12845056 | tf_op jit(solution)/shard_map/dot_general | solution.py:251
  400.8 2.6 collective-permute-done.10
  403.7 1.5 collective-permute-start.11
  405.2 11.8 %collective-permute-done.11 = bf16[160,1536]{1,0:T(8,128)(2,1)S(1)} collective-permute-done((bf16[160,1536]{1,0:T(8,128)(2,1)S(1)}, bf16[160,1536]{1,0:T(8,128)(2,1)S(1)}, u32[]{:S(2)}, u32[]{:S(2)}) %collective-permute-start.11) | collective-permute-done | bytes 491552 | tf_op jit(solution)/shard_map/ppermute | solution.py:101
  418.7 10.9 %collective-permute-done.12 = bf16[160,1536]{1,0:T(8,128)(2,1)S(1)} collective-permute-done((bf16[160,1536]{1,0:T(8,128)(2,1)S(1)}, bf16[160,1536]{1,0:T(8,128)(2,1)S(1)}, u32[]{:S(2)}, u32[]{:S(2)}) %collective-permute-start.12) | collective-permute-done | bytes 491552 | tf_op jit(solution)/shard_map/ppermute | solution.py:101
  430.0 2.3 collective-permute-done.13
  432.5 2.7 fusion.9
  (82 shorter events, 16.2 us)
Async XLA Ops:
  6.5 230.1 %copy-start = (bf16[1536,8]{0,1:T(8,128)(2,1)S(1)}, bf16[1536,8]{0,1:T(8,128)(2,1)}, u32[]{:S(2)}) copy-start(bf16[1536,8]{0,1:T(8,128)(2,1)} %param.18) | copy-start | bytes 73732
  6.5 175.9 %reduce-scatter.3.cloned.1.call-start = ((), (), s32[]{:S(2)}) async-start(), calls=%async_computation.2 | async-start | bytes 7864320 | tf_op jit(solution)/shard_map/reduce_scatter | solution.py:204
  7.9 16.0 %collective-permute-start = (bf16[512,512]{1,0:T(8,128)(2,1)S(1)}, bf16[512,512]{1,0:T(8,128)(2,1)S(1)}, u32[]{:S(2)}, u32[]{:S(2)}) collective-permute-start(bf16[512,512]{1,0:T(8,128)(2,1)S(1)} %get-tuple-element.13), channel_id=1, source_target_pairs={{0,2},{1,3},{4,6},{5,7},{8,10},{9,11},{12,14},{13,15},{16,18},{17,... | collective-permute-start | bytes 1572872 | tf_op jit(solution)/shard_map/ppermute | solution.py:128
  25.0 3.0 collective-permute-start.1
  25.0 5.2 %copy-start.1 = (bf16[512,1536]{1,0:T(8,128)(2,1)S(1)}, bf16[512,1536]{1,0:T(8,128)(2,1)}, u32[]{:S(2)}) copy-start(bf16[512,1536]{1,0:T(8,128)(2,1)} %q_ref.1) | copy-start | bytes 4718596
  69.3 0.7 copy-start.3
  69.3 0.7 copy-start.4
  69.3 113.2 %copy-start.6 = (bf16[512,1536]{1,0:T(8,128)(2,1)S(1)}, bf16[512,1536]{1,0:T(8,128)(2,1)}, u32[]{:S(2)}) copy-start(bf16[512,1536]{1,0:T(8,128)(2,1)} %param.15) | copy-start | bytes 4718596
  69.3 265.9 %reduce-scatter.5.cloned.1.call-start = ((), (), s32[]{:S(2)}) async-start(), calls=%async_computation.3 | async-start | bytes 6553600 | tf_op jit(solution)/shard_map/reduce_scatter | solution.py:235
  185.2 1.9 copy-start.2
  187.2 2.6 collective-permute-start.2
  191.7 13.3 %collective-permute-start.3 = (bf16[160,1536]{1,0:T(8,128)(2,1)S(1)}, bf16[160,1536]{1,0:T(8,128)(2,1)S(1)}, u32[]{:S(2)}, u32[]{:S(2)}) collective-permute-start(bf16[160,1536]{1,0:T(8,128)(2,1)S(1)} %dynamic-slice_convert_fusion.3), channel_id=1, source_target_pairs={{0,2},{1,3},{2,0},{3,1},{4,6},{5,7},{6,4},{7,5},{8,10},{9,11},{10,... | collective-permute-start | bytes 1474568 | tf_op jit(solution)/shard_map/ppermute | solution.py:101
  205.1 12.7 %copy-start.5 = (bf16[1536]{0:T(1024)(128)(2,1)S(1)}, bf16[1536]{0:T(1024)(128)(2,1)}, u32[]{:S(2)}) copy-start(bf16[1536]{0:T(1024)(128)(2,1)} %param.17) | copy-start | bytes 9220
  205.2 12.5 %collective-permute-start.4 = (bf16[160,1536]{1,0:T(8,128)(2,1)S(1)}, bf16[160,1536]{1,0:T(8,128)(2,1)S(1)}, u32[]{:S(2)}, u32[]{:S(2)}) collective-permute-start(bf16[160,1536]{1,0:T(8,128)(2,1)S(1)} %get-tuple-element.12), channel_id=1, source_target_pairs={{0,2},{1,3},{2,0},{3,1},{4,6},{5,7},{6,4},{7,5},{8,10},{9,11},{10,... | collective-permute-start | bytes 1474568 | tf_op jit(solution)/shard_map/ppermute | solution.py:101
  217.7 2.6 collective-permute-start.5
  235.8 157.7 %all-gather.2.cloned.1.call-start = ((), (), s32[]{:S(2)}) async-start(), calls=%async_computation.4 | async-start | bytes 3276800 | tf_op jit(solution)/shard_map/all_gather | solution.py:250
  237.5 4.9 %collective-permute-start.6 = (bf16[320,128]{0,1:T(8,128)(2,1)S(1)}, bf16[320,128]{0,1:T(8,128)(2,1)S(1)}, u32[]{:S(2)}, u32[]{:S(2)}) collective-permute-start(bf16[320,128]{0,1:T(8,128)(2,1)S(1)} %dynamic-slice_convert_fusion.4), channel_id=1, source_target_pairs={{0,4},{4,0},{8,12},{12,8},{1,5},{5,1},{9,13},{13,9},{2,6},{6,2},{1... | collective-permute-start | bytes 245768 | tf_op jit(solution)/shard_map/ppermute | solution.py:101
  242.6 11.3 %collective-permute-start.7 = (bf16[160,128]{0,1:T(8,128)(2,1)S(1)}, bf16[160,128]{0,1:T(8,128)(2,1)S(1)}, u32[]{:S(2)}, u32[]{:S(2)}) collective-permute-start(bf16[160,128]{0,1:T(8,128)(2,1)S(1)} %dynamic-slice_convert_fusion.5), channel_id=1, source_target_pairs={{0,8},{4,12},{8,0},{12,4},{1,9},{5,13},{9,1},{13,5},{2,10},{6,14},... | collective-permute-start | bytes 122888 | tf_op jit(solution)/shard_map/ppermute | solution.py:101
  254.0 8.7 %collective-permute-start.8 = (bf16[160,128]{0,1:T(8,128)(2,1)S(1)}, bf16[160,128]{0,1:T(8,128)(2,1)S(1)}, u32[]{:S(2)}, u32[]{:S(2)}) collective-permute-start(bf16[160,128]{0,1:T(8,128)(2,1)S(1)} %add_convert_fusion.4), channel_id=1, source_target_pairs={{0,8},{4,12},{8,0},{12,4},{1,9},{5,13},{9,1},{13,5},{2,10},{6,14},... | collective-permute-start | bytes 122888 | tf_op jit(solution)/shard_map/ppermute | solution.py:101
  263.3 7.8 %collective-permute-start.9 = (bf16[320,128]{0,1:T(8,128)(2,1)S(1)}, bf16[320,128]{0,1:T(8,128)(2,1)S(1)}, u32[]{:S(2)}, u32[]{:S(2)}) collective-permute-start(bf16[320,128]{0,1:T(8,128)(2,1)S(1)} %dynamic_update_slice.57), channel_id=1, source_target_pairs={{0,4},{4,0},{8,12},{12,8},{1,5},{5,1},{9,13},{13,9},{2,6},{6,2},{1... | collective-permute-start | bytes 245768 | tf_op jit(solution)/shard_map/ppermute | solution.py:101
  400.7 2.6 collective-permute-start.10
  403.7 13.3 %collective-permute-start.11 = (bf16[160,1536]{1,0:T(8,128)(2,1)S(1)}, bf16[160,1536]{1,0:T(8,128)(2,1)S(1)}, u32[]{:S(2)}, u32[]{:S(2)}) collective-permute-start(bf16[160,1536]{1,0:T(8,128)(2,1)S(1)} %dynamic-slice_convert_fusion.2), channel_id=1, source_target_pairs={{0,2},{1,3},{2,0},{3,1},{4,6},{5,7},{6,4},{7,5},{8,10},{9,11},{10,... | collective-permute-start | bytes 1474568 | tf_op jit(solution)/shard_map/ppermute | solution.py:101
  417.2 12.5 %collective-permute-start.12 = (bf16[160,1536]{1,0:T(8,128)(2,1)S(1)}, bf16[160,1536]{1,0:T(8,128)(2,1)S(1)}, u32[]{:S(2)}, u32[]{:S(2)}) collective-permute-start(bf16[160,1536]{1,0:T(8,128)(2,1)S(1)} %get-tuple-element.8), channel_id=1, source_target_pairs={{0,2},{1,3},{2,0},{3,1},{4,6},{5,7},{6,4},{7,5},{8,10},{9,11},{10,... | collective-permute-start | bytes 1474568 | tf_op jit(solution)/shard_map/ppermute | solution.py:101
  429.7 2.6 collective-permute-start.13
  429.9 2.5 copy-start.7
  429.9 2.5 copy-start.8
Sparse Core Ops, SparseCore 0:
  69.4 113.0 reduce-scatter.2
  235.9 99.2 reduce-scatter.4
  338.2 55.1 all-gather.1

commit v10 on v9

--- a/solution.py
+++ b/solution.py
@@ -52,15 +52,12 @@
     values = v_ref[...]
     for head in range(per_shared):
         query = q_ref[:, head * HEAD_SIZE : (head + 1) * HEAD_SIZE]
-        scores = (
-            lax.dot_general(
-                query, keys, (((1,), (1,)), ((), ())), preferred_element_type=jnp.float32
-            )
-            * scale
+        scores = lax.dot_general(
+            query, keys, (((1,), (1,)), ((), ())), preferred_element_type=jnp.float32
         )
         masked = jnp.where(allowed, scores, NEG_FILL)
         row_max = jnp.max(masked, axis=1, keepdims=True)
-        weights = jnp.exp(masked - row_max)
+        weights = jnp.exp((masked - row_max) * scale)
         total = jnp.sum(weights, axis=1, keepdims=True)
         acc = jnp.dot(weights.astype(jnp.bfloat16), values, preferred_element_type=jnp.float32)
         o_ref[:, head * HEAD_SIZE : (head + 1) * HEAD_SIZE] = (acc / total).astype(o_ref.dtype)
@@ -147,7 +144,7 @@
     index = lax.axis_index(axis)
     acc = x.astype(jnp.float32)
     bit = 1
-    while bit < count:
+    while bit < count // 2:
         half = acc.shape[0] // 2
         upper = (index // bit) % 2
         keep = lax.dynamic_slice_in_dim(acc, upper * half, half, 0)
@@ -155,8 +152,15 @@
         other = pair_exchange(send.astype(jnp.bfloat16), axis, count, bit)
         acc = keep + other.astype(jnp.float32)
         bit *= 2
+    if bit < count:
+        mine = acc.astype(jnp.bfloat16)
+        other = pair_exchange(mine, axis, count, bit)
+        upper = (index // bit) % 2
+        low = jnp.where(upper == 0, mine, other).astype(jnp.float32)
+        high = jnp.where(upper == 0, other, mine).astype(jnp.float32)
+        acc = low + high
     out = acc.astype(jnp.bfloat16)
-    bit = count // 2
+    bit = count // 4
     while bit >= 1:
         other = pair_exchange(out, axis, count, bit)
         upper = (index // bit) % 2

time: 442 us -> 441 us (level)
    ppermute x13 -> x10, starting transfers between devices: 12 us -> 8.02 us  [pair_exchange(): return lax.ppermute(x, axis, perm=[(i, i ^ bit) for i in range(count)])]
    ppermute x13 -> x10, waiting for transfers between devices: 83.6 us -> 84.4 us  [pair_exchange(): return lax.ppermute(x, axis, perm=[(i, i ^ bit) for i in range(count)])]
  transfers between devices with their start and end apart: 17 -> 14, of which waited for: 17 -> 14; matrix products, arithmetic and copies ran while one was open for 1% -> 1% of each run, Pallas kernels for 0% -> 0%
where the time goes in v10:
time: 441 us
  waiting for transfers between devices  327 us (74%)
  matrix products  44.1 us (10%)
  Pallas kernels  25.2 us (6%)
  between operations  13.5 us (3%)
  starting transfers between devices  13.4 us (3%)
  other arithmetic  9.39 us (2%)
  local copies, waits for them, and re-layouts  8.28 us (2%)
    reduce_scatter x1, waiting for transfers between devices, local(): lax.psum_scatter(partial_out.astype(jnp.bfloat16), 'wide', scatter_dimens...  112 us
    ppermute x10, waiting for transfers between devices, pair_exchange(): return lax.ppermute(x, axis, perm=[(i, i ^ bit) for i in range(count)])  84.4 us
    reduce_scatter x1, waiting for transfers between devices, local(): lax.psum_scatter(both_part.astype(jnp.bfloat16), 'wide', scatter_dimensio...  63.7 us
    all_gather x1, waiting for transfers between devices, local(): hidden = lax.all_gather(hidden_chunk, 'wide', axis=0, tiled=True)  55.4 us
    pallas_call x1, Pallas kernels, attend(): pl.pallas_call(kernel, grid_spec=grid_spec, out_shape=jax.ShapeDtypeStruc...  25.2 us
    dot_general x1, matrix products, local(): jnp.dot(attended, out_weight, preferred_element_type=jnp.float32)  15.8 us
    dot_general x1, matrix products, local(): jnp.dot(scaled, jnp.concatenate([gate_weight, up_weight], axis=1), prefer...  15.3 us
    ppermute x1, waiting for transfers between devices, gather_causal(): lower = lax.ppermute(x, axis, perm=[(0, 2), (1, 3)])  11.1 us
  transfers between devices with their start and end apart: 14, of which 14 were waited for; matrix products, arithmetic and copies ran while one was open for 1% of the time, Pallas kernels for 0%

profile of v10, /device:TPU:0, one launch (start us, length us, event | category | flops | bytes accessed | tf_op | source)
XLA Modules:
  0.0 440.8 jit_solution(11944107157425518000)
XLA Ops:
  6.5 1.1 constant_dynamic-slice_fusion
  7.9 4.9 %collective-permute-start = (bf16[512,512]{1,0:T(8,128)(2,1)S(1)}, bf16[512,512]{1,0:T(8,128)(2,1)S(1)}, u32[]{:S(2)}, u32[]{:S(2)}) collective-permute-start(bf16[512,512]{1,0:T(8,128)(2,1)S(1)} %get-tuple-element.13), channel_id=1, source_target_pairs={{0,2},{1,3},{4,6},{5,7},{8,10},{9,11},{12,14},{13,15},{16,18},{17,... | collective-permute-start | bytes 1572872 | tf_op jit(solution)/shard_map/ppermute | solution.py:125
  12.8 11.1 %collective-permute-done = bf16[512,512]{1,0:T(8,128)(2,1)S(1)} collective-permute-done((bf16[512,512]{1,0:T(8,128)(2,1)S(1)}, bf16[512,512]{1,0:T(8,128)(2,1)S(1)}, u32[]{:S(2)}, u32[]{:S(2)}) %collective-permute-start) | collective-permute-done | bytes 524320 | tf_op jit(solution)/shard_map/ppermute | solution.py:125
  25.0 3.0 collective-permute-done.1
  29.0 1.1 slice_dynamic-update-slice_fusion.k_ref.v_ref
  30.1 25.2 %shard_map.118 = bf16[512,1536]{1,0:T(8,128)(2,1)S(1)} custom-call(s32[1]{0:T(128)} %bitcast.offset_ref, bf16[512,1536]{1,0:T(8,128)(2,1)S(1)} %copy-done.1, bf16[2048,512]{1,0:T(8,128)(2,1)S(1)} %slice_dynamic-update-slice_fusion.k_ref.v_ref, bf16[2048,512]{1,0:T(8,128)(2,1)S(1)} %slice_dynamic-update-slice_fusion.k_ref.v_ref), custom_call_target="tpu_custom_call" | custom-call | tf_op jit(solution)/shard_map/pallas_call | solution.py:88
  55.3 15.8 %convolution_convert_fusion = bf16[512,6144]{1,0:T(8,128)(2,1)} fusion(bf16[512,1536]{1,0:T(8,128)(2,1)S(1)} %shard_map.118, bf16[1536,6144]{1,0:T(8,128)(2,1)} %param.16), kind=kOutput, calls=%fused_computation.4 | convolution fusion | flops 9666822144 | bytes 26738688 | tf_op jit(solution)/shard_map/dot_general | solution.py:207
  72.0 112.3 %reduce-scatter.3.cloned.1.call-done = bf16[512,1536]{1,0:T(8,128)(2,1)} async-done(((bf16[512,6144]{1,0:T(8,128)(2,1)}), bf16[512,1536]{1,0:T(8,128)(2,1)}) %reduce-scatter.3.cloned.1.call-update) | async-done | bytes 1572880 | tf_op jit(solution)/shard_map/reduce_scatter | solution.py:208
  184.3 2.7 fusion.16
  187.0 1.9 copy-done.2
  189.1 2.5 collective-permute-done.2
  191.6 1.8 add_convert_fusion.4
  193.5 1.5 collective-permute-start.3
  195.0 22.4 %collective-permute-done.3 = bf16[320,1536]{1,0:T(8,128)(2,1)} collective-permute-done((bf16[320,1536]{1,0:T(8,128)(2,1)S(1)}, bf16[320,1536]{1,0:T(8,128)(2,1)}, u32[]{:S(2)}, u32[]{:S(2)}) %collective-permute-start.3) | collective-permute-done | bytes 983072 | tf_op jit(solution)/shard_map/ppermute | solution.py:98
  217.6 1.6 constant_dynamic-update-slice_fusion.3
  219.3 2.5 collective-permute-done.4
  222.0 15.3 %fusion.4 = bf16[640,4096]{1,0:T(8,128)(2,1)} fusion(bf16[1536,2048]{1,0:T(8,128)(2,1)} %param.20, bf16[1536,2048]{1,0:T(8,128)(2,1)} %param.19, bf16[640,1536]{1,0:T(8,128)(2,1)S(1)} %constant_dynamic-update-slice_fusion.2, f32[1536]{0:T(1024)S(1)} %convert_element_type.107), kind=kOutput, calls=%fused_computation.5 | convolution fusion | flops 8083800064 | bytes 19798016 | tf_op jit(solution)/shard_map/dot_general | solution.py:227
  238.9 1.6 collective-permute-start.5
  240.5 3.3 collective-permute-done.5
  244.0 3.0 collective-permute-start.6
  247.0 13.9 %collective-permute-done.6 = bf16[320,128]{0,1:T(8,128)(2,1)S(1)} collective-permute-done((bf16[320,128]{0,1:T(8,128)(2,1)S(1)}, bf16[320,128]{0,1:T(8,128)(2,1)S(1)}, u32[]{:S(2)}, u32[]{:S(2)}) %collective-permute-start.6) | collective-permute-done | bytes 81952 | tf_op jit(solution)/shard_map/ppermute | solution.py:98
  262.1 9.3 %collective-permute-done.7 = bf16[320,128]{0,1:T(8,128)(2,1)S(1)} collective-permute-done((bf16[320,128]{0,1:T(8,128)(2,1)S(1)}, bf16[320,128]{0,1:T(8,128)(2,1)S(1)}, u32[]{:S(2)}, u32[]{:S(2)}) %collective-permute-start.7) | collective-permute-done | bytes 81952 | tf_op jit(solution)/shard_map/ppermute | solution.py:98
  272.3 63.7 %reduce-scatter.5.cloned.1.call-done = bf16[160,4096]{1,0:T(8,128)(2,1)} async-done(((bf16[640,4096]{1,0:T(8,128)(2,1)}), bf16[160,4096]{1,0:T(8,128)(2,1)}) %reduce-scatter.5.cloned.1.call-update) | async-done | bytes 1310736 | tf_op jit(solution)/shard_map/reduce_scatter | solution.py:239
  335.9 1.6 convert_element_type.110
  337.5 1.3 fusion.15
  338.9 55.4 %all-gather.2.cloned.1.call-done = bf16[640,2048]{1,0:T(8,128)(2,1)} async-done(((bf16[160,2048]{1,0:T(8,128)(2,1)}), bf16[640,2048]{1,0:T(8,128)(2,1)}) %all-gather.2.cloned.1.call-update) | async-done | bytes 2621456 | tf_op jit(solution)/shard_map/all_gather | solution.py:254
  394.3 7.1 %fusion.25 = f32[640,1536]{1,0:T(8,128)S(1)} fusion(bf16[640,2048]{1,0:T(8,128)(2,1)} %all-gather.2.cloned.1.call-done, bf16[2048,1536]{1,0:T(8,128)(2,1)} %param.21), kind=kOutput, calls=%fused_computation.63 | convolution fusion | flops 4026531840 | bytes 12845056 | tf_op jit(solution)/shard_map/dot_general | solution.py:255
  401.6 2.6 collective-permute-done.8
  404.5 1.5 collective-permute-start.9
  406.0 22.3 %collective-permute-done.9 = bf16[320,1536]{1,0:T(8,128)(2,1)S(1)} collective-permute-done((bf16[320,1536]{1,0:T(8,128)(2,1)S(1)}, bf16[320,1536]{1,0:T(8,128)(2,1)S(1)}, u32[]{:S(2)}, u32[]{:S(2)}) %collective-permute-start.9) | collective-permute-done | bytes 983072 | tf_op jit(solution)/shard_map/ppermute | solution.py:98
  429.0 2.6 collective-permute-done.10
  431.6 2.7 fusion.9
  (64 shorter events, 8.7 us)
Async XLA Ops:
  6.5 231.6 %copy-start = (bf16[1536,8]{0,1:T(8,128)(2,1)S(1)}, bf16[1536,8]{0,1:T(8,128)(2,1)}, u32[]{:S(2)}) copy-start(bf16[1536,8]{0,1:T(8,128)(2,1)} %param.18) | copy-start | bytes 73732
  6.5 177.7 %reduce-scatter.3.cloned.1.call-start = ((), (), s32[]{:S(2)}) async-start(), calls=%async_computation.2 | async-start | bytes 7864320 | tf_op jit(solution)/shard_map/reduce_scatter | solution.py:208
  7.9 16.0 %collective-permute-start = (bf16[512,512]{1,0:T(8,128)(2,1)S(1)}, bf16[512,512]{1,0:T(8,128)(2,1)S(1)}, u32[]{:S(2)}, u32[]{:S(2)}) collective-permute-start(bf16[512,512]{1,0:T(8,128)(2,1)S(1)} %get-tuple-element.13), channel_id=1, source_target_pairs={{0,2},{1,3},{4,6},{5,7},{8,10},{9,11},{12,14},{13,15},{16,18},{17,... | collective-permute-start | bytes 1572872 | tf_op jit(solution)/shard_map/ppermute | solution.py:125
  25.0 3.0 collective-permute-start.1
  25.0 5.2 %copy-start.1 = (bf16[512,1536]{1,0:T(8,128)(2,1)S(1)}, bf16[512,1536]{1,0:T(8,128)(2,1)}, u32[]{:S(2)}) copy-start(bf16[512,1536]{1,0:T(8,128)(2,1)} %q_ref.1) | copy-start | bytes 4718596
  71.1 0.7 copy-start.3
  71.1 0.7 copy-start.4
  71.1 113.2 %copy-start.6 = (bf16[512,1536]{1,0:T(8,128)(2,1)S(1)}, bf16[512,1536]{1,0:T(8,128)(2,1)}, u32[]{:S(2)}) copy-start(bf16[512,1536]{1,0:T(8,128)(2,1)} %param.15) | copy-start | bytes 4718596
  71.1 264.8 %reduce-scatter.5.cloned.1.call-start = ((), (), s32[]{:S(2)}) async-start(), calls=%async_computation.3 | async-start | bytes 6553600 | tf_op jit(solution)/shard_map/reduce_scatter | solution.py:239
  187.0 1.9 copy-start.2
  189.0 2.6 collective-permute-start.2
  193.5 24.0 %collective-permute-start.3 = (bf16[320,1536]{1,0:T(8,128)(2,1)S(1)}, bf16[320,1536]{1,0:T(8,128)(2,1)}, u32[]{:S(2)}, u32[]{:S(2)}) collective-permute-start(bf16[320,1536]{1,0:T(8,128)(2,1)S(1)} %add_convert_fusion.4), channel_id=1, source_target_pairs={{0,2},{1,3},{2,0},{3,1},{4,6},{5,7},{6,4},{7,5},{8,10},{9,11},{10,... | collective-permute-start | bytes 2949128 | tf_op jit(solution)/shard_map/ppermute | solution.py:98
  217.6 1.7 copy-start.5
  219.2 2.6 collective-permute-start.4
  237.3 157.0 %all-gather.2.cloned.1.call-start = ((), (), s32[]{:S(2)}) async-start(), calls=%async_computation.4 | async-start | bytes 3276800 | tf_op jit(solution)/shard_map/all_gather | solution.py:254
  238.9 4.9 %collective-permute-start.5 = (bf16[320,128]{0,1:T(8,128)(2,1)S(1)}, bf16[320,128]{0,1:T(8,128)(2,1)S(1)}, u32[]{:S(2)}, u32[]{:S(2)}) collective-permute-start(bf16[320,128]{0,1:T(8,128)(2,1)S(1)} %dynamic-slice_convert_fusion.2), channel_id=1, source_target_pairs={{0,4},{4,0},{8,12},{12,8},{1,5},{5,1},{9,13},{13,9},{2,6},{6,2},{1... | collective-permute-start | bytes 245768 | tf_op jit(solution)/shard_map/ppermute | solution.py:98
  244.0 16.9 %collective-permute-start.6 = (bf16[320,128]{0,1:T(8,128)(2,1)S(1)}, bf16[320,128]{0,1:T(8,128)(2,1)S(1)}, u32[]{:S(2)}, u32[]{:S(2)}) collective-permute-start(bf16[320,128]{0,1:T(8,128)(2,1)S(1)} %add_convert_fusion.7), channel_id=1, source_target_pairs={{0,8},{4,12},{8,0},{12,4},{1,9},{5,13},{9,1},{13,5},{2,10},{6,14},... | collective-permute-start | bytes 245768 | tf_op jit(solution)/shard_map/ppermute | solution.py:98
  260.9 10.4 %collective-permute-start.7 = (bf16[320,128]{0,1:T(8,128)(2,1)S(1)}, bf16[320,128]{0,1:T(8,128)(2,1)S(1)}, u32[]{:S(2)}, u32[]{:S(2)}) collective-permute-start(bf16[320,128]{0,1:T(8,128)(2,1)S(1)} %add_convert_fusion.6), channel_id=1, source_target_pairs={{0,4},{4,0},{8,12},{12,8},{1,5},{5,1},{9,13},{13,9},{2,6},{6,2},{1... | collective-permute-start | bytes 245768 | tf_op jit(solution)/shard_map/ppermute | solution.py:98
  401.5 2.6 collective-permute-start.8
  404.5 23.9 %collective-permute-start.9 = (bf16[320,1536]{1,0:T(8,128)(2,1)S(1)}, bf16[320,1536]{1,0:T(8,128)(2,1)S(1)}, u32[]{:S(2)}, u32[]{:S(2)}) collective-permute-start(bf16[320,1536]{1,0:T(8,128)(2,1)S(1)} %add_convert_fusion.2), channel_id=1, source_target_pairs={{0,2},{1,3},{2,0},{3,1},{4,6},{5,7},{6,4},{7,5},{8,10},{9,11},{10,... | collective-permute-start | bytes 2949128 | tf_op jit(solution)/shard_map/ppermute | solution.py:98
  428.5 3.1 copy-start.8
  428.9 2.7 copy-start.7
  428.9 2.6 collective-permute-start.10
Sparse Core Ops, SparseCore 0:
  71.2 113.0 reduce-scatter.2
  237.4 98.5 reduce-scatter.4
  339.0 55.2 all-gather.1

commit v11 on v10

--- a/solution.py
+++ b/solution.py
@@ -52,12 +52,15 @@
     values = v_ref[...]
     for head in range(per_shared):
         query = q_ref[:, head * HEAD_SIZE : (head + 1) * HEAD_SIZE]
-        scores = lax.dot_general(
-            query, keys, (((1,), (1,)), ((), ())), preferred_element_type=jnp.float32
+        scores = (
+            lax.dot_general(
+                query, keys, (((1,), (1,)), ((), ())), preferred_element_type=jnp.float32
+            )
+            * scale
         )
         masked = jnp.where(allowed, scores, NEG_FILL)
         row_max = jnp.max(masked, axis=1, keepdims=True)
-        weights = jnp.exp((masked - row_max) * scale)
+        weights = jnp.exp(masked - row_max)
         total = jnp.sum(weights, axis=1, keepdims=True)
         acc = jnp.dot(weights.astype(jnp.bfloat16), values, preferred_element_type=jnp.float32)
         o_ref[:, head * HEAD_SIZE : (head + 1) * HEAD_SIZE] = (acc / total).astype(o_ref.dtype)
@@ -251,11 +254,41 @@
         jnp.where(chunk_slots[:, None] == slot_of_token[None, :], partner[None, :], 0), axis=1
     )
     hidden_chunk = expert_hidden(gate_sum, up_sum, square_sum, logit_sum, other_chunk, D)
-    hidden = lax.all_gather(hidden_chunk, "wide", axis=0, tiled=True)
-    expert_part = jnp.dot(hidden, down_weight, preferred_element_type=jnp.float32)
-    expert_sum = sum_rows(expert_part, "ctx")
-    pick = (slot_local[:, None] == slot_ids_all[None, :]).astype(jnp.bfloat16)
-    moe_rows = jnp.dot(pick, expert_sum, preferred_element_type=jnp.float32)
+    if wide_count > 4:
+        hidden = lax.all_gather(hidden_chunk, "wide", axis=0, tiled=True)
+        expert_part = jnp.dot(hidden, down_weight, preferred_element_type=jnp.float32)
+        expert_sum = sum_rows(expert_part, "ctx")
+        pick = (slot_local[:, None] == slot_ids_all[None, :]).astype(jnp.bfloat16)
+        moe_rows = jnp.dot(pick, expert_sum, preferred_element_type=jnp.float32)
+        return (resid.astype(jnp.float32) + moe_rows).astype(jnp.bfloat16)
+    moe_rows = jnp.zeros((rows_local, width_local), jnp.float32)
+
+    def settle(moe_rows, hidden_rows, owners):
+        expert_part = jnp.dot(hidden_rows, down_weight, preferred_element_type=jnp.float32)
+        expert_sum = sum_rows(expert_part, "ctx")
+        for place_at, owner in enumerate(owners):
+            ids = owner * chunk + jnp.arange(chunk, dtype=jnp.int32)
+            valid = jnp.logical_and(owner >= 0, owner < wide_count)
+            pick = jnp.logical_and(slot_local[:, None] == ids[None, :], valid)
+            block = expert_sum[place_at * chunk : (place_at + 1) * chunk]
+            moe_rows = moe_rows + jnp.dot(
+                pick.astype(jnp.bfloat16), block, preferred_element_type=jnp.float32
+            )
+        return moe_rows
+
+    moe_rows = settle(moe_rows, hidden_chunk, (wide_index,))
+    rightward = [(i, i + 1) for i in range(wide_count - 1)]
+    leftward = [(i + 1, i) for i in range(wide_count - 1)]
+    from_left = hidden_chunk
+    from_right = hidden_chunk
+    for step in range(1, wide_count):
+        from_left = lax.ppermute(from_left, "wide", perm=rightward)
+        from_right = lax.ppermute(from_right, "wide", perm=leftward)
+        moe_rows = settle(
+            moe_rows,
+            jnp.concatenate([from_left, from_right], axis=0),
+            (wide_index - step, wide_index + step),
+        )
     return (resid.astype(jnp.float32) + moe_rows).astype(jnp.bfloat16)
 
 

time: 441 us -> 449 us (1.018)
  waiting for transfers between devices: 327 us -> 297 us
  starting transfers between devices: 13.4 us -> 34.9 us
  matrix products: 44.1 us -> 56.6 us
    all_gather x1 -> x0, waiting for transfers between devices: 55.4 us -> none  [local(): hidden = lax.all_gather(hidden_chunk, 'wide', axis=0, tiled=True)]
    ppermute x0 -> x6, waiting for transfers between devices: none -> 37.8 us  [the longest x3 34.2 us: local(): from_right = lax.ppermute(from_right, 'wide', perm=leftward)]
    ppermute x0 -> x6, starting transfers between devices: none -> 18.8 us  [the longest x3 14.9 us: local(): from_left = lax.ppermute(from_left, 'wide', perm=rightward)]
    dot_general x2 -> x11, matrix products: 9.77 us -> 22.6 us  [the longest x4 16.4 us: settle(): jnp.dot(hidden_rows, down_weight, preferred_element_type=jnp.float32)]
    ppermute x10 -> x19, waiting for transfers between devices: 84.4 us -> 71.8 us  [pair_exchange(): return lax.ppermute(x, axis, perm=[(i, i ^ bit) for i in range(count)])]
    ppermute x10 -> x19, starting transfers between devices: 8.02 us -> 10.9 us  [pair_exchange(): return lax.ppermute(x, axis, perm=[(i, i ^ bit) for i in range(count)])]
  transfers between devices with their start and end apart: 14 -> 28, of which waited for: 14 -> 21; matrix products, arithmetic and copies ran while one was open for 1% -> 5% of each run, Pallas kernels for 0% -> 0%
where the time goes in v11:
time: 449 us; the launch traced here: 448 us
  waiting for transfers between devices  297 us (66%)
  matrix products  56.6 us (13%)
  starting transfers between devices  34.9 us (8%)
  Pallas kernels  23.4 us (5%)
  between operations  14.1 us (3%)
  local copies, waits for them, and re-layouts  11.3 us (3%)
  other arithmetic  10.9 us (2%)
    reduce_scatter x1, waiting for transfers between devices, local(): lax.psum_scatter(partial_out.astype(jnp.bfloat16), 'wide', scatter_dimens...  112 us
    ppermute x19, waiting for transfers between devices, pair_exchange(): return lax.ppermute(x, axis, perm=[(i, i ^ bit) for i in range(count)])  71.8 us
    reduce_scatter x1, waiting for transfers between devices, local(): lax.psum_scatter(both_part.astype(jnp.bfloat16), 'wide', scatter_dimensio...  64 us
    ppermute x3, waiting for transfers between devices, local(): from_right = lax.ppermute(from_right, 'wide', perm=leftward)  34.2 us
    pallas_call x1, Pallas kernels, attend(): pl.pallas_call(kernel, grid_spec=grid_spec, out_shape=jax.ShapeDtypeStruc...  23.4 us
    dot_general x4, matrix products, settle(): jnp.dot(hidden_rows, down_weight, preferred_element_type=jnp.float32)  16.4 us
    dot_general x1, matrix products, local(): jnp.dot(attended, out_weight, preferred_element_type=jnp.float32)  15.5 us
    dot_general x1, matrix products, local(): jnp.dot(scaled, jnp.concatenate([gate_weight, up_weight], axis=1), prefer...  15.2 us
  transfers between devices with their start and end apart: 28, of which 21 were waited for; matrix products, arithmetic and copies ran while one was open for 5% of the time, Pallas kernels for 0%

profile of v11, /device:TPU:0, one launch (start us, length us, event | category | flops | bytes accessed | tf_op | source)
XLA Modules:
  0.0 448.3 jit_solution(3179896866774143526)
XLA Ops:
  7.9 4.9 %collective-permute-start = (bf16[512,512]{1,0:T(8,128)(2,1)S(1)}, bf16[512,512]{1,0:T(8,128)(2,1)S(1)}, u32[]{:S(2)}, u32[]{:S(2)}) collective-permute-start(bf16[512,512]{1,0:T(8,128)(2,1)S(1)} %get-tuple-element.19), channel_id=1, source_target_pairs={{0,2},{1,3},{4,6},{5,7},{8,10},{9,11},{12,14},{13,15},{16,18},{17,... | collective-permute-start | bytes 1572872 | tf_op jit(solution)/shard_map/ppermute | solution.py:128
  12.8 11.1 %collective-permute-done = bf16[512,512]{1,0:T(8,128)(2,1)S(1)} collective-permute-done((bf16[512,512]{1,0:T(8,128)(2,1)S(1)}, bf16[512,512]{1,0:T(8,128)(2,1)S(1)}, u32[]{:S(2)}, u32[]{:S(2)}) %collective-permute-start) | collective-permute-done | bytes 524320 | tf_op jit(solution)/shard_map/ppermute | solution.py:128
  25.0 3.0 collective-permute-done.1
  30.1 23.4 %shard_map.118 = bf16[512,1536]{1,0:T(8,128)(2,1)S(1)} custom-call(s32[1]{0:T(128)} %bitcast.offset_ref, bf16[512,1536]{1,0:T(8,128)(2,1)S(1)} %copy-done.2, bf16[2048,512]{1,0:T(8,128)(2,1)S(1)} %slice_dynamic-update-slice_fusion.k_ref.v_ref, bf16[2048,512]{1,0:T(8,128)(2,1)S(1)} %slice_dynamic-update-slice_fusion.k_ref.v_ref), custom_call_target="tpu_custom_call" | custom-call | tf_op jit(solution)/shard_map/pallas_call | solution.py:91
  53.5 15.5 %convolution_convert_fusion = bf16[512,6144]{1,0:T(8,128)(2,1)} fusion(bf16[512,1536]{1,0:T(8,128)(2,1)S(1)} %shard_map.118, bf16[1536,6144]{1,0:T(8,128)(2,1)} %param.16), kind=kOutput, calls=%fused_computation.4 | convolution fusion | flops 9666822144 | bytes 26738688 | tf_op jit(solution)/shard_map/dot_general | solution.py:210
  69.9 112.3 %reduce-scatter.3.cloned.1.call-done = bf16[512,1536]{1,0:T(8,128)(2,1)} async-done(((bf16[512,6144]{1,0:T(8,128)(2,1)}), bf16[512,1536]{1,0:T(8,128)(2,1)}) %reduce-scatter.3.cloned.1.call-update) | async-done | bytes 1572880 | tf_op jit(solution)/shard_map/reduce_scatter | solution.py:211
  182.2 2.7 fusion.34
  184.9 1.9 copy-done.3
  187.0 2.5 collective-permute-done.2
  189.6 1.8 add_convert_fusion.2
  192.9 22.4 %collective-permute-done.3 = bf16[320,1536]{1,0:T(8,128)(2,1)} collective-permute-done((bf16[320,1536]{1,0:T(8,128)(2,1)S(1)}, bf16[320,1536]{1,0:T(8,128)(2,1)}, u32[]{:S(2)}, u32[]{:S(2)}) %collective-permute-start.3) | collective-permute-done | bytes 983072 | tf_op jit(solution)/shard_map/ppermute | solution.py:101
  215.5 1.6 constant_dynamic-update-slice_fusion.9
  217.2 2.5 collective-permute-done.4
  219.8 15.2 %fusion.4 = bf16[640,4096]{1,0:T(8,128)(2,1)} fusion(bf16[1536,2048]{1,0:T(8,128)(2,1)} %param.20, bf16[1536,2048]{1,0:T(8,128)(2,1)} %param.19, bf16[640,1536]{1,0:T(8,128)(2,1)S(1)} %constant_dynamic-update-slice_fusion.8, f32[1536]{0:T(1024)S(1)} %convert_element_type.167), kind=kOutput, calls=%fused_computation.5 | convolution fusion | flops 8083800064 | bytes 19798016 | tf_op jit(solution)/shard_map/dot_general | solution.py:230
  238.0 3.3 collective-permute-done.5
  241.5 3.0 collective-permute-start.6
  244.5 13.9 %collective-permute-done.6 = bf16[320,128]{0,1:T(8,128)(2,1)S(1)} collective-permute-done((bf16[320,128]{0,1:T(8,128)(2,1)S(1)}, bf16[320,128]{0,1:T(8,128)(2,1)S(1)}, u32[]{:S(2)}, u32[]{:S(2)}) %collective-permute-start.6) | collective-permute-done | bytes 81952 | tf_op jit(solution)/shard_map/ppermute | solution.py:101
  259.8 9.0 %collective-permute-done.7 = bf16[320,128]{0,1:T(8,128)(2,1)S(1)} collective-permute-done((bf16[320,128]{0,1:T(8,128)(2,1)S(1)}, bf16[320,128]{0,1:T(8,128)(2,1)S(1)}, u32[]{:S(2)}, u32[]{:S(2)}) %collective-permute-start.7) | collective-permute-done | bytes 81952 | tf_op jit(solution)/shard_map/ppermute | solution.py:101
  269.8 64.0 %reduce-scatter.5.cloned.1.call-done = bf16[160,4096]{1,0:T(8,128)(2,1)} async-done(((bf16[640,4096]{1,0:T(8,128)(2,1)}), bf16[160,4096]{1,0:T(8,128)(2,1)}) %reduce-scatter.5.cloned.1.call-update) | async-done | bytes 1310736 | tf_op jit(solution)/shard_map/reduce_scatter | solution.py:242
  333.7 1.6 convert_element_type.170
  335.8 4.0 fusion.92
  344.3 4.6 %collective-permute-start.11 = (bf16[160,2048]{1,0:T(8,128)(2,1)S(1)}, bf16[160,2048]{1,0:T(8,128)(2,1)S(1)}, u32[]{:S(2)}, u32[]{:S(2)}) collective-permute-start(bf16[160,2048]{1,0:T(8,128)(2,1)S(1)} %fusion.21), channel_id=1, source_target_pairs={{0,4},{4,8},{8,12},{1,5},{5,9},{9,13},{2,6},{6,10},{10,14},{3,7},{... | collective-permute-start | bytes 1966088 | tf_op jit(solution)/shard_map/ppermute | solution.py:285
  350.4 11.0 %collective-permute-done.12 = bf16[160,2048]{1,0:T(8,128)(2,1)S(1)} collective-permute-done((bf16[160,2048]{1,0:T(8,128)(2,1)S(1)}, bf16[160,2048]{1,0:T(8,128)(2,1)S(1)}, u32[]{:S(2)}, u32[]{:S(2)}) %collective-permute-start.12) | collective-permute-done | bytes 655392 | tf_op jit(solution)/shard_map/ppermute | solution.py:286
  362.6 5.2 %fusion.22 = f32[320,1536]{1,0:T(8,128)S(1)} fusion(bf16[2048,1536]{1,0:T(8,128)(2,1)} %param.21, bf16[160,2048]{1,0:T(8,128)(2,1)S(1)} %collective-permute-done.12, bf16[160,2048]{1,0:T(8,128)(2,1)S(1)} %collective-permute-done.11), kind=kOutput, calls=%fused_computation.28 | convolution fusion | flops 2015887360 | bytes 9568256 | tf_op jit(solution)/shard_map/dot_general | solution.py:267
  370.8 5.1 %collective-permute-start.16 = (bf16[160,2048]{1,0:T(8,128)(2,1)}, bf16[160,2048]{1,0:T(8,128)(2,1)S(1)}, u32[]{:S(2)}, u32[]{:S(2)}) collective-permute-start(bf16[160,2048]{1,0:T(8,128)(2,1)} %copy-done.12), channel_id=1, source_target_pairs={{0,4},{4,8},{8,12},{1,5},{5,9},{9,13},{2,6},{6,10},{10,14},{3,7},{... | collective-permute-start | bytes 1966088 | tf_op jit(solution)/shard_map/ppermute | solution.py:285
  378.0 11.3 %collective-permute-done.17 = bf16[160,2048]{1,0:T(8,128)(2,1)S(1)} collective-permute-done((bf16[160,2048]{1,0:T(8,128)(2,1)}, bf16[160,2048]{1,0:T(8,128)(2,1)S(1)}, u32[]{:S(2)}, u32[]{:S(2)}) %collective-permute-start.17) | collective-permute-done | bytes 655392 | tf_op jit(solution)/shard_map/ppermute | solution.py:286
  390.5 5.0 %fusion.26 = f32[320,1536]{1,0:T(8,128)S(1)} fusion(bf16[2048,1536]{1,0:T(8,128)(2,1)} %param.21, bf16[160,2048]{1,0:T(8,128)(2,1)S(1)} %collective-permute-done.17, bf16[160,2048]{1,0:T(8,128)(2,1)S(1)} %collective-permute-done.16), kind=kOutput, calls=%fused_computation.32 | convolution fusion | flops 2015887360 | bytes 9568256 | tf_op jit(solution)/shard_map/dot_general | solution.py:267
  397.0 5.2 %collective-permute-start.21 = (bf16[160,2048]{1,0:T(8,128)(2,1)S(1)}, bf16[160,2048]{1,0:T(8,128)(2,1)S(1)}, u32[]{:S(2)}, u32[]{:S(2)}) collective-permute-start(bf16[160,2048]{1,0:T(8,128)(2,1)S(1)} %collective-permute-done.16), channel_id=1, source_target_pairs={{0,4},{4,8},{8,12},{1,5},{5,9},{9,13},{2,6},{6,10},{10,14},{3,7},{... | collective-permute-start | bytes 1966088 | tf_op jit(solution)/shard_map/ppermute | solution.py:285
  403.5 11.8 %collective-permute-done.22 = bf16[160,2048]{1,0:T(8,128)(2,1)S(1)} collective-permute-done((bf16[160,2048]{1,0:T(8,128)(2,1)S(1)}, bf16[160,2048]{1,0:T(8,128)(2,1)S(1)}, u32[]{:S(2)}, u32[]{:S(2)}) %collective-permute-start.22) | collective-permute-done | bytes 655392 | tf_op jit(solution)/shard_map/ppermute | solution.py:286
  416.5 2.2 fusion.30
  422.1 12.0 %collective-permute-done.24 = bf16[160,1536]{1,0:T(8,128)(2,1)S(1)} collective-permute-done((bf16[160,1536]{1,0:T(8,128)(2,1)S(1)}, bf16[160,1536]{1,0:T(8,128)(2,1)S(1)}, u32[]{:S(2)}, u32[]{:S(2)}) %collective-permute-start.24) | collective-permute-done | bytes 491552 | tf_op jit(solution)/shard_map/ppermute | solution.py:101
  438.9 2.6 fusion.15
  (134 shorter events, 38.4 us)
Async XLA Ops:
  6.5 229.1 %copy-start = (bf16[1536,8]{0,1:T(8,128)(2,1)S(1)}, bf16[1536,8]{0,1:T(8,128)(2,1)}, u32[]{:S(2)}) copy-start(bf16[1536,8]{0,1:T(8,128)(2,1)} %param.18) | copy-start | bytes 73732
  6.5 175.7 %reduce-scatter.3.cloned.1.call-start = ((), (), s32[]{:S(2)}) async-start(), calls=%async_computation.2 | async-start | bytes 7864320 | tf_op jit(solution)/shard_map/reduce_scatter | solution.py:211
  7.9 16.0 %collective-permute-start = (bf16[512,512]{1,0:T(8,128)(2,1)S(1)}, bf16[512,512]{1,0:T(8,128)(2,1)S(1)}, u32[]{:S(2)}, u32[]{:S(2)}) collective-permute-start(bf16[512,512]{1,0:T(8,128)(2,1)S(1)} %get-tuple-element.19), channel_id=1, source_target_pairs={{0,2},{1,3},{4,6},{5,7},{8,10},{9,11},{12,14},{13,15},{16,18},{17,... | collective-permute-start | bytes 1572872 | tf_op jit(solution)/shard_map/ppermute | solution.py:128
  25.0 3.0 collective-permute-start.1
  69.0 113.2 %copy-start.4 = (bf16[512,1536]{1,0:T(8,128)(2,1)S(1)}, bf16[512,1536]{1,0:T(8,128)(2,1)}, u32[]{:S(2)}) copy-start(bf16[512,1536]{1,0:T(8,128)(2,1)} %param.15) | copy-start | bytes 4718596
  69.0 264.7 %reduce-scatter.5.cloned.1.call-start = ((), (), s32[]{:S(2)}) async-start(), calls=%async_computation.3 | async-start | bytes 6553600 | tf_op jit(solution)/shard_map/reduce_scatter | solution.py:242
  186.9 2.6 collective-permute-start.2
  191.4 24.0 %collective-permute-start.3 = (bf16[320,1536]{1,0:T(8,128)(2,1)S(1)}, bf16[320,1536]{1,0:T(8,128)(2,1)}, u32[]{:S(2)}, u32[]{:S(2)}) collective-permute-start(bf16[320,1536]{1,0:T(8,128)(2,1)S(1)} %add_convert_fusion.2), channel_id=1, source_target_pairs={{0,2},{1,3},{2,0},{3,1},{4,6},{5,7},{6,4},{7,5},{8,10},{9,11},{10,... | collective-permute-start | bytes 2949128 | tf_op jit(solution)/shard_map/ppermute | solution.py:101
  217.1 2.6 collective-permute-start.4
  236.5 4.9 %collective-permute-start.5 = (bf16[320,128]{0,1:T(8,128)(2,1)S(1)}, bf16[320,128]{0,1:T(8,128)(2,1)S(1)}, u32[]{:S(2)}, u32[]{:S(2)}) collective-permute-start(bf16[320,128]{0,1:T(8,128)(2,1)S(1)} %dynamic-slice_convert_fusion.5), channel_id=1, source_target_pairs={{0,4},{4,0},{8,12},{12,8},{1,5},{5,1},{9,13},{13,9},{2,6},{6,2},{1... | collective-permute-start | bytes 245768 | tf_op jit(solution)/shard_map/ppermute | solution.py:101
  241.5 16.9 %collective-permute-start.6 = (bf16[320,128]{0,1:T(8,128)(2,1)S(1)}, bf16[320,128]{0,1:T(8,128)(2,1)S(1)}, u32[]{:S(2)}, u32[]{:S(2)}) collective-permute-start(bf16[320,128]{0,1:T(8,128)(2,1)S(1)} %add_convert_fusion.13), channel_id=1, source_target_pairs={{0,8},{4,12},{8,0},{12,4},{1,9},{5,13},{9,1},{13,5},{2,10},{6,14},... | collective-permute-start | bytes 245768 | tf_op jit(solution)/shard_map/ppermute | solution.py:101
  258.4 10.4 %collective-permute-start.7 = (bf16[320,128]{0,1:T(8,128)(2,1)S(1)}, bf16[320,128]{0,1:T(8,128)(2,1)S(1)}, u32[]{:S(2)}, u32[]{:S(2)}) collective-permute-start(bf16[320,128]{0,1:T(8,128)(2,1)S(1)} %add_convert_fusion.12), channel_id=1, source_target_pairs={{0,4},{4,0},{8,12},{12,8},{1,5},{5,1},{9,13},{13,9},{2,6},{6,2},{1... | collective-permute-start | bytes 245768 | tf_op jit(solution)/shard_map/ppermute | solution.py:101
  339.9 1.6 collective-permute-start.8
  341.5 8.1 %collective-permute-start.9 = (bf16[80,1536]{1,0:T(8,128)(2,1)S(1)}, bf16[80,1536]{1,0:T(8,128)(2,1)S(1)}, u32[]{:S(2)}, u32[]{:S(2)}) collective-permute-start(bf16[80,1536]{1,0:T(8,128)(2,1)S(1)} %add_convert_fusion.11), channel_id=1, source_target_pairs={{0,2},{1,3},{2,0},{3,1},{4,6},{5,7},{6,4},{7,5},{8,10},{9,11},{10,... | collective-permute-start | bytes 737288 | tf_op jit(solution)/shard_map/ppermute | solution.py:101
  343.0 18.4 %collective-permute-start.12 = (bf16[160,2048]{1,0:T(8,128)(2,1)S(1)}, bf16[160,2048]{1,0:T(8,128)(2,1)S(1)}, u32[]{:S(2)}, u32[]{:S(2)}) collective-permute-start(bf16[160,2048]{1,0:T(8,128)(2,1)S(1)} %fusion.21), channel_id=1, source_target_pairs={{4,0},{8,4},{12,8},{5,1},{9,5},{13,9},{6,2},{10,6},{14,10},{7,3},{... | collective-permute-start | bytes 1966088 | tf_op jit(solution)/shard_map/ppermute | solution.py:286
  344.3 18.3 %collective-permute-start.11 = (bf16[160,2048]{1,0:T(8,128)(2,1)S(1)}, bf16[160,2048]{1,0:T(8,128)(2,1)S(1)}, u32[]{:S(2)}, u32[]{:S(2)}) collective-permute-start(bf16[160,2048]{1,0:T(8,128)(2,1)S(1)} %fusion.21), channel_id=1, source_target_pairs={{0,4},{4,8},{8,12},{1,5},{5,9},{9,13},{2,6},{6,10},{10,14},{3,7},{... | collective-permute-start | bytes 1966088 | tf_op jit(solution)/shard_map/ppermute | solution.py:285
  350.4 25.5 %collective-permute-start.10 = (bf16[80,1536]{1,0:T(8,128)(2,1)}, bf16[80,1536]{1,0:T(8,128)(2,1)S(1)}, u32[]{:S(2)}, u32[]{:S(2)}) collective-permute-start(bf16[80,1536]{1,0:T(8,128)(2,1)} %get-tuple-element.8), channel_id=1, source_target_pairs={{0,1},{1,0},{2,3},{3,2},{4,5},{5,4},{6,7},{7,6},{8,9},{9,8},{10,11... | collective-permute-start | bytes 737288 | tf_op jit(solution)/shard_map/ppermute | solution.py:101
  369.1 47.4 %slice-start = ((s8[6291456]{0:T(1024)(128)(4,1)}), s8[2097152]{0:T(1024)(128)(4,1)S(1)}, s32[]{:S(2)}) async-start(s8[6291456]{0:T(1024)(128)(4,1)} %bitcast.13), calls=%async_computation.4 | async-start | bytes 4194304
  369.2 6.7 %collective-permute-start.13 = (bf16[160,1536]{1,0:T(8,128)(2,1)S(1)}, bf16[160,1536]{1,0:T(8,128)(2,1)}, u32[]{:S(2)}, u32[]{:S(2)}) collective-permute-start(bf16[160,1536]{1,0:T(8,128)(2,1)S(1)} %dynamic-slice_convert_fusion.3), channel_id=1, source_target_pairs={{0,1},{1,0},{2,3},{3,2},{4,5},{5,4},{6,7},{7,6},{8,9},{9,8},{10,11... | collective-permute-start | bytes 1474568 | tf_op jit(solution)/shard_map/ppermute | solution.py:101
  369.3 19.9 %collective-permute-start.17 = (bf16[160,2048]{1,0:T(8,128)(2,1)}, bf16[160,2048]{1,0:T(8,128)(2,1)S(1)}, u32[]{:S(2)}, u32[]{:S(2)}) collective-permute-start(bf16[160,2048]{1,0:T(8,128)(2,1)} %copy-done.11), channel_id=1, source_target_pairs={{4,0},{8,4},{12,8},{5,1},{9,5},{13,9},{6,2},{10,6},{14,10},{7,3},{... | collective-permute-start | bytes 1966088 | tf_op jit(solution)/shard_map/ppermute | solution.py:286
  370.8 19.8 %collective-permute-start.16 = (bf16[160,2048]{1,0:T(8,128)(2,1)}, bf16[160,2048]{1,0:T(8,128)(2,1)S(1)}, u32[]{:S(2)}, u32[]{:S(2)}) collective-permute-start(bf16[160,2048]{1,0:T(8,128)(2,1)} %copy-done.12), channel_id=1, source_target_pairs={{0,4},{4,8},{8,12},{1,5},{5,9},{9,13},{2,6},{6,10},{10,14},{3,7},{... | collective-permute-start | bytes 1966088 | tf_op jit(solution)/shard_map/ppermute | solution.py:285
  377.3 39.2 %slice-start.1 = ((s8[6291456]{0:T(1024)(128)(4,1)}), s8[4194304]{0:T(1024)(128)(4,1)S(1)}, s32[]{:S(2)}) async-start(s8[6291456]{0:T(1024)(128)(4,1)} %bitcast.13), calls=%async_computation.5 | async-start | bytes 8388608
  377.3 24.9 %collective-permute-start.14 = (bf16[160,1536]{1,0:T(8,128)(2,1)S(1)}, bf16[160,1536]{1,0:T(8,128)(2,1)S(1)}, u32[]{:S(2)}, u32[]{:S(2)}) collective-permute-start(bf16[160,1536]{1,0:T(8,128)(2,1)S(1)} %add_convert_fusion.8), channel_id=1, source_target_pairs={{0,2},{1,3},{2,0},{3,1},{4,6},{5,7},{6,4},{7,5},{8,10},{9,11},{10,... | collective-permute-start | bytes 1474568 | tf_op jit(solution)/shard_map/ppermute | solution.py:101
  395.6 7.2 %collective-permute-start.18 = (bf16[160,1536]{1,0:T(8,128)(2,1)S(1)}, bf16[160,1536]{1,0:T(8,128)(2,1)S(1)}, u32[]{:S(2)}, u32[]{:S(2)}) collective-permute-start(bf16[160,1536]{1,0:T(8,128)(2,1)S(1)} %dynamic-slice_convert_fusion.2), channel_id=1, source_target_pairs={{0,1},{1,0},{2,3},{3,2},{4,5},{5,4},{6,7},{7,6},{8,9},{9,8},{10,11... | collective-permute-start | bytes 1474568 | tf_op jit(solution)/shard_map/ppermute | solution.py:101
  395.7 19.7 %collective-permute-start.22 = (bf16[160,2048]{1,0:T(8,128)(2,1)S(1)}, bf16[160,2048]{1,0:T(8,128)(2,1)S(1)}, u32[]{:S(2)}, u32[]{:S(2)}) collective-permute-start(bf16[160,2048]{1,0:T(8,128)(2,1)S(1)} %collective-permute-done.17), channel_id=1, source_target_pairs={{4,0},{8,4},{12,8},{5,1},{9,5},{13,9},{6,2},{10,6},{14,10},{7,3},{... | collective-permute-start | bytes 1966088 | tf_op jit(solution)/shard_map/ppermute | solution.py:286
  397.0 19.5 %collective-permute-start.21 = (bf16[160,2048]{1,0:T(8,128)(2,1)S(1)}, bf16[160,2048]{1,0:T(8,128)(2,1)S(1)}, u32[]{:S(2)}, u32[]{:S(2)}) collective-permute-start(bf16[160,2048]{1,0:T(8,128)(2,1)S(1)} %collective-permute-done.16), channel_id=1, source_target_pairs={{0,4},{4,8},{8,12},{1,5},{5,9},{9,13},{2,6},{6,10},{10,14},{3,7},{... | collective-permute-start | bytes 1966088 | tf_op jit(solution)/shard_map/ppermute | solution.py:285
  402.5 16.4 %collective-permute-start.15 = (bf16[160,1536]{1,0:T(8,128)(2,1)S(1)}, bf16[160,1536]{1,0:T(8,128)(2,1)S(1)}, u32[]{:S(2)}, u32[]{:S(2)}) collective-permute-start(bf16[160,1536]{1,0:T(8,128)(2,1)S(1)} %get-tuple-element.10), channel_id=1, source_target_pairs={{0,1},{1,0},{2,3},{3,2},{4,5},{5,4},{6,7},{7,6},{8,9},{9,8},{10,11... | collective-permute-start | bytes 1474568 | tf_op jit(solution)/shard_map/ppermute | solution.py:101
  402.9 16.7 %collective-permute-start.19 = (bf16[160,1536]{1,0:T(8,128)(2,1)S(1)}, bf16[160,1536]{1,0:T(8,128)(2,1)S(1)}, u32[]{:S(2)}, u32[]{:S(2)}) collective-permute-start(bf16[160,1536]{1,0:T(8,128)(2,1)S(1)} %add_convert_fusion.6), channel_id=1, source_target_pairs={{0,2},{1,3},{2,0},{3,1},{4,6},{5,7},{6,4},{7,5},{8,10},{9,11},{10,... | collective-permute-start | bytes 1474568 | tf_op jit(solution)/shard_map/ppermute | solution.py:101
  418.8 1.9 collective-permute-start.23
  419.8 2.2 collective-permute-start.20
  420.8 13.3 %collective-permute-start.24 = (bf16[160,1536]{1,0:T(8,128)(2,1)S(1)}, bf16[160,1536]{1,0:T(8,128)(2,1)S(1)}, u32[]{:S(2)}, u32[]{:S(2)}) collective-permute-start(bf16[160,1536]{1,0:T(8,128)(2,1)S(1)} %add_convert_fusion.4), channel_id=1, source_target_pairs={{0,2},{1,3},{2,0},{3,1},{4,6},{5,7},{6,4},{7,5},{8,10},{9,11},{10,... | collective-permute-start | bytes 1474568 | tf_op jit(solution)/shard_map/ppermute | solution.py:101
  434.4 1.9 collective-permute-start.25
  (11 other events, 23.8 us)
Sparse Core Ops, SparseCore 0:
  69.2 113.0 reduce-scatter.2
  235.2 98.5 reduce-scatter.4

commit v12 on v11

--- a/solution.py
+++ b/solution.py
@@ -261,22 +261,11 @@
         pick = (slot_local[:, None] == slot_ids_all[None, :]).astype(jnp.bfloat16)
         moe_rows = jnp.dot(pick, expert_sum, preferred_element_type=jnp.float32)
         return (resid.astype(jnp.float32) + moe_rows).astype(jnp.bfloat16)
-    moe_rows = jnp.zeros((rows_local, width_local), jnp.float32)
-
-    def settle(moe_rows, hidden_rows, owners):
-        expert_part = jnp.dot(hidden_rows, down_weight, preferred_element_type=jnp.float32)
-        expert_sum = sum_rows(expert_part, "ctx")
-        for place_at, owner in enumerate(owners):
-            ids = owner * chunk + jnp.arange(chunk, dtype=jnp.int32)
-            valid = jnp.logical_and(owner >= 0, owner < wide_count)
-            pick = jnp.logical_and(slot_local[:, None] == ids[None, :], valid)
-            block = expert_sum[place_at * chunk : (place_at + 1) * chunk]
-            moe_rows = moe_rows + jnp.dot(
-                pick.astype(jnp.bfloat16), block, preferred_element_type=jnp.float32
-            )
-        return moe_rows
-
-    moe_rows = settle(moe_rows, hidden_chunk, (wide_index,))
+    span = 3 * wide_count - 2
+    gathered = jnp.zeros((span * chunk, hidden_chunk.shape[1]), hidden_chunk.dtype)
+    gathered = lax.dynamic_update_slice_in_dim(
+        gathered, hidden_chunk, (wide_index + wide_count - 1) * chunk, 0
+    )
     rightward = [(i, i + 1) for i in range(wide_count - 1)]
     leftward = [(i + 1, i) for i in range(wide_count - 1)]
     from_left = hidden_chunk
@@ -284,11 +273,19 @@
     for step in range(1, wide_count):
         from_left = lax.ppermute(from_left, "wide", perm=rightward)
         from_right = lax.ppermute(from_right, "wide", perm=leftward)
-        moe_rows = settle(
-            moe_rows,
-            jnp.concatenate([from_left, from_right], axis=0),
-            (wide_index - step, wide_index + step),
+        gathered = lax.dynamic_update_slice_in_dim(
+            gathered, from_left, (wide_index - step + wide_count - 1) * chunk, 0
         )
+        gathered = lax.dynamic_update_slice_in_dim(
+            gathered, from_right, (wide_index + step + wide_count - 1) * chunk, 0
+        )
+    hidden = lax.slice_in_dim(
+        gathered, (wide_count - 1) * chunk, (2 * wide_count - 1) * chunk, axis=0
+    )
+    expert_part = jnp.dot(hidden, down_weight, preferred_element_type=jnp.float32)
+    expert_sum = sum_rows(expert_part, "ctx")
+    pick = (slot_local[:, None] == slot_ids_all[None, :]).astype(jnp.bfloat16)
+    moe_rows = jnp.dot(pick, expert_sum, preferred_element_type=jnp.float32)
     return (resid.astype(jnp.float32) + moe_rows).astype(jnp.bfloat16)
 
 

time: 449 us -> 445 us (level)
  matrix products: 56.6 us -> 44.1 us
  waiting for transfers between devices: 297 us -> 308 us
  local copies, waits for them, and re-layouts: 11.3 us -> 17.3 us
  starting transfers between devices: 34.9 us -> 29.3 us
    ppermute x3, waiting for transfers between devices: 34.2 us -> 4.13 us  [local(): from_right = lax.ppermute(from_right, 'wide', perm=leftward)]
    ppermute x3, waiting for transfers between devices: 3.64 us -> 32.2 us  [local(): from_left = lax.ppermute(from_left, 'wide', perm=rightward)]
    dot_general x11 -> x2, matrix products: 22.6 us -> 9.77 us  [the longest x1 7.11 us: local(): jnp.dot(hidden, down_weight, preferred_element_type=jnp.float32)]
    ppermute x19 -> x10, waiting for transfers between devices: 71.8 us -> 84.1 us  [pair_exchange(): return lax.ppermute(x, axis, perm=[(i, i ^ bit) for i in range(count)])]
    dynamic_update_slice x0 -> x6, local copies, waits for them, and re-layouts: none -> 5.37 us  [the longest x3 2.69 us: local(): lax.dynamic_update_slice_in_dim(gathered, from_left, (wide_index - step +...]
    ppermute x19 -> x10, starting transfers between devices: 10.9 us -> 8.01 us  [pair_exchange(): return lax.ppermute(x, axis, perm=[(i, i ^ bit) for i in range(count)])]
  transfers between devices with their start and end apart: 28 -> 19, of which waited for: 21 -> 17; matrix products, arithmetic and copies ran while one was open for 5% -> 2% of each run, Pallas kernels for 0% -> 0%
where the time goes in v12:
time: 445 us; the launch traced here: 444 us
  waiting for transfers between devices  308 us (69%)
  matrix products  44.1 us (10%)
  starting transfers between devices  29.3 us (7%)
  Pallas kernels  23.4 us (5%)
  local copies, waits for them, and re-layouts  17.3 us (4%)
  between operations  13.9 us (3%)
  other arithmetic  8.56 us (2%)
    reduce_scatter x1, waiting for transfers between devices, local(): lax.psum_scatter(partial_out.astype(jnp.bfloat16), 'wide', scatter_dimens...  112 us
    ppermute x10, waiting for transfers between devices, pair_exchange(): return lax.ppermute(x, axis, perm=[(i, i ^ bit) for i in range(count)])  84.1 us
    reduce_scatter x1, waiting for transfers between devices, local(): lax.psum_scatter(both_part.astype(jnp.bfloat16), 'wide', scatter_dimensio...  64 us
    ppermute x3, waiting for transfers between devices, local(): from_left = lax.ppermute(from_left, 'wide', perm=rightward)  32.2 us
    pallas_call x1, Pallas kernels, attend(): pl.pallas_call(kernel, grid_spec=grid_spec, out_shape=jax.ShapeDtypeStruc...  23.4 us
    dot_general x1, matrix products, local(): jnp.dot(attended, out_weight, preferred_element_type=jnp.float32)  15.8 us
    dot_general x1, matrix products, local(): jnp.dot(scaled, jnp.concatenate([gate_weight, up_weight], axis=1), prefer...  15.2 us
    ppermute x3, starting transfers between devices, local(): from_left = lax.ppermute(from_left, 'wide', perm=rightward)  12.3 us
  transfers between devices with their start and end apart: 19, of which 17 were waited for; matrix products, arithmetic and copies ran while one was open for 2% of the time, Pallas kernels for 0%

profile of v12, /device:TPU:0, one launch (start us, length us, event | category | flops | bytes accessed | tf_op | source)
XLA Modules:
  0.0 444.4 jit_solution(3823541488083725724)
XLA Ops:
  7.9 4.9 %collective-permute-start = (bf16[512,512]{1,0:T(8,128)(2,1)S(1)}, bf16[512,512]{1,0:T(8,128)(2,1)S(1)}, u32[]{:S(2)}, u32[]{:S(2)}) collective-permute-start(bf16[512,512]{1,0:T(8,128)(2,1)S(1)} %get-tuple-element.15), channel_id=1, source_target_pairs={{0,2},{1,3},{4,6},{5,7},{8,10},{9,11},{12,14},{13,15},{16,18},{17,... | collective-permute-start | bytes 1572872 | tf_op jit(solution)/shard_map/ppermute | solution.py:128
  12.8 11.1 %collective-permute-done = bf16[512,512]{1,0:T(8,128)(2,1)S(1)} collective-permute-done((bf16[512,512]{1,0:T(8,128)(2,1)S(1)}, bf16[512,512]{1,0:T(8,128)(2,1)S(1)}, u32[]{:S(2)}, u32[]{:S(2)}) %collective-permute-start) | collective-permute-done | bytes 524320 | tf_op jit(solution)/shard_map/ppermute | solution.py:128
  25.0 3.0 collective-permute-done.1
  30.1 23.4 %shard_map.118 = bf16[512,1536]{1,0:T(8,128)(2,1)S(1)} custom-call(s32[1]{0:T(128)} %bitcast.offset_ref, bf16[512,1536]{1,0:T(8,128)(2,1)S(1)} %copy-done.1, bf16[2048,512]{1,0:T(8,128)(2,1)S(1)} %slice_dynamic-update-slice_fusion.k_ref.v_ref, bf16[2048,512]{1,0:T(8,128)(2,1)S(1)} %slice_dynamic-update-slice_fusion.k_ref.v_ref), custom_call_target="tpu_custom_call" | custom-call | tf_op jit(solution)/shard_map/pallas_call | solution.py:91
  53.5 15.8 %convolution_convert_fusion = bf16[512,6144]{1,0:T(8,128)(2,1)} fusion(bf16[512,1536]{1,0:T(8,128)(2,1)S(1)} %shard_map.118, bf16[1536,6144]{1,0:T(8,128)(2,1)} %param.16), kind=kOutput, calls=%fused_computation.4 | convolution fusion | flops 9666822144 | bytes 26738688 | tf_op jit(solution)/shard_map/dot_general | solution.py:210
  70.2 112.3 %reduce-scatter.3.cloned.1.call-done = bf16[512,1536]{1,0:T(8,128)(2,1)} async-done(((bf16[512,6144]{1,0:T(8,128)(2,1)}), bf16[512,1536]{1,0:T(8,128)(2,1)}) %reduce-scatter.3.cloned.1.call-update) | async-done | bytes 1572880 | tf_op jit(solution)/shard_map/reduce_scatter | solution.py:211
  182.5 2.7 fusion.18
  185.2 1.9 copy-done.3
  187.3 2.5 collective-permute-done.2
  189.8 1.8 add_convert_fusion.4
  193.2 22.4 %collective-permute-done.3 = bf16[320,1536]{1,0:T(8,128)(2,1)} collective-permute-done((bf16[320,1536]{1,0:T(8,128)(2,1)S(1)}, bf16[320,1536]{1,0:T(8,128)(2,1)}, u32[]{:S(2)}, u32[]{:S(2)}) %collective-permute-start.3) | collective-permute-done | bytes 983072 | tf_op jit(solution)/shard_map/ppermute | solution.py:101
  215.7 1.6 constant_dynamic-update-slice_fusion.10
  217.5 2.5 collective-permute-done.4
  220.1 15.2 %fusion.4 = bf16[640,4096]{1,0:T(8,128)(2,1)} fusion(bf16[1536,2048]{1,0:T(8,128)(2,1)} %param.20, bf16[1536,2048]{1,0:T(8,128)(2,1)} %param.19, bf16[640,1536]{1,0:T(8,128)(2,1)S(1)} %constant_dynamic-update-slice_fusion.9, f32[1536]{0:T(1024)S(1)} %convert_element_type.107), kind=kOutput, calls=%fused_computation.5 | convolution fusion | flops 8083800064 | bytes 19798016 | tf_op jit(solution)/shard_map/dot_general | solution.py:230
  238.3 3.3 collective-permute-done.5
  241.8 3.0 collective-permute-start.6
  244.8 13.9 %collective-permute-done.6 = bf16[320,128]{0,1:T(8,128)(2,1)S(1)} collective-permute-done((bf16[320,128]{0,1:T(8,128)(2,1)S(1)}, bf16[320,128]{0,1:T(8,128)(2,1)S(1)}, u32[]{:S(2)}, u32[]{:S(2)}) %collective-permute-start.6) | collective-permute-done | bytes 81952 | tf_op jit(solution)/shard_map/ppermute | solution.py:101
  260.1 9.0 %collective-permute-done.7 = bf16[320,128]{0,1:T(8,128)(2,1)S(1)} collective-permute-done((bf16[320,128]{0,1:T(8,128)(2,1)S(1)}, bf16[320,128]{0,1:T(8,128)(2,1)S(1)}, u32[]{:S(2)}, u32[]{:S(2)}) %collective-permute-start.7) | collective-permute-done | bytes 81952 | tf_op jit(solution)/shard_map/ppermute | solution.py:101
  270.0 64.0 %reduce-scatter.5.cloned.1.call-done = bf16[160,4096]{1,0:T(8,128)(2,1)} async-done(((bf16[640,4096]{1,0:T(8,128)(2,1)}), bf16[160,4096]{1,0:T(8,128)(2,1)}) %reduce-scatter.5.cloned.1.call-update) | async-done | bytes 1310736 | tf_op jit(solution)/shard_map/reduce_scatter | solution.py:242
  337.0 2.7 copy-done.2
  339.7 3.4 collective-permute-start.8
  344.4 12.8 %collective-permute-done.8 = bf16[160,2048]{1,0:T(8,128)(2,1)S(1)} collective-permute-done((bf16[160,2048]{1,0:T(8,128)(2,1)S(1)}, bf16[160,2048]{1,0:T(8,128)(2,1)S(1)}, u32[]{:S(2)}, u32[]{:S(2)}) %collective-permute-start.8) | collective-permute-done | bytes 655392 | tf_op jit(solution)/shard_map/ppermute | solution.py:274
  357.2 4.4 collective-permute-start.10
  363.8 11.0 %collective-permute-done.10 = bf16[160,2048]{1,0:T(8,128)(2,1)S(1)} collective-permute-done((bf16[160,2048]{1,0:T(8,128)(2,1)S(1)}, bf16[160,2048]{1,0:T(8,128)(2,1)S(1)}, u32[]{:S(2)}, u32[]{:S(2)}) %collective-permute-start.10) | collective-permute-done | bytes 655392 | tf_op jit(solution)/shard_map/ppermute | solution.py:274
  374.8 4.4 collective-permute-start.12
  383.2 8.4 %collective-permute-done.12 = bf16[160,2048]{1,0:T(8,128)(2,1)S(1)} collective-permute-done((bf16[160,2048]{1,0:T(8,128)(2,1)S(1)}, bf16[160,2048]{1,0:T(8,128)(2,1)S(1)}, u32[]{:S(2)}, u32[]{:S(2)}) %collective-permute-start.12) | collective-permute-done | bytes 655392 | tf_op jit(solution)/shard_map/ppermute | solution.py:274
  392.5 4.1 collective-permute-done.13
  397.6 7.1 %fusion.10 = f32[640,1536]{1,0:T(8,128)S(1)} fusion(bf16[2048,1536]{1,0:T(8,128)(2,1)} %param.21, bf16[1600,2048]{1,0:T(8,128)(2,1)} %constant_dynamic-update-slice_fusion.1), kind=kOutput, calls=%fused_computation.13 | convolution fusion | flops 4026531840 | bytes 12845056 | tf_op jit(solution)/shard_map/dot_general | solution.py:285
  404.9 2.6 collective-permute-done.14
  409.3 22.3 %collective-permute-done.15 = bf16[320,1536]{1,0:T(8,128)(2,1)S(1)} collective-permute-done((bf16[320,1536]{1,0:T(8,128)(2,1)S(1)}, bf16[320,1536]{1,0:T(8,128)(2,1)S(1)}, u32[]{:S(2)}, u32[]{:S(2)}) %collective-permute-start.15) | collective-permute-done | bytes 983072 | tf_op jit(solution)/shard_map/ppermute | solution.py:101
  432.2 2.6 collective-permute-done.16
  434.9 2.7 fusion.9
  (82 shorter events, 27.6 us)
Async XLA Ops:
  6.5 229.4 %copy-start = (bf16[1536,8]{0,1:T(8,128)(2,1)S(1)}, bf16[1536,8]{0,1:T(8,128)(2,1)}, u32[]{:S(2)}) copy-start(bf16[1536,8]{0,1:T(8,128)(2,1)} %param.18) | copy-start | bytes 73732
  6.5 176.0 %reduce-scatter.3.cloned.1.call-start = ((), (), s32[]{:S(2)}) async-start(), calls=%async_computation.2 | async-start | bytes 7864320 | tf_op jit(solution)/shard_map/reduce_scatter | solution.py:211
  7.9 16.0 %collective-permute-start = (bf16[512,512]{1,0:T(8,128)(2,1)S(1)}, bf16[512,512]{1,0:T(8,128)(2,1)S(1)}, u32[]{:S(2)}, u32[]{:S(2)}) collective-permute-start(bf16[512,512]{1,0:T(8,128)(2,1)S(1)} %get-tuple-element.15), channel_id=1, source_target_pairs={{0,2},{1,3},{4,6},{5,7},{8,10},{9,11},{12,14},{13,15},{16,18},{17,... | collective-permute-start | bytes 1572872 | tf_op jit(solution)/shard_map/ppermute | solution.py:128
  25.0 3.0 collective-permute-start.1
  25.0 5.2 %copy-start.1 = (bf16[512,1536]{1,0:T(8,128)(2,1)S(1)}, bf16[512,1536]{1,0:T(8,128)(2,1)}, u32[]{:S(2)}) copy-start(bf16[512,1536]{1,0:T(8,128)(2,1)} %q_ref.1) | copy-start | bytes 4718596
  69.3 0.7 copy-start.4
  69.3 0.7 copy-start.5
  69.3 113.2 %copy-start.7 = (bf16[512,1536]{1,0:T(8,128)(2,1)S(1)}, bf16[512,1536]{1,0:T(8,128)(2,1)}, u32[]{:S(2)}) copy-start(bf16[512,1536]{1,0:T(8,128)(2,1)} %param.15) | copy-start | bytes 4718596
  69.3 264.7 %reduce-scatter.5.cloned.1.call-start = ((), (), s32[]{:S(2)}) async-start(), calls=%async_computation.3 | async-start | bytes 6553600 | tf_op jit(solution)/shard_map/reduce_scatter | solution.py:242
  185.2 1.9 copy-start.3
  187.2 2.6 collective-permute-start.2
  191.6 24.0 %collective-permute-start.3 = (bf16[320,1536]{1,0:T(8,128)(2,1)S(1)}, bf16[320,1536]{1,0:T(8,128)(2,1)}, u32[]{:S(2)}, u32[]{:S(2)}) collective-permute-start(bf16[320,1536]{1,0:T(8,128)(2,1)S(1)} %add_convert_fusion.4), channel_id=1, source_target_pairs={{0,2},{1,3},{2,0},{3,1},{4,6},{5,7},{6,4},{7,5},{8,10},{9,11},{10,... | collective-permute-start | bytes 2949128 | tf_op jit(solution)/shard_map/ppermute | solution.py:101
  215.7 1.7 copy-start.6
  217.4 2.6 collective-permute-start.4
  236.8 4.9 %collective-permute-start.5 = (bf16[320,128]{0,1:T(8,128)(2,1)S(1)}, bf16[320,128]{0,1:T(8,128)(2,1)S(1)}, u32[]{:S(2)}, u32[]{:S(2)}) collective-permute-start(bf16[320,128]{0,1:T(8,128)(2,1)S(1)} %dynamic-slice_convert_fusion.2), channel_id=1, source_target_pairs={{0,4},{4,0},{8,12},{12,8},{1,5},{5,1},{9,13},{13,9},{2,6},{6,2},{1... | collective-permute-start | bytes 245768 | tf_op jit(solution)/shard_map/ppermute | solution.py:101
  241.8 16.9 %collective-permute-start.6 = (bf16[320,128]{0,1:T(8,128)(2,1)S(1)}, bf16[320,128]{0,1:T(8,128)(2,1)S(1)}, u32[]{:S(2)}, u32[]{:S(2)}) collective-permute-start(bf16[320,128]{0,1:T(8,128)(2,1)S(1)} %add_convert_fusion.7), channel_id=1, source_target_pairs={{0,8},{4,12},{8,0},{12,4},{1,9},{5,13},{9,1},{13,5},{2,10},{6,14},... | collective-permute-start | bytes 245768 | tf_op jit(solution)/shard_map/ppermute | solution.py:101
  258.7 10.4 %collective-permute-start.7 = (bf16[320,128]{0,1:T(8,128)(2,1)S(1)}, bf16[320,128]{0,1:T(8,128)(2,1)S(1)}, u32[]{:S(2)}, u32[]{:S(2)}) collective-permute-start(bf16[320,128]{0,1:T(8,128)(2,1)S(1)} %add_convert_fusion.6), channel_id=1, source_target_pairs={{0,4},{4,0},{8,12},{12,8},{1,5},{5,1},{9,13},{13,9},{2,6},{6,2},{1... | collective-permute-start | bytes 245768 | tf_op jit(solution)/shard_map/ppermute | solution.py:101
  336.9 2.7 copy-start.2
  339.7 17.5 %collective-permute-start.8 = (bf16[160,2048]{1,0:T(8,128)(2,1)S(1)}, bf16[160,2048]{1,0:T(8,128)(2,1)S(1)}, u32[]{:S(2)}, u32[]{:S(2)}) collective-permute-start(bf16[160,2048]{1,0:T(8,128)(2,1)S(1)} %get-tuple-element.10), channel_id=1, source_target_pairs={{0,4},{4,8},{8,12},{1,5},{5,9},{9,13},{2,6},{6,10},{10,14},{3,7},{... | collective-permute-start | bytes 1966088 | tf_op jit(solution)/shard_map/ppermute | solution.py:274
  343.1 18.5 %collective-permute-start.9 = (bf16[160,2048]{1,0:T(8,128)(2,1)S(1)}, bf16[160,2048]{1,0:T(8,128)(2,1)S(1)}, u32[]{:S(2)}, u32[]{:S(2)}) collective-permute-start(bf16[160,2048]{1,0:T(8,128)(2,1)S(1)} %get-tuple-element.10), channel_id=1, source_target_pairs={{4,0},{8,4},{12,8},{5,1},{9,5},{13,9},{6,2},{10,6},{14,10},{7,3},{... | collective-permute-start | bytes 1966088 | tf_op jit(solution)/shard_map/ppermute | solution.py:275
  357.2 17.7 %collective-permute-start.10 = (bf16[160,2048]{1,0:T(8,128)(2,1)S(1)}, bf16[160,2048]{1,0:T(8,128)(2,1)S(1)}, u32[]{:S(2)}, u32[]{:S(2)}) collective-permute-start(bf16[160,2048]{1,0:T(8,128)(2,1)S(1)} %collective-permute-done.8), channel_id=1, source_target_pairs={{0,4},{4,8},{8,12},{1,5},{5,9},{9,13},{2,6},{6,10},{10,14},{3,7},{... | collective-permute-start | bytes 1966088 | tf_op jit(solution)/shard_map/ppermute | solution.py:274
  361.6 18.5 %collective-permute-start.11 = (bf16[160,2048]{1,0:T(8,128)(2,1)S(1)}, bf16[160,2048]{1,0:T(8,128)(2,1)S(1)}, u32[]{:S(2)}, u32[]{:S(2)}) collective-permute-start(bf16[160,2048]{1,0:T(8,128)(2,1)S(1)} %collective-permute-done.9), channel_id=1, source_target_pairs={{4,0},{8,4},{12,8},{5,1},{9,5},{13,9},{6,2},{10,6},{14,10},{7,3},{... | collective-permute-start | bytes 1966088 | tf_op jit(solution)/shard_map/ppermute | solution.py:275
  374.8 16.8 %collective-permute-start.12 = (bf16[160,2048]{1,0:T(8,128)(2,1)S(1)}, bf16[160,2048]{1,0:T(8,128)(2,1)S(1)}, u32[]{:S(2)}, u32[]{:S(2)}) collective-permute-start(bf16[160,2048]{1,0:T(8,128)(2,1)S(1)} %collective-permute-done.10), channel_id=1, source_target_pairs={{0,4},{4,8},{8,12},{1,5},{5,9},{9,13},{2,6},{6,10},{10,14},{3,7},{... | collective-permute-start | bytes 1966088 | tf_op jit(solution)/shard_map/ppermute | solution.py:274
  380.1 16.5 %collective-permute-start.13 = (bf16[160,2048]{1,0:T(8,128)(2,1)S(1)}, bf16[160,2048]{1,0:T(8,128)(2,1)S(1)}, u32[]{:S(2)}, u32[]{:S(2)}) collective-permute-start(bf16[160,2048]{1,0:T(8,128)(2,1)S(1)} %collective-permute-done.11), channel_id=1, source_target_pairs={{4,0},{8,4},{12,8},{5,1},{9,5},{13,9},{6,2},{10,6},{14,10},{7,3},{... | collective-permute-start | bytes 1966088 | tf_op jit(solution)/shard_map/ppermute | solution.py:275
  404.8 2.6 collective-permute-start.14
  407.7 23.9 %collective-permute-start.15 = (bf16[320,1536]{1,0:T(8,128)(2,1)S(1)}, bf16[320,1536]{1,0:T(8,128)(2,1)S(1)}, u32[]{:S(2)}, u32[]{:S(2)}) collective-permute-start(bf16[320,1536]{1,0:T(8,128)(2,1)S(1)} %add_convert_fusion.2), channel_id=1, source_target_pairs={{0,2},{1,3},{2,0},{3,1},{4,6},{5,7},{6,4},{7,5},{8,10},{9,11},{10,... | collective-permute-start | bytes 2949128 | tf_op jit(solution)/shard_map/ppermute | solution.py:101
  431.7 3.1 copy-start.8
  431.8 3.1 copy-start.9
  432.2 2.6 collective-permute-start.16
Sparse Core Ops, SparseCore 0:
  69.5 113.0 reduce-scatter.2
  235.5 98.5 reduce-scatter.4

commit v13 on v10

--- a/solution.py
+++ b/solution.py
@@ -50,23 +50,30 @@
     allowed = cols <= rows
     keys = k_ref[...]
     values = v_ref[...]
-    for head in range(per_shared):
-        query = q_ref[:, head * HEAD_SIZE : (head + 1) * HEAD_SIZE]
-        scores = lax.dot_general(
-            query, keys, (((1,), (1,)), ((), ())), preferred_element_type=jnp.float32
+    def one_head(head, carry):
+        start = pl.multiple_of(head * HEAD_SIZE, HEAD_SIZE)
+        query = q_ref[:, pl.ds(start, HEAD_SIZE)]
+        scores = (
+            lax.dot_general(
+                query, keys, (((1,), (1,)), ((), ())), preferred_element_type=jnp.float32
+            )
+            * scale
         )
         masked = jnp.where(allowed, scores, NEG_FILL)
         row_max = jnp.max(masked, axis=1, keepdims=True)
-        weights = jnp.exp((masked - row_max) * scale)
+        weights = jnp.exp(masked - row_max)
         total = jnp.sum(weights, axis=1, keepdims=True)
         acc = jnp.dot(weights.astype(jnp.bfloat16), values, preferred_element_type=jnp.float32)
-        o_ref[:, head * HEAD_SIZE : (head + 1) * HEAD_SIZE] = (acc / total).astype(o_ref.dtype)
+        o_ref[:, pl.ds(start, HEAD_SIZE)] = (acc / total).astype(o_ref.dtype)
+        return carry
+
+    lax.fori_loop(0, per_shared, one_head, 0)
 
 
 def attend(queries, packed_kv, offset, shared_heads, per_shared, interpret=False):
     rows_local = queries.shape[0]
     seq = packed_kv.shape[0]
-    block_q = 256 if seq <= 2048 else 128
+    block_q = 512 if seq <= 2048 else 128
     block_q = min(block_q, rows_local)
     width = per_shared * HEAD_SIZE
     kernel = functools.partial(

time: 441 us -> 456 us (1.034)
  Pallas kernels: 25.2 us -> 40.4 us
    pallas_call x1, Pallas kernels: 25.2 us -> 40.4 us  [attend(): pl.pallas_call(kernel, grid_spec=grid_spec, out_shape=jax.ShapeDtypeStruc...]
where the time goes in v13:
time: 456 us
  waiting for transfers between devices  327 us (72%)
  matrix products  44.1 us (10%)
  Pallas kernels  40.4 us (9%)
  between operations  13.5 us (3%)
  starting transfers between devices  13.4 us (3%)
  other arithmetic  9.39 us (2%)
  local copies, waits for them, and re-layouts  8.28 us (2%)
    reduce_scatter x1, waiting for transfers between devices, local(): lax.psum_scatter(partial_out.astype(jnp.bfloat16), 'wide', scatter_dimens...  112 us
    ppermute x10, waiting for transfers between devices, pair_exchange(): return lax.ppermute(x, axis, perm=[(i, i ^ bit) for i in range(count)])  84.4 us
    reduce_scatter x1, waiting for transfers between devices, local(): lax.psum_scatter(both_part.astype(jnp.bfloat16), 'wide', scatter_dimensio...  63.7 us
    all_gather x1, waiting for transfers between devices, local(): hidden = lax.all_gather(hidden_chunk, 'wide', axis=0, tiled=True)  55.4 us
    pallas_call x1, Pallas kernels, attend(): pl.pallas_call(kernel, grid_spec=grid_spec, out_shape=jax.ShapeDtypeStruc...  40.4 us
    dot_general x1, matrix products, local(): jnp.dot(attended, out_weight, preferred_element_type=jnp.float32)  15.8 us
    dot_general x1, matrix products, local(): jnp.dot(scaled, jnp.concatenate([gate_weight, up_weight], axis=1), prefer...  15.3 us
    ppermute x1, waiting for transfers between devices, gather_causal(): lower = lax.ppermute(x, axis, perm=[(0, 2), (1, 3)])  11.1 us
  transfers between devices with their start and end apart: 14, of which 14 were waited for; matrix products, arithmetic and copies ran while one was open for 1% of the time, Pallas kernels for 0%

profile of v13, /device:TPU:0, one launch (start us, length us, event | category | flops | bytes accessed | tf_op | source)
XLA Modules:
  0.0 456.0 jit_solution(6376815052682202958)
XLA Ops:
  6.5 1.1 constant_dynamic-slice_fusion
  7.9 4.9 %collective-permute-start = (bf16[512,512]{1,0:T(8,128)(2,1)S(1)}, bf16[512,512]{1,0:T(8,128)(2,1)S(1)}, u32[]{:S(2)}, u32[]{:S(2)}) collective-permute-start(bf16[512,512]{1,0:T(8,128)(2,1)S(1)} %get-tuple-element.13), channel_id=1, source_target_pairs={{0,2},{1,3},{4,6},{5,7},{8,10},{9,11},{12,14},{13,15},{16,18},{17,... | collective-permute-start | bytes 1572872 | tf_op jit(solution)/shard_map/ppermute | solution.py:132
  12.8 11.1 %collective-permute-done = bf16[512,512]{1,0:T(8,128)(2,1)S(1)} collective-permute-done((bf16[512,512]{1,0:T(8,128)(2,1)S(1)}, bf16[512,512]{1,0:T(8,128)(2,1)S(1)}, u32[]{:S(2)}, u32[]{:S(2)}) %collective-permute-start) | collective-permute-done | bytes 524320 | tf_op jit(solution)/shard_map/ppermute | solution.py:132
  25.0 3.0 collective-permute-done.1
  29.0 1.1 slice_dynamic-update-slice_fusion.k_ref.v_ref
  30.1 40.4 %shard_map.118 = bf16[512,1536]{1,0:T(8,128)(2,1)S(1)} custom-call(s32[1]{0:T(128)} %bitcast.offset_ref, bf16[512,1536]{1,0:T(8,128)(2,1)S(1)} %copy-done.1, bf16[2048,512]{1,0:T(8,128)(2,1)S(1)} %slice_dynamic-update-slice_fusion.k_ref.v_ref, bf16[2048,512]{1,0:T(8,128)(2,1)S(1)} %slice_dynamic-update-slice_fusion.k_ref.v_ref), custom_call_target="tpu_custom_call" | custom-call | tf_op jit(solution)/shard_map/pallas_call | solution.py:95
  70.5 15.8 %convolution_convert_fusion = bf16[512,6144]{1,0:T(8,128)(2,1)} fusion(bf16[512,1536]{1,0:T(8,128)(2,1)S(1)} %shard_map.118, bf16[1536,6144]{1,0:T(8,128)(2,1)} %param.16), kind=kOutput, calls=%fused_computation.4 | convolution fusion | flops 9666822144 | bytes 26738688 | tf_op jit(solution)/shard_map/dot_general | solution.py:214
  87.2 112.3 %reduce-scatter.3.cloned.1.call-done = bf16[512,1536]{1,0:T(8,128)(2,1)} async-done(((bf16[512,6144]{1,0:T(8,128)(2,1)}), bf16[512,1536]{1,0:T(8,128)(2,1)}) %reduce-scatter.3.cloned.1.call-update) | async-done | bytes 1572880 | tf_op jit(solution)/shard_map/reduce_scatter | solution.py:215
  199.5 2.7 fusion.16
  202.2 1.9 copy-done.2
  204.3 2.5 collective-permute-done.2
  206.9 1.8 add_convert_fusion.4
  208.7 1.5 collective-permute-start.3
  210.2 22.4 %collective-permute-done.3 = bf16[320,1536]{1,0:T(8,128)(2,1)} collective-permute-done((bf16[320,1536]{1,0:T(8,128)(2,1)S(1)}, bf16[320,1536]{1,0:T(8,128)(2,1)}, u32[]{:S(2)}, u32[]{:S(2)}) %collective-permute-start.3) | collective-permute-done | bytes 983072 | tf_op jit(solution)/shard_map/ppermute | solution.py:105
  232.8 1.6 constant_dynamic-update-slice_fusion.3
  234.6 2.5 collective-permute-done.4
  237.2 15.3 %fusion.4 = bf16[640,4096]{1,0:T(8,128)(2,1)} fusion(bf16[1536,2048]{1,0:T(8,128)(2,1)} %param.20, bf16[1536,2048]{1,0:T(8,128)(2,1)} %param.19, bf16[640,1536]{1,0:T(8,128)(2,1)S(1)} %constant_dynamic-update-slice_fusion.2, f32[1536]{0:T(1024)S(1)} %convert_element_type.107), kind=kOutput, calls=%fused_computation.5 | convolution fusion | flops 8083800064 | bytes 19798016 | tf_op jit(solution)/shard_map/dot_general | solution.py:234
  254.2 1.6 collective-permute-start.5
  255.7 3.4 collective-permute-done.5
  259.2 3.0 collective-permute-start.6
  262.2 13.9 %collective-permute-done.6 = bf16[320,128]{0,1:T(8,128)(2,1)S(1)} collective-permute-done((bf16[320,128]{0,1:T(8,128)(2,1)S(1)}, bf16[320,128]{0,1:T(8,128)(2,1)S(1)}, u32[]{:S(2)}, u32[]{:S(2)}) %collective-permute-start.6) | collective-permute-done | bytes 81952 | tf_op jit(solution)/shard_map/ppermute | solution.py:105
  277.3 9.3 %collective-permute-done.7 = bf16[320,128]{0,1:T(8,128)(2,1)S(1)} collective-permute-done((bf16[320,128]{0,1:T(8,128)(2,1)S(1)}, bf16[320,128]{0,1:T(8,128)(2,1)S(1)}, u32[]{:S(2)}, u32[]{:S(2)}) %collective-permute-start.7) | collective-permute-done | bytes 81952 | tf_op jit(solution)/shard_map/ppermute | solution.py:105
  287.5 63.7 %reduce-scatter.5.cloned.1.call-done = bf16[160,4096]{1,0:T(8,128)(2,1)} async-done(((bf16[640,4096]{1,0:T(8,128)(2,1)}), bf16[160,4096]{1,0:T(8,128)(2,1)}) %reduce-scatter.5.cloned.1.call-update) | async-done | bytes 1310736 | tf_op jit(solution)/shard_map/reduce_scatter | solution.py:246
  351.2 1.6 convert_element_type.110
  352.8 1.3 fusion.15
  354.1 55.4 %all-gather.2.cloned.1.call-done = bf16[640,2048]{1,0:T(8,128)(2,1)} async-done(((bf16[160,2048]{1,0:T(8,128)(2,1)}), bf16[640,2048]{1,0:T(8,128)(2,1)}) %all-gather.2.cloned.1.call-update) | async-done | bytes 2621456 | tf_op jit(solution)/shard_map/all_gather | solution.py:261
  409.5 7.1 %fusion.25 = f32[640,1536]{1,0:T(8,128)S(1)} fusion(bf16[640,2048]{1,0:T(8,128)(2,1)} %all-gather.2.cloned.1.call-done, bf16[2048,1536]{1,0:T(8,128)(2,1)} %param.21), kind=kOutput, calls=%fused_computation.63 | convolution fusion | flops 4026531840 | bytes 12845056 | tf_op jit(solution)/shard_map/dot_general | solution.py:262
  416.8 2.6 collective-permute-done.8
  419.7 1.5 collective-permute-start.9
  421.2 22.3 %collective-permute-done.9 = bf16[320,1536]{1,0:T(8,128)(2,1)S(1)} collective-permute-done((bf16[320,1536]{1,0:T(8,128)(2,1)S(1)}, bf16[320,1536]{1,0:T(8,128)(2,1)S(1)}, u32[]{:S(2)}, u32[]{:S(2)}) %collective-permute-start.9) | collective-permute-done | bytes 983072 | tf_op jit(solution)/shard_map/ppermute | solution.py:105
  444.2 2.6 collective-permute-done.10
  446.8 2.7 fusion.9
  (64 shorter events, 8.7 us)
Async XLA Ops:
  6.5 246.8 %copy-start = (bf16[1536,8]{0,1:T(8,128)(2,1)S(1)}, bf16[1536,8]{0,1:T(8,128)(2,1)}, u32[]{:S(2)}) copy-start(bf16[1536,8]{0,1:T(8,128)(2,1)} %param.18) | copy-start | bytes 73732
  6.5 193.0 %reduce-scatter.3.cloned.1.call-start = ((), (), s32[]{:S(2)}) async-start(), calls=%async_computation.2 | async-start | bytes 7864320 | tf_op jit(solution)/shard_map/reduce_scatter | solution.py:215
  7.9 16.0 %collective-permute-start = (bf16[512,512]{1,0:T(8,128)(2,1)S(1)}, bf16[512,512]{1,0:T(8,128)(2,1)S(1)}, u32[]{:S(2)}, u32[]{:S(2)}) collective-permute-start(bf16[512,512]{1,0:T(8,128)(2,1)S(1)} %get-tuple-element.13), channel_id=1, source_target_pairs={{0,2},{1,3},{4,6},{5,7},{8,10},{9,11},{12,14},{13,15},{16,18},{17,... | collective-permute-start | bytes 1572872 | tf_op jit(solution)/shard_map/ppermute | solution.py:132
  25.0 3.0 collective-permute-start.1
  25.0 5.2 %copy-start.1 = (bf16[512,1536]{1,0:T(8,128)(2,1)S(1)}, bf16[512,1536]{1,0:T(8,128)(2,1)}, u32[]{:S(2)}) copy-start(bf16[512,1536]{1,0:T(8,128)(2,1)} %q_ref.1) | copy-start | bytes 4718596
  86.3 0.7 copy-start.3
  86.3 0.7 copy-start.4
  86.3 113.2 %copy-start.6 = (bf16[512,1536]{1,0:T(8,128)(2,1)S(1)}, bf16[512,1536]{1,0:T(8,128)(2,1)}, u32[]{:S(2)}) copy-start(bf16[512,1536]{1,0:T(8,128)(2,1)} %param.15) | copy-start | bytes 4718596
  86.3 264.8 %reduce-scatter.5.cloned.1.call-start = ((), (), s32[]{:S(2)}) async-start(), calls=%async_computation.3 | async-start | bytes 6553600 | tf_op jit(solution)/shard_map/reduce_scatter | solution.py:246
  202.2 1.9 copy-start.2
  204.2 2.6 collective-permute-start.2
  208.7 24.0 %collective-permute-start.3 = (bf16[320,1536]{1,0:T(8,128)(2,1)S(1)}, bf16[320,1536]{1,0:T(8,128)(2,1)}, u32[]{:S(2)}, u32[]{:S(2)}) collective-permute-start(bf16[320,1536]{1,0:T(8,128)(2,1)S(1)} %add_convert_fusion.4), channel_id=1, source_target_pairs={{0,2},{1,3},{2,0},{3,1},{4,6},{5,7},{6,4},{7,5},{8,10},{9,11},{10,... | collective-permute-start | bytes 2949128 | tf_op jit(solution)/shard_map/ppermute | solution.py:105
  232.8 1.7 copy-start.5
  234.5 2.6 collective-permute-start.4
  252.5 157.0 %all-gather.2.cloned.1.call-start = ((), (), s32[]{:S(2)}) async-start(), calls=%async_computation.4 | async-start | bytes 3276800 | tf_op jit(solution)/shard_map/all_gather | solution.py:261
  254.2 4.9 %collective-permute-start.5 = (bf16[320,128]{0,1:T(8,128)(2,1)S(1)}, bf16[320,128]{0,1:T(8,128)(2,1)S(1)}, u32[]{:S(2)}, u32[]{:S(2)}) collective-permute-start(bf16[320,128]{0,1:T(8,128)(2,1)S(1)} %dynamic-slice_convert_fusion.2), channel_id=1, source_target_pairs={{0,4},{4,0},{8,12},{12,8},{1,5},{5,1},{9,13},{13,9},{2,6},{6,2},{1... | collective-permute-start | bytes 245768 | tf_op jit(solution)/shard_map/ppermute | solution.py:105
  259.2 16.9 %collective-permute-start.6 = (bf16[320,128]{0,1:T(8,128)(2,1)S(1)}, bf16[320,128]{0,1:T(8,128)(2,1)S(1)}, u32[]{:S(2)}, u32[]{:S(2)}) collective-permute-start(bf16[320,128]{0,1:T(8,128)(2,1)S(1)} %add_convert_fusion.7), channel_id=1, source_target_pairs={{0,8},{4,12},{8,0},{12,4},{1,9},{5,13},{9,1},{13,5},{2,10},{6,14},... | collective-permute-start | bytes 245768 | tf_op jit(solution)/shard_map/ppermute | solution.py:105
  276.2 10.4 %collective-permute-start.7 = (bf16[320,128]{0,1:T(8,128)(2,1)S(1)}, bf16[320,128]{0,1:T(8,128)(2,1)S(1)}, u32[]{:S(2)}, u32[]{:S(2)}) collective-permute-start(bf16[320,128]{0,1:T(8,128)(2,1)S(1)} %add_convert_fusion.6), channel_id=1, source_target_pairs={{0,4},{4,0},{8,12},{12,8},{1,5},{5,1},{9,13},{13,9},{2,6},{6,2},{1... | collective-permute-start | bytes 245768 | tf_op jit(solution)/shard_map/ppermute | solution.py:105
  416.7 2.6 collective-permute-start.8
  419.7 23.9 %collective-permute-start.9 = (bf16[320,1536]{1,0:T(8,128)(2,1)S(1)}, bf16[320,1536]{1,0:T(8,128)(2,1)S(1)}, u32[]{:S(2)}, u32[]{:S(2)}) collective-permute-start(bf16[320,1536]{1,0:T(8,128)(2,1)S(1)} %add_convert_fusion.2), channel_id=1, source_target_pairs={{0,2},{1,3},{2,0},{3,1},{4,6},{5,7},{6,4},{7,5},{8,10},{9,11},{10,... | collective-permute-start | bytes 2949128 | tf_op jit(solution)/shard_map/ppermute | solution.py:105
  443.7 3.1 copy-start.8
  444.1 2.7 copy-start.7
  444.1 2.6 collective-permute-start.10
Sparse Core Ops, SparseCore 0:
  86.5 113.0 reduce-scatter.2
  252.6 98.5 reduce-scatter.4
  354.2 55.2 all-gather.1

commit v14 on v10

--- a/solution.py
+++ b/solution.py
@@ -52,12 +52,15 @@
     values = v_ref[...]
     for head in range(per_shared):
         query = q_ref[:, head * HEAD_SIZE : (head + 1) * HEAD_SIZE]
-        scores = lax.dot_general(
-            query, keys, (((1,), (1,)), ((), ())), preferred_element_type=jnp.float32
+        scores = (
+            lax.dot_general(
+                query, keys, (((1,), (1,)), ((), ())), preferred_element_type=jnp.float32
+            )
+            * scale
         )
         masked = jnp.where(allowed, scores, NEG_FILL)
         row_max = jnp.max(masked, axis=1, keepdims=True)
-        weights = jnp.exp((masked - row_max) * scale)
+        weights = jnp.exp(masked - row_max)
         total = jnp.sum(weights, axis=1, keepdims=True)
         acc = jnp.dot(weights.astype(jnp.bfloat16), values, preferred_element_type=jnp.float32)
         o_ref[:, head * HEAD_SIZE : (head + 1) * HEAD_SIZE] = (acc / total).astype(o_ref.dtype)

time: 441 us -> 439 us (level)
  no operation moved by 1% of the time
where the time goes in v14:
time: 439 us
  waiting for transfers between devices  327 us (74%)
  matrix products  44.1 us (10%)
  Pallas kernels  23.4 us (5%)
  between operations  13.5 us (3%)
  starting transfers between devices  13.4 us (3%)
  other arithmetic  9.39 us (2%)
  local copies, waits for them, and re-layouts  8.28 us (2%)
    reduce_scatter x1, waiting for transfers between devices, local(): lax.psum_scatter(partial_out.astype(jnp.bfloat16), 'wide', scatter_dimens...  112 us
    ppermute x10, waiting for transfers between devices, pair_exchange(): return lax.ppermute(x, axis, perm=[(i, i ^ bit) for i in range(count)])  84.4 us
    reduce_scatter x1, waiting for transfers between devices, local(): lax.psum_scatter(both_part.astype(jnp.bfloat16), 'wide', scatter_dimensio...  63.7 us
    all_gather x1, waiting for transfers between devices, local(): hidden = lax.all_gather(hidden_chunk, 'wide', axis=0, tiled=True)  55.4 us
    pallas_call x1, Pallas kernels, attend(): pl.pallas_call(kernel, grid_spec=grid_spec, out_shape=jax.ShapeDtypeStruc...  23.4 us
    dot_general x1, matrix products, local(): jnp.dot(attended, out_weight, preferred_element_type=jnp.float32)  15.8 us
    dot_general x1, matrix products, local(): jnp.dot(scaled, jnp.concatenate([gate_weight, up_weight], axis=1), prefer...  15.3 us
    ppermute x1, waiting for transfers between devices, gather_causal(): lower = lax.ppermute(x, axis, perm=[(0, 2), (1, 3)])  11.1 us
  transfers between devices with their start and end apart: 14, of which 14 were waited for; matrix products, arithmetic and copies ran while one was open for 1% of the time, Pallas kernels for 0%

profile of v14, /device:TPU:0, one launch (start us, length us, event | category | flops | bytes accessed | tf_op | source)
XLA Modules:
  0.0 439.0 jit_solution(3376677052317492874)
XLA Ops:
  6.5 1.1 constant_dynamic-slice_fusion
  7.9 4.9 %collective-permute-start = (bf16[512,512]{1,0:T(8,128)(2,1)S(1)}, bf16[512,512]{1,0:T(8,128)(2,1)S(1)}, u32[]{:S(2)}, u32[]{:S(2)}) collective-permute-start(bf16[512,512]{1,0:T(8,128)(2,1)S(1)} %get-tuple-element.13), channel_id=1, source_target_pairs={{0,2},{1,3},{4,6},{5,7},{8,10},{9,11},{12,14},{13,15},{16,18},{17,... | collective-permute-start | bytes 1572872 | tf_op jit(solution)/shard_map/ppermute | solution.py:128
  12.8 11.1 %collective-permute-done = bf16[512,512]{1,0:T(8,128)(2,1)S(1)} collective-permute-done((bf16[512,512]{1,0:T(8,128)(2,1)S(1)}, bf16[512,512]{1,0:T(8,128)(2,1)S(1)}, u32[]{:S(2)}, u32[]{:S(2)}) %collective-permute-start) | collective-permute-done | bytes 524320 | tf_op jit(solution)/shard_map/ppermute | solution.py:128
  25.0 3.0 collective-permute-done.1
  29.0 1.1 slice_dynamic-update-slice_fusion.k_ref.v_ref
  30.1 23.4 %shard_map.118 = bf16[512,1536]{1,0:T(8,128)(2,1)S(1)} custom-call(s32[1]{0:T(128)} %bitcast.offset_ref, bf16[512,1536]{1,0:T(8,128)(2,1)S(1)} %copy-done.1, bf16[2048,512]{1,0:T(8,128)(2,1)S(1)} %slice_dynamic-update-slice_fusion.k_ref.v_ref, bf16[2048,512]{1,0:T(8,128)(2,1)S(1)} %slice_dynamic-update-slice_fusion.k_ref.v_ref), custom_call_target="tpu_custom_call" | custom-call | tf_op jit(solution)/shard_map/pallas_call | solution.py:91
  53.5 15.8 %convolution_convert_fusion = bf16[512,6144]{1,0:T(8,128)(2,1)} fusion(bf16[512,1536]{1,0:T(8,128)(2,1)S(1)} %shard_map.118, bf16[1536,6144]{1,0:T(8,128)(2,1)} %param.16), kind=kOutput, calls=%fused_computation.4 | convolution fusion | flops 9666822144 | bytes 26738688 | tf_op jit(solution)/shard_map/dot_general | solution.py:210
  70.1 112.3 %reduce-scatter.3.cloned.1.call-done = bf16[512,1536]{1,0:T(8,128)(2,1)} async-done(((bf16[512,6144]{1,0:T(8,128)(2,1)}), bf16[512,1536]{1,0:T(8,128)(2,1)}) %reduce-scatter.3.cloned.1.call-update) | async-done | bytes 1572880 | tf_op jit(solution)/shard_map/reduce_scatter | solution.py:211
  182.5 2.7 fusion.16
  185.1 1.9 copy-done.2
  187.3 2.5 collective-permute-done.2
  189.8 1.8 add_convert_fusion.4
  191.6 1.5 collective-permute-start.3
  193.2 22.4 %collective-permute-done.3 = bf16[320,1536]{1,0:T(8,128)(2,1)} collective-permute-done((bf16[320,1536]{1,0:T(8,128)(2,1)S(1)}, bf16[320,1536]{1,0:T(8,128)(2,1)}, u32[]{:S(2)}, u32[]{:S(2)}) %collective-permute-start.3) | collective-permute-done | bytes 983072 | tf_op jit(solution)/shard_map/ppermute | solution.py:101
  215.8 1.6 constant_dynamic-update-slice_fusion.3
  217.5 2.5 collective-permute-done.4
  220.1 15.3 %fusion.4 = bf16[640,4096]{1,0:T(8,128)(2,1)} fusion(bf16[1536,2048]{1,0:T(8,128)(2,1)} %param.20, bf16[1536,2048]{1,0:T(8,128)(2,1)} %param.19, bf16[640,1536]{1,0:T(8,128)(2,1)S(1)} %constant_dynamic-update-slice_fusion.2, f32[1536]{0:T(1024)S(1)} %convert_element_type.107), kind=kOutput, calls=%fused_computation.5 | convolution fusion | flops 8083800064 | bytes 19798016 | tf_op jit(solution)/shard_map/dot_general | solution.py:230
  237.1 1.6 collective-permute-start.5
  238.7 3.3 collective-permute-done.5
  242.1 3.0 collective-permute-start.6
  245.2 13.9 %collective-permute-done.6 = bf16[320,128]{0,1:T(8,128)(2,1)S(1)} collective-permute-done((bf16[320,128]{0,1:T(8,128)(2,1)S(1)}, bf16[320,128]{0,1:T(8,128)(2,1)S(1)}, u32[]{:S(2)}, u32[]{:S(2)}) %collective-permute-start.6) | collective-permute-done | bytes 81952 | tf_op jit(solution)/shard_map/ppermute | solution.py:101
  260.3 9.3 %collective-permute-done.7 = bf16[320,128]{0,1:T(8,128)(2,1)S(1)} collective-permute-done((bf16[320,128]{0,1:T(8,128)(2,1)S(1)}, bf16[320,128]{0,1:T(8,128)(2,1)S(1)}, u32[]{:S(2)}, u32[]{:S(2)}) %collective-permute-start.7) | collective-permute-done | bytes 81952 | tf_op jit(solution)/shard_map/ppermute | solution.py:101
  270.4 63.7 %reduce-scatter.5.cloned.1.call-done = bf16[160,4096]{1,0:T(8,128)(2,1)} async-done(((bf16[640,4096]{1,0:T(8,128)(2,1)}), bf16[160,4096]{1,0:T(8,128)(2,1)}) %reduce-scatter.5.cloned.1.call-update) | async-done | bytes 1310736 | tf_op jit(solution)/shard_map/reduce_scatter | solution.py:242
  334.1 1.6 convert_element_type.110
  335.7 1.3 fusion.15
  337.0 55.4 %all-gather.2.cloned.1.call-done = bf16[640,2048]{1,0:T(8,128)(2,1)} async-done(((bf16[160,2048]{1,0:T(8,128)(2,1)}), bf16[640,2048]{1,0:T(8,128)(2,1)}) %all-gather.2.cloned.1.call-update) | async-done | bytes 2621456 | tf_op jit(solution)/shard_map/all_gather | solution.py:257
  392.5 7.1 %fusion.25 = f32[640,1536]{1,0:T(8,128)S(1)} fusion(bf16[640,2048]{1,0:T(8,128)(2,1)} %all-gather.2.cloned.1.call-done, bf16[2048,1536]{1,0:T(8,128)(2,1)} %param.21), kind=kOutput, calls=%fused_computation.63 | convolution fusion | flops 4026531840 | bytes 12845056 | tf_op jit(solution)/shard_map/dot_general | solution.py:258
  399.8 2.6 collective-permute-done.8
  402.7 1.5 collective-permute-start.9
  404.2 22.3 %collective-permute-done.9 = bf16[320,1536]{1,0:T(8,128)(2,1)S(1)} collective-permute-done((bf16[320,1536]{1,0:T(8,128)(2,1)S(1)}, bf16[320,1536]{1,0:T(8,128)(2,1)S(1)}, u32[]{:S(2)}, u32[]{:S(2)}) %collective-permute-start.9) | collective-permute-done | bytes 983072 | tf_op jit(solution)/shard_map/ppermute | solution.py:101
  427.1 2.6 collective-permute-done.10
  429.8 2.7 fusion.9
  (64 shorter events, 8.7 us)
Async XLA Ops:
  6.5 229.7 %copy-start = (bf16[1536,8]{0,1:T(8,128)(2,1)S(1)}, bf16[1536,8]{0,1:T(8,128)(2,1)}, u32[]{:S(2)}) copy-start(bf16[1536,8]{0,1:T(8,128)(2,1)} %param.18) | copy-start | bytes 73732
  6.5 175.9 %reduce-scatter.3.cloned.1.call-start = ((), (), s32[]{:S(2)}) async-start(), calls=%async_computation.2 | async-start | bytes 7864320 | tf_op jit(solution)/shard_map/reduce_scatter | solution.py:211
  7.9 16.0 %collective-permute-start = (bf16[512,512]{1,0:T(8,128)(2,1)S(1)}, bf16[512,512]{1,0:T(8,128)(2,1)S(1)}, u32[]{:S(2)}, u32[]{:S(2)}) collective-permute-start(bf16[512,512]{1,0:T(8,128)(2,1)S(1)} %get-tuple-element.13), channel_id=1, source_target_pairs={{0,2},{1,3},{4,6},{5,7},{8,10},{9,11},{12,14},{13,15},{16,18},{17,... | collective-permute-start | bytes 1572872 | tf_op jit(solution)/shard_map/ppermute | solution.py:128
  25.0 3.0 collective-permute-start.1
  25.0 5.2 %copy-start.1 = (bf16[512,1536]{1,0:T(8,128)(2,1)S(1)}, bf16[512,1536]{1,0:T(8,128)(2,1)}, u32[]{:S(2)}) copy-start(bf16[512,1536]{1,0:T(8,128)(2,1)} %q_ref.1) | copy-start | bytes 4718596
  69.3 0.7 copy-start.3
  69.3 0.7 copy-start.4
  69.3 113.2 %copy-start.6 = (bf16[512,1536]{1,0:T(8,128)(2,1)S(1)}, bf16[512,1536]{1,0:T(8,128)(2,1)}, u32[]{:S(2)}) copy-start(bf16[512,1536]{1,0:T(8,128)(2,1)} %param.15) | copy-start | bytes 4718596
  69.3 264.8 %reduce-scatter.5.cloned.1.call-start = ((), (), s32[]{:S(2)}) async-start(), calls=%async_computation.3 | async-start | bytes 6553600 | tf_op jit(solution)/shard_map/reduce_scatter | solution.py:242
  185.1 1.9 copy-start.2
  187.2 2.6 collective-permute-start.2
  191.6 24.0 %collective-permute-start.3 = (bf16[320,1536]{1,0:T(8,128)(2,1)S(1)}, bf16[320,1536]{1,0:T(8,128)(2,1)}, u32[]{:S(2)}, u32[]{:S(2)}) collective-permute-start(bf16[320,1536]{1,0:T(8,128)(2,1)S(1)} %add_convert_fusion.4), channel_id=1, source_target_pairs={{0,2},{1,3},{2,0},{3,1},{4,6},{5,7},{6,4},{7,5},{8,10},{9,11},{10,... | collective-permute-start | bytes 2949128 | tf_op jit(solution)/shard_map/ppermute | solution.py:101
  215.7 1.7 copy-start.5
  217.4 2.6 collective-permute-start.4
  235.4 157.0 %all-gather.2.cloned.1.call-start = ((), (), s32[]{:S(2)}) async-start(), calls=%async_computation.4 | async-start | bytes 3276800 | tf_op jit(solution)/shard_map/all_gather | solution.py:257
  237.1 4.9 %collective-permute-start.5 = (bf16[320,128]{0,1:T(8,128)(2,1)S(1)}, bf16[320,128]{0,1:T(8,128)(2,1)S(1)}, u32[]{:S(2)}, u32[]{:S(2)}) collective-permute-start(bf16[320,128]{0,1:T(8,128)(2,1)S(1)} %dynamic-slice_convert_fusion.2), channel_id=1, source_target_pairs={{0,4},{4,0},{8,12},{12,8},{1,5},{5,1},{9,13},{13,9},{2,6},{6,2},{1... | collective-permute-start | bytes 245768 | tf_op jit(solution)/shard_map/ppermute | solution.py:101
  242.1 16.9 %collective-permute-start.6 = (bf16[320,128]{0,1:T(8,128)(2,1)S(1)}, bf16[320,128]{0,1:T(8,128)(2,1)S(1)}, u32[]{:S(2)}, u32[]{:S(2)}) collective-permute-start(bf16[320,128]{0,1:T(8,128)(2,1)S(1)} %add_convert_fusion.7), channel_id=1, source_target_pairs={{0,8},{4,12},{8,0},{12,4},{1,9},{5,13},{9,1},{13,5},{2,10},{6,14},... | collective-permute-start | bytes 245768 | tf_op jit(solution)/shard_map/ppermute | solution.py:101
  259.1 10.4 %collective-permute-start.7 = (bf16[320,128]{0,1:T(8,128)(2,1)S(1)}, bf16[320,128]{0,1:T(8,128)(2,1)S(1)}, u32[]{:S(2)}, u32[]{:S(2)}) collective-permute-start(bf16[320,128]{0,1:T(8,128)(2,1)S(1)} %add_convert_fusion.6), channel_id=1, source_target_pairs={{0,4},{4,0},{8,12},{12,8},{1,5},{5,1},{9,13},{13,9},{2,6},{6,2},{1... | collective-permute-start | bytes 245768 | tf_op jit(solution)/shard_map/ppermute | solution.py:101
  399.7 2.6 collective-permute-start.8
  402.7 23.9 %collective-permute-start.9 = (bf16[320,1536]{1,0:T(8,128)(2,1)S(1)}, bf16[320,1536]{1,0:T(8,128)(2,1)S(1)}, u32[]{:S(2)}, u32[]{:S(2)}) collective-permute-start(bf16[320,1536]{1,0:T(8,128)(2,1)S(1)} %add_convert_fusion.2), channel_id=1, source_target_pairs={{0,2},{1,3},{2,0},{3,1},{4,6},{5,7},{6,4},{7,5},{8,10},{9,11},{10,... | collective-permute-start | bytes 2949128 | tf_op jit(solution)/shard_map/ppermute | solution.py:101
  426.7 3.1 copy-start.8
  427.1 2.7 copy-start.7
  427.1 2.6 collective-permute-start.10
Sparse Core Ops, SparseCore 0:
  69.4 113.0 reduce-scatter.2
  235.6 98.5 reduce-scatter.4
  337.2 55.2 all-gather.1

commit v15 on v14

--- a/solution.py
+++ b/solution.py
@@ -69,7 +69,7 @@
 def attend(queries, packed_kv, offset, shared_heads, per_shared, interpret=False):
     rows_local = queries.shape[0]
     seq = packed_kv.shape[0]
-    block_q = 256 if seq <= 2048 else 128
+    block_q = 128
     block_q = min(block_q, rows_local)
     width = per_shared * HEAD_SIZE
     kernel = functools.partial(

time: 439 us -> 444 us (1.011)
  no operation moved by 1% of the time
where the time goes in v15:
time: 444 us; the launch traced here: 443 us
  waiting for transfers between devices  327 us (74%)
  matrix products  44.1 us (10%)
  Pallas kernels  27.7 us (6%)
  between operations  13.5 us (3%)
  starting transfers between devices  13.4 us (3%)
  other arithmetic  9.39 us (2%)
  local copies, waits for them, and re-layouts  8.28 us (2%)
    reduce_scatter x1, waiting for transfers between devices, local(): lax.psum_scatter(partial_out.astype(jnp.bfloat16), 'wide', scatter_dimens...  112 us
    ppermute x10, waiting for transfers between devices, pair_exchange(): return lax.ppermute(x, axis, perm=[(i, i ^ bit) for i in range(count)])  84.4 us
    reduce_scatter x1, waiting for transfers between devices, local(): lax.psum_scatter(both_part.astype(jnp.bfloat16), 'wide', scatter_dimensio...  63.7 us
    all_gather x1, waiting for transfers between devices, local(): hidden = lax.all_gather(hidden_chunk, 'wide', axis=0, tiled=True)  55.4 us
    pallas_call x1, Pallas kernels, attend(): pl.pallas_call(kernel, grid_spec=grid_spec, out_shape=jax.ShapeDtypeStruc...  27.7 us
    dot_general x1, matrix products, local(): jnp.dot(attended, out_weight, preferred_element_type=jnp.float32)  15.8 us
    dot_general x1, matrix products, local(): jnp.dot(scaled, jnp.concatenate([gate_weight, up_weight], axis=1), prefer...  15.3 us
    ppermute x1, waiting for transfers between devices, gather_causal(): lower = lax.ppermute(x, axis, perm=[(0, 2), (1, 3)])  11.1 us
  transfers between devices with their start and end apart: 14, of which 14 were waited for; matrix products, arithmetic and copies ran while one was open for 1% of the time, Pallas kernels for 0%

profile of v15, /device:TPU:0, one launch (start us, length us, event | category | flops | bytes accessed | tf_op | source)
XLA Modules:
  0.0 443.3 jit_solution(2171415437569605312)
XLA Ops:
  6.5 1.1 constant_dynamic-slice_fusion
  7.9 4.9 %collective-permute-start = (bf16[512,512]{1,0:T(8,128)(2,1)S(1)}, bf16[512,512]{1,0:T(8,128)(2,1)S(1)}, u32[]{:S(2)}, u32[]{:S(2)}) collective-permute-start(bf16[512,512]{1,0:T(8,128)(2,1)S(1)} %get-tuple-element.13), channel_id=1, source_target_pairs={{0,2},{1,3},{4,6},{5,7},{8,10},{9,11},{12,14},{13,15},{16,18},{17,... | collective-permute-start | bytes 1572872 | tf_op jit(solution)/shard_map/ppermute | solution.py:128
  12.8 11.1 %collective-permute-done = bf16[512,512]{1,0:T(8,128)(2,1)S(1)} collective-permute-done((bf16[512,512]{1,0:T(8,128)(2,1)S(1)}, bf16[512,512]{1,0:T(8,128)(2,1)S(1)}, u32[]{:S(2)}, u32[]{:S(2)}) %collective-permute-start) | collective-permute-done | bytes 524320 | tf_op jit(solution)/shard_map/ppermute | solution.py:128
  25.0 3.0 collective-permute-done.1
  29.0 1.1 slice_dynamic-update-slice_fusion.k_ref.v_ref
  30.1 27.7 %shard_map.118 = bf16[512,1536]{1,0:T(8,128)(2,1)S(1)} custom-call(s32[1]{0:T(128)} %bitcast.offset_ref, bf16[512,1536]{1,0:T(8,128)(2,1)S(1)} %copy-done.1, bf16[2048,512]{1,0:T(8,128)(2,1)S(1)} %slice_dynamic-update-slice_fusion.k_ref.v_ref, bf16[2048,512]{1,0:T(8,128)(2,1)S(1)} %slice_dynamic-update-slice_fusion.k_ref.v_ref), custom_call_target="tpu_custom_call" | custom-call | tf_op jit(solution)/shard_map/pallas_call | solution.py:91
  57.8 15.8 %convolution_convert_fusion = bf16[512,6144]{1,0:T(8,128)(2,1)} fusion(bf16[512,1536]{1,0:T(8,128)(2,1)S(1)} %shard_map.118, bf16[1536,6144]{1,0:T(8,128)(2,1)} %param.16), kind=kOutput, calls=%fused_computation.4 | convolution fusion | flops 9666822144 | bytes 26738688 | tf_op jit(solution)/shard_map/dot_general | solution.py:210
  74.5 112.3 %reduce-scatter.3.cloned.1.call-done = bf16[512,1536]{1,0:T(8,128)(2,1)} async-done(((bf16[512,6144]{1,0:T(8,128)(2,1)}), bf16[512,1536]{1,0:T(8,128)(2,1)}) %reduce-scatter.3.cloned.1.call-update) | async-done | bytes 1572880 | tf_op jit(solution)/shard_map/reduce_scatter | solution.py:211
  186.8 2.7 fusion.16
  189.5 1.9 copy-done.2
  191.6 2.5 collective-permute-done.2
  194.2 1.8 add_convert_fusion.4
  196.0 1.5 collective-permute-start.3
  197.5 22.4 %collective-permute-done.3 = bf16[320,1536]{1,0:T(8,128)(2,1)} collective-permute-done((bf16[320,1536]{1,0:T(8,128)(2,1)S(1)}, bf16[320,1536]{1,0:T(8,128)(2,1)}, u32[]{:S(2)}, u32[]{:S(2)}) %collective-permute-start.3) | collective-permute-done | bytes 983072 | tf_op jit(solution)/shard_map/ppermute | solution.py:101
  220.1 1.6 constant_dynamic-update-slice_fusion.3
  221.8 2.5 collective-permute-done.4
  224.5 15.3 %fusion.4 = bf16[640,4096]{1,0:T(8,128)(2,1)} fusion(bf16[1536,2048]{1,0:T(8,128)(2,1)} %param.20, bf16[1536,2048]{1,0:T(8,128)(2,1)} %param.19, bf16[640,1536]{1,0:T(8,128)(2,1)S(1)} %constant_dynamic-update-slice_fusion.2, f32[1536]{0:T(1024)S(1)} %convert_element_type.107), kind=kOutput, calls=%fused_computation.5 | convolution fusion | flops 8083800064 | bytes 19798016 | tf_op jit(solution)/shard_map/dot_general | solution.py:230
  241.5 1.6 collective-permute-start.5
  243.0 3.3 collective-permute-done.5
  246.5 3.0 collective-permute-start.6
  249.5 13.9 %collective-permute-done.6 = bf16[320,128]{0,1:T(8,128)(2,1)S(1)} collective-permute-done((bf16[320,128]{0,1:T(8,128)(2,1)S(1)}, bf16[320,128]{0,1:T(8,128)(2,1)S(1)}, u32[]{:S(2)}, u32[]{:S(2)}) %collective-permute-start.6) | collective-permute-done | bytes 81952 | tf_op jit(solution)/shard_map/ppermute | solution.py:101
  264.6 9.3 %collective-permute-done.7 = bf16[320,128]{0,1:T(8,128)(2,1)S(1)} collective-permute-done((bf16[320,128]{0,1:T(8,128)(2,1)S(1)}, bf16[320,128]{0,1:T(8,128)(2,1)S(1)}, u32[]{:S(2)}, u32[]{:S(2)}) %collective-permute-start.7) | collective-permute-done | bytes 81952 | tf_op jit(solution)/shard_map/ppermute | solution.py:101
  274.8 63.7 %reduce-scatter.5.cloned.1.call-done = bf16[160,4096]{1,0:T(8,128)(2,1)} async-done(((bf16[640,4096]{1,0:T(8,128)(2,1)}), bf16[160,4096]{1,0:T(8,128)(2,1)}) %reduce-scatter.5.cloned.1.call-update) | async-done | bytes 1310736 | tf_op jit(solution)/shard_map/reduce_scatter | solution.py:242
  338.5 1.6 convert_element_type.110
  340.1 1.3 fusion.15
  341.4 55.4 %all-gather.2.cloned.1.call-done = bf16[640,2048]{1,0:T(8,128)(2,1)} async-done(((bf16[160,2048]{1,0:T(8,128)(2,1)}), bf16[640,2048]{1,0:T(8,128)(2,1)}) %all-gather.2.cloned.1.call-update) | async-done | bytes 2621456 | tf_op jit(solution)/shard_map/all_gather | solution.py:257
  396.8 7.1 %fusion.25 = f32[640,1536]{1,0:T(8,128)S(1)} fusion(bf16[640,2048]{1,0:T(8,128)(2,1)} %all-gather.2.cloned.1.call-done, bf16[2048,1536]{1,0:T(8,128)(2,1)} %param.21), kind=kOutput, calls=%fused_computation.63 | convolution fusion | flops 4026531840 | bytes 12845056 | tf_op jit(solution)/shard_map/dot_general | solution.py:258
  404.1 2.6 collective-permute-done.8
  407.0 1.5 collective-permute-start.9
  408.5 22.3 %collective-permute-done.9 = bf16[320,1536]{1,0:T(8,128)(2,1)S(1)} collective-permute-done((bf16[320,1536]{1,0:T(8,128)(2,1)S(1)}, bf16[320,1536]{1,0:T(8,128)(2,1)S(1)}, u32[]{:S(2)}, u32[]{:S(2)}) %collective-permute-start.9) | collective-permute-done | bytes 983072 | tf_op jit(solution)/shard_map/ppermute | solution.py:101
  431.5 2.6 collective-permute-done.10
  434.1 2.7 fusion.9
  (64 shorter events, 8.7 us)
Async XLA Ops:
  6.5 234.1 %copy-start = (bf16[1536,8]{0,1:T(8,128)(2,1)S(1)}, bf16[1536,8]{0,1:T(8,128)(2,1)}, u32[]{:S(2)}) copy-start(bf16[1536,8]{0,1:T(8,128)(2,1)} %param.18) | copy-start | bytes 73732
  6.5 180.3 %reduce-scatter.3.cloned.1.call-start = ((), (), s32[]{:S(2)}) async-start(), calls=%async_computation.2 | async-start | bytes 7864320 | tf_op jit(solution)/shard_map/reduce_scatter | solution.py:211
  7.9 16.0 %collective-permute-start = (bf16[512,512]{1,0:T(8,128)(2,1)S(1)}, bf16[512,512]{1,0:T(8,128)(2,1)S(1)}, u32[]{:S(2)}, u32[]{:S(2)}) collective-permute-start(bf16[512,512]{1,0:T(8,128)(2,1)S(1)} %get-tuple-element.13), channel_id=1, source_target_pairs={{0,2},{1,3},{4,6},{5,7},{8,10},{9,11},{12,14},{13,15},{16,18},{17,... | collective-permute-start | bytes 1572872 | tf_op jit(solution)/shard_map/ppermute | solution.py:128
  25.0 3.0 collective-permute-start.1
  25.0 5.2 %copy-start.1 = (bf16[512,1536]{1,0:T(8,128)(2,1)S(1)}, bf16[512,1536]{1,0:T(8,128)(2,1)}, u32[]{:S(2)}) copy-start(bf16[512,1536]{1,0:T(8,128)(2,1)} %q_ref.1) | copy-start | bytes 4718596
  73.6 0.7 copy-start.3
  73.6 0.7 copy-start.4
  73.6 113.2 %copy-start.6 = (bf16[512,1536]{1,0:T(8,128)(2,1)S(1)}, bf16[512,1536]{1,0:T(8,128)(2,1)}, u32[]{:S(2)}) copy-start(bf16[512,1536]{1,0:T(8,128)(2,1)} %param.15) | copy-start | bytes 4718596
  73.6 264.8 %reduce-scatter.5.cloned.1.call-start = ((), (), s32[]{:S(2)}) async-start(), calls=%async_computation.3 | async-start | bytes 6553600 | tf_op jit(solution)/shard_map/reduce_scatter | solution.py:242
  189.5 1.9 copy-start.2
  191.5 2.6 collective-permute-start.2
  196.0 24.0 %collective-permute-start.3 = (bf16[320,1536]{1,0:T(8,128)(2,1)S(1)}, bf16[320,1536]{1,0:T(8,128)(2,1)}, u32[]{:S(2)}, u32[]{:S(2)}) collective-permute-start(bf16[320,1536]{1,0:T(8,128)(2,1)S(1)} %add_convert_fusion.4), channel_id=1, source_target_pairs={{0,2},{1,3},{2,0},{3,1},{4,6},{5,7},{6,4},{7,5},{8,10},{9,11},{10,... | collective-permute-start | bytes 2949128 | tf_op jit(solution)/shard_map/ppermute | solution.py:101
  220.1 1.7 copy-start.5
  221.7 2.6 collective-permute-start.4
  239.8 157.0 %all-gather.2.cloned.1.call-start = ((), (), s32[]{:S(2)}) async-start(), calls=%async_computation.4 | async-start | bytes 3276800 | tf_op jit(solution)/shard_map/all_gather | solution.py:257
  241.5 4.9 %collective-permute-start.5 = (bf16[320,128]{0,1:T(8,128)(2,1)S(1)}, bf16[320,128]{0,1:T(8,128)(2,1)S(1)}, u32[]{:S(2)}, u32[]{:S(2)}) collective-permute-start(bf16[320,128]{0,1:T(8,128)(2,1)S(1)} %dynamic-slice_convert_fusion.2), channel_id=1, source_target_pairs={{0,4},{4,0},{8,12},{12,8},{1,5},{5,1},{9,13},{13,9},{2,6},{6,2},{1... | collective-permute-start | bytes 245768 | tf_op jit(solution)/shard_map/ppermute | solution.py:101
  246.5 16.9 %collective-permute-start.6 = (bf16[320,128]{0,1:T(8,128)(2,1)S(1)}, bf16[320,128]{0,1:T(8,128)(2,1)S(1)}, u32[]{:S(2)}, u32[]{:S(2)}) collective-permute-start(bf16[320,128]{0,1:T(8,128)(2,1)S(1)} %add_convert_fusion.7), channel_id=1, source_target_pairs={{0,8},{4,12},{8,0},{12,4},{1,9},{5,13},{9,1},{13,5},{2,10},{6,14},... | collective-permute-start | bytes 245768 | tf_op jit(solution)/shard_map/ppermute | solution.py:101
  263.5 10.4 %collective-permute-start.7 = (bf16[320,128]{0,1:T(8,128)(2,1)S(1)}, bf16[320,128]{0,1:T(8,128)(2,1)S(1)}, u32[]{:S(2)}, u32[]{:S(2)}) collective-permute-start(bf16[320,128]{0,1:T(8,128)(2,1)S(1)} %add_convert_fusion.6), channel_id=1, source_target_pairs={{0,4},{4,0},{8,12},{12,8},{1,5},{5,1},{9,13},{13,9},{2,6},{6,2},{1... | collective-permute-start | bytes 245768 | tf_op jit(solution)/shard_map/ppermute | solution.py:101
  404.1 2.6 collective-permute-start.8
  407.0 23.9 %collective-permute-start.9 = (bf16[320,1536]{1,0:T(8,128)(2,1)S(1)}, bf16[320,1536]{1,0:T(8,128)(2,1)S(1)}, u32[]{:S(2)}, u32[]{:S(2)}) collective-permute-start(bf16[320,1536]{1,0:T(8,128)(2,1)S(1)} %add_convert_fusion.2), channel_id=1, source_target_pairs={{0,2},{1,3},{2,0},{3,1},{4,6},{5,7},{6,4},{7,5},{8,10},{9,11},{10,... | collective-permute-start | bytes 2949128 | tf_op jit(solution)/shard_map/ppermute | solution.py:101
  431.0 3.1 copy-start.8
  431.4 2.7 copy-start.7
  431.4 2.6 collective-permute-start.10
Sparse Core Ops, SparseCore 0:
  73.7 113.0 reduce-scatter.2
  239.9 98.5 reduce-scatter.4
  341.5 55.2 all-gather.1

commit v16 on v13

--- a/solution.py
+++ b/solution.py
@@ -73,7 +73,7 @@
 def attend(queries, packed_kv, offset, shared_heads, per_shared, interpret=False):
     rows_local = queries.shape[0]
     seq = packed_kv.shape[0]
-    block_q = 512 if seq <= 2048 else 128
+    block_q = 256 if seq <= 2048 else 128
     block_q = min(block_q, rows_local)
     width = per_shared * HEAD_SIZE
     kernel = functools.partial(

time: 456 us -> 448 us (0.982)
  Pallas kernels: 40.4 us -> 31.9 us
    pallas_call x1, Pallas kernels: 40.4 us -> 31.9 us  [attend(): pl.pallas_call(kernel, grid_spec=grid_spec, out_shape=jax.ShapeDtypeStruc...]
where the time goes in v16:
time: 448 us
  waiting for transfers between devices  327 us (73%)
  matrix products  44.1 us (10%)
  Pallas kernels  31.9 us (7%)
  between operations  13.5 us (3%)
  starting transfers between devices  13.4 us (3%)
  other arithmetic  9.39 us (2%)
  local copies, waits for them, and re-layouts  8.28 us (2%)
    reduce_scatter x1, waiting for transfers between devices, local(): lax.psum_scatter(partial_out.astype(jnp.bfloat16), 'wide', scatter_dimens...  112 us
    ppermute x10, waiting for transfers between devices, pair_exchange(): return lax.ppermute(x, axis, perm=[(i, i ^ bit) for i in range(count)])  84.4 us
    reduce_scatter x1, waiting for transfers between devices, local(): lax.psum_scatter(both_part.astype(jnp.bfloat16), 'wide', scatter_dimensio...  63.7 us
    all_gather x1, waiting for transfers between devices, local(): hidden = lax.all_gather(hidden_chunk, 'wide', axis=0, tiled=True)  55.4 us
    pallas_call x1, Pallas kernels, attend(): pl.pallas_call(kernel, grid_spec=grid_spec, out_shape=jax.ShapeDtypeStruc...  31.9 us
    dot_general x1, matrix products, local(): jnp.dot(attended, out_weight, preferred_element_type=jnp.float32)  15.8 us
    dot_general x1, matrix products, local(): jnp.dot(scaled, jnp.concatenate([gate_weight, up_weight], axis=1), prefer...  15.3 us
    ppermute x1, waiting for transfers between devices, gather_causal(): lower = lax.ppermute(x, axis, perm=[(0, 2), (1, 3)])  11.1 us
  transfers between devices with their start and end apart: 14, of which 14 were waited for; matrix products, arithmetic and copies ran while one was open for 1% of the time, Pallas kernels for 0%

profile of v16, /device:TPU:0, one launch (start us, length us, event | category | flops | bytes accessed | tf_op | source)
XLA Modules:
  0.0 447.5 jit_solution(11826753221873335194)
XLA Ops:
  6.5 1.1 constant_dynamic-slice_fusion
  7.9 4.9 %collective-permute-start = (bf16[512,512]{1,0:T(8,128)(2,1)S(1)}, bf16[512,512]{1,0:T(8,128)(2,1)S(1)}, u32[]{:S(2)}, u32[]{:S(2)}) collective-permute-start(bf16[512,512]{1,0:T(8,128)(2,1)S(1)} %get-tuple-element.13), channel_id=1, source_target_pairs={{0,2},{1,3},{4,6},{5,7},{8,10},{9,11},{12,14},{13,15},{16,18},{17,... | collective-permute-start | bytes 1572872 | tf_op jit(solution)/shard_map/ppermute | solution.py:132
  12.8 11.1 %collective-permute-done = bf16[512,512]{1,0:T(8,128)(2,1)S(1)} collective-permute-done((bf16[512,512]{1,0:T(8,128)(2,1)S(1)}, bf16[512,512]{1,0:T(8,128)(2,1)S(1)}, u32[]{:S(2)}, u32[]{:S(2)}) %collective-permute-start) | collective-permute-done | bytes 524320 | tf_op jit(solution)/shard_map/ppermute | solution.py:132
  25.0 3.0 collective-permute-done.1
  29.0 1.1 slice_dynamic-update-slice_fusion.k_ref.v_ref
  30.1 31.9 %shard_map.118 = bf16[512,1536]{1,0:T(8,128)(2,1)S(1)} custom-call(s32[1]{0:T(128)} %bitcast.offset_ref, bf16[512,1536]{1,0:T(8,128)(2,1)S(1)} %copy-done.1, bf16[2048,512]{1,0:T(8,128)(2,1)S(1)} %slice_dynamic-update-slice_fusion.k_ref.v_ref, bf16[2048,512]{1,0:T(8,128)(2,1)S(1)} %slice_dynamic-update-slice_fusion.k_ref.v_ref), custom_call_target="tpu_custom_call" | custom-call | tf_op jit(solution)/shard_map/pallas_call | solution.py:95
  62.0 15.8 %convolution_convert_fusion = bf16[512,6144]{1,0:T(8,128)(2,1)} fusion(bf16[512,1536]{1,0:T(8,128)(2,1)S(1)} %shard_map.118, bf16[1536,6144]{1,0:T(8,128)(2,1)} %param.16), kind=kOutput, calls=%fused_computation.4 | convolution fusion | flops 9666822144 | bytes 26738688 | tf_op jit(solution)/shard_map/dot_general | solution.py:214
  78.7 112.3 %reduce-scatter.3.cloned.1.call-done = bf16[512,1536]{1,0:T(8,128)(2,1)} async-done(((bf16[512,6144]{1,0:T(8,128)(2,1)}), bf16[512,1536]{1,0:T(8,128)(2,1)}) %reduce-scatter.3.cloned.1.call-update) | async-done | bytes 1572880 | tf_op jit(solution)/shard_map/reduce_scatter | solution.py:215
  191.0 2.7 fusion.16
  193.7 1.9 copy-done.2
  195.8 2.5 collective-permute-done.2
  198.3 1.8 add_convert_fusion.4
  200.2 1.6 collective-permute-start.3
  201.7 22.4 %collective-permute-done.3 = bf16[320,1536]{1,0:T(8,128)(2,1)} collective-permute-done((bf16[320,1536]{1,0:T(8,128)(2,1)S(1)}, bf16[320,1536]{1,0:T(8,128)(2,1)}, u32[]{:S(2)}, u32[]{:S(2)}) %collective-permute-start.3) | collective-permute-done | bytes 983072 | tf_op jit(solution)/shard_map/ppermute | solution.py:105
  224.3 1.6 constant_dynamic-update-slice_fusion.3
  226.0 2.5 collective-permute-done.4
  228.7 15.3 %fusion.4 = bf16[640,4096]{1,0:T(8,128)(2,1)} fusion(bf16[1536,2048]{1,0:T(8,128)(2,1)} %param.20, bf16[1536,2048]{1,0:T(8,128)(2,1)} %param.19, bf16[640,1536]{1,0:T(8,128)(2,1)S(1)} %constant_dynamic-update-slice_fusion.2, f32[1536]{0:T(1024)S(1)} %convert_element_type.107), kind=kOutput, calls=%fused_computation.5 | convolution fusion | flops 8083800064 | bytes 19798016 | tf_op jit(solution)/shard_map/dot_general | solution.py:234
  245.7 1.5 collective-permute-start.5
  247.2 3.4 collective-permute-done.5
  250.7 3.0 collective-permute-start.6
  253.7 13.9 %collective-permute-done.6 = bf16[320,128]{0,1:T(8,128)(2,1)S(1)} collective-permute-done((bf16[320,128]{0,1:T(8,128)(2,1)S(1)}, bf16[320,128]{0,1:T(8,128)(2,1)S(1)}, u32[]{:S(2)}, u32[]{:S(2)}) %collective-permute-start.6) | collective-permute-done | bytes 81952 | tf_op jit(solution)/shard_map/ppermute | solution.py:105
  268.8 9.3 %collective-permute-done.7 = bf16[320,128]{0,1:T(8,128)(2,1)S(1)} collective-permute-done((bf16[320,128]{0,1:T(8,128)(2,1)S(1)}, bf16[320,128]{0,1:T(8,128)(2,1)S(1)}, u32[]{:S(2)}, u32[]{:S(2)}) %collective-permute-start.7) | collective-permute-done | bytes 81952 | tf_op jit(solution)/shard_map/ppermute | solution.py:105
  279.0 63.7 %reduce-scatter.5.cloned.1.call-done = bf16[160,4096]{1,0:T(8,128)(2,1)} async-done(((bf16[640,4096]{1,0:T(8,128)(2,1)}), bf16[160,4096]{1,0:T(8,128)(2,1)}) %reduce-scatter.5.cloned.1.call-update) | async-done | bytes 1310736 | tf_op jit(solution)/shard_map/reduce_scatter | solution.py:246
  342.6 1.6 convert_element_type.110
  344.2 1.3 fusion.15
  345.6 55.4 %all-gather.2.cloned.1.call-done = bf16[640,2048]{1,0:T(8,128)(2,1)} async-done(((bf16[160,2048]{1,0:T(8,128)(2,1)}), bf16[640,2048]{1,0:T(8,128)(2,1)}) %all-gather.2.cloned.1.call-update) | async-done | bytes 2621456 | tf_op jit(solution)/shard_map/all_gather | solution.py:261
  401.0 7.1 %fusion.25 = f32[640,1536]{1,0:T(8,128)S(1)} fusion(bf16[640,2048]{1,0:T(8,128)(2,1)} %all-gather.2.cloned.1.call-done, bf16[2048,1536]{1,0:T(8,128)(2,1)} %param.21), kind=kOutput, calls=%fused_computation.63 | convolution fusion | flops 4026531840 | bytes 12845056 | tf_op jit(solution)/shard_map/dot_general | solution.py:262
  408.3 2.6 collective-permute-done.8
  411.2 1.5 collective-permute-start.9
  412.7 22.3 %collective-permute-done.9 = bf16[320,1536]{1,0:T(8,128)(2,1)S(1)} collective-permute-done((bf16[320,1536]{1,0:T(8,128)(2,1)S(1)}, bf16[320,1536]{1,0:T(8,128)(2,1)S(1)}, u32[]{:S(2)}, u32[]{:S(2)}) %collective-permute-start.9) | collective-permute-done | bytes 983072 | tf_op jit(solution)/shard_map/ppermute | solution.py:105
  435.7 2.6 collective-permute-done.10
  438.3 2.7 fusion.9
  (64 shorter events, 8.7 us)
Async XLA Ops:
  6.5 238.3 %copy-start = (bf16[1536,8]{0,1:T(8,128)(2,1)S(1)}, bf16[1536,8]{0,1:T(8,128)(2,1)}, u32[]{:S(2)}) copy-start(bf16[1536,8]{0,1:T(8,128)(2,1)} %param.18) | copy-start | bytes 73732
  6.5 184.5 %reduce-scatter.3.cloned.1.call-start = ((), (), s32[]{:S(2)}) async-start(), calls=%async_computation.2 | async-start | bytes 7864320 | tf_op jit(solution)/shard_map/reduce_scatter | solution.py:215
  7.9 16.0 %collective-permute-start = (bf16[512,512]{1,0:T(8,128)(2,1)S(1)}, bf16[512,512]{1,0:T(8,128)(2,1)S(1)}, u32[]{:S(2)}, u32[]{:S(2)}) collective-permute-start(bf16[512,512]{1,0:T(8,128)(2,1)S(1)} %get-tuple-element.13), channel_id=1, source_target_pairs={{0,2},{1,3},{4,6},{5,7},{8,10},{9,11},{12,14},{13,15},{16,18},{17,... | collective-permute-start | bytes 1572872 | tf_op jit(solution)/shard_map/ppermute | solution.py:132
  25.0 3.0 collective-permute-start.1
  25.0 5.2 %copy-start.1 = (bf16[512,1536]{1,0:T(8,128)(2,1)S(1)}, bf16[512,1536]{1,0:T(8,128)(2,1)}, u32[]{:S(2)}) copy-start(bf16[512,1536]{1,0:T(8,128)(2,1)} %q_ref.1) | copy-start | bytes 4718596
  77.8 0.7 copy-start.3
  77.8 0.7 copy-start.4
  77.8 113.2 %copy-start.6 = (bf16[512,1536]{1,0:T(8,128)(2,1)S(1)}, bf16[512,1536]{1,0:T(8,128)(2,1)}, u32[]{:S(2)}) copy-start(bf16[512,1536]{1,0:T(8,128)(2,1)} %param.15) | copy-start | bytes 4718596
  77.8 264.8 %reduce-scatter.5.cloned.1.call-start = ((), (), s32[]{:S(2)}) async-start(), calls=%async_computation.3 | async-start | bytes 6553600 | tf_op jit(solution)/shard_map/reduce_scatter | solution.py:246
  193.7 1.9 copy-start.2
  195.7 2.6 collective-permute-start.2
  200.2 24.0 %collective-permute-start.3 = (bf16[320,1536]{1,0:T(8,128)(2,1)S(1)}, bf16[320,1536]{1,0:T(8,128)(2,1)}, u32[]{:S(2)}, u32[]{:S(2)}) collective-permute-start(bf16[320,1536]{1,0:T(8,128)(2,1)S(1)} %add_convert_fusion.4), channel_id=1, source_target_pairs={{0,2},{1,3},{2,0},{3,1},{4,6},{5,7},{6,4},{7,5},{8,10},{9,11},{10,... | collective-permute-start | bytes 2949128 | tf_op jit(solution)/shard_map/ppermute | solution.py:105
  224.3 1.7 copy-start.5
  225.9 2.6 collective-permute-start.4
  244.0 157.0 %all-gather.2.cloned.1.call-start = ((), (), s32[]{:S(2)}) async-start(), calls=%async_computation.4 | async-start | bytes 3276800 | tf_op jit(solution)/shard_map/all_gather | solution.py:261
  245.7 4.9 %collective-permute-start.5 = (bf16[320,128]{0,1:T(8,128)(2,1)S(1)}, bf16[320,128]{0,1:T(8,128)(2,1)S(1)}, u32[]{:S(2)}, u32[]{:S(2)}) collective-permute-start(bf16[320,128]{0,1:T(8,128)(2,1)S(1)} %dynamic-slice_convert_fusion.2), channel_id=1, source_target_pairs={{0,4},{4,0},{8,12},{12,8},{1,5},{5,1},{9,13},{13,9},{2,6},{6,2},{1... | collective-permute-start | bytes 245768 | tf_op jit(solution)/shard_map/ppermute | solution.py:105
  250.7 16.9 %collective-permute-start.6 = (bf16[320,128]{0,1:T(8,128)(2,1)S(1)}, bf16[320,128]{0,1:T(8,128)(2,1)S(1)}, u32[]{:S(2)}, u32[]{:S(2)}) collective-permute-start(bf16[320,128]{0,1:T(8,128)(2,1)S(1)} %add_convert_fusion.7), channel_id=1, source_target_pairs={{0,8},{4,12},{8,0},{12,4},{1,9},{5,13},{9,1},{13,5},{2,10},{6,14},... | collective-permute-start | bytes 245768 | tf_op jit(solution)/shard_map/ppermute | solution.py:105
  267.6 10.4 %collective-permute-start.7 = (bf16[320,128]{0,1:T(8,128)(2,1)S(1)}, bf16[320,128]{0,1:T(8,128)(2,1)S(1)}, u32[]{:S(2)}, u32[]{:S(2)}) collective-permute-start(bf16[320,128]{0,1:T(8,128)(2,1)S(1)} %add_convert_fusion.6), channel_id=1, source_target_pairs={{0,4},{4,0},{8,12},{12,8},{1,5},{5,1},{9,13},{13,9},{2,6},{6,2},{1... | collective-permute-start | bytes 245768 | tf_op jit(solution)/shard_map/ppermute | solution.py:105
  408.3 2.6 collective-permute-start.8
  411.2 23.9 %collective-permute-start.9 = (bf16[320,1536]{1,0:T(8,128)(2,1)S(1)}, bf16[320,1536]{1,0:T(8,128)(2,1)S(1)}, u32[]{:S(2)}, u32[]{:S(2)}) collective-permute-start(bf16[320,1536]{1,0:T(8,128)(2,1)S(1)} %add_convert_fusion.2), channel_id=1, source_target_pairs={{0,2},{1,3},{2,0},{3,1},{4,6},{5,7},{6,4},{7,5},{8,10},{9,11},{10,... | collective-permute-start | bytes 2949128 | tf_op jit(solution)/shard_map/ppermute | solution.py:105
  435.2 3.1 copy-start.8
  435.6 2.7 copy-start.7
  435.6 2.6 collective-permute-start.10
Sparse Core Ops, SparseCore 0:
  77.9 113.0 reduce-scatter.2
  244.1 98.5 reduce-scatter.4
  345.7 55.2 all-gather.1
